TPU v7x, 512 devices: a whole 4x8x8 slice. The times are simulated.
512 devices in a mesh: pipe: 16 (over x_lo, z), dp: 32 (over y, x_hi, core).
Axes of the slice: x: 4 (x_hi: 2, x_lo: 2; x = x_hi * 2 + x_lo), y: 8, z: 8, core: 2. Of those that a mesh axis runs over, the one named last changes fastest.
Arguments:
- section_input: bfloat16 [16, 4096, 4096], P('pipe', 'dp'), may hold values from -6 to 6
- out_grad: bfloat16 [16, 4096, 4096], P('pipe', 'dp'), may hold values from -6 to 6
- short_filter: bfloat16 [16, 2, 7, 4096], P('pipe', None, None, 'dp'), may hold values from -2 to 2
- long_filter: bfloat16 [16, 2, 256, 128], P('pipe', None, 'dp'), may hold values from -0.5 to 0.5
Outputs:
- passed_grad: bfloat16 [16, 4096, 4096], P('pipe', 'dp')
- short_grad: float32 [16, 2, 7, 4096], P('pipe', None, None, 'dp')
- long_grad: float32 [16, 2, 256, 128], P('pipe', None, 'dp')
All inputs are finite; a program needn't handle non-finite values.
Results may differ from a plain program's by a relative error of at most 0.0058.
Values may be sent and summed in bfloat16 or wider, within the bound.
No kernel may reach another device: no remote copies, remote signals or barrier semaphores. Data moves between devices by JAX's collectives and lax.ppermute only.
A program may use at most 64 MiB of HBM per device.

v0:
```python
import jax
import jax.numpy as jnp
from jax import lax
from jax.sharding import PartitionSpec as P


def from_behind(shard, axis, by):
    devices = lax.axis_size(axis)
    pairs = [(i, i + by) for i in range(devices) if 0 <= i + by < devices]
    return lax.ppermute(shard, axis, pairs)


def circulants(long_pair):
    pair_count, group_count, taps = long_pair.shape
    row_pos = jnp.arange(taps, dtype=jnp.int32)[:, None]
    col_pos = jnp.arange(taps, dtype=jnp.int32)[None, :]
    lag_table = (col_pos - row_pos + taps) % taps
    table = (lag_table.reshape(1, -1) == jnp.arange(taps, dtype=jnp.int32)[:, None]).astype(
        jnp.bfloat16
    )
    flat = jnp.dot(long_pair.reshape(-1, taps), table, preferred_element_type=jnp.float32).astype(
        jnp.bfloat16
    )
    circ = flat.reshape(pair_count, group_count, taps, taps)
    upper = row_pos <= col_pos
    zero_value = jnp.zeros((), jnp.bfloat16)
    return (jnp.where(upper, circ, zero_value), jnp.where(upper, zero_value, circ))


def as_groups(field, group_count, taps):
    return field.reshape(group_count, field.shape[0] // group_count, field.shape[1] // taps, taps)


def causal_long(field, circ_now, circ_past):
    group_count, taps = (circ_now.shape[0], circ_now.shape[2])
    blocks = as_groups(field, group_count, taps)
    earlier_blocks = jnp.concatenate([jnp.zeros_like(blocks[:, :, :1]), blocks[:, :, :-1]], axis=2)
    total = jnp.einsum("gcbt,gts->gcbs", blocks, circ_now, preferred_element_type=jnp.float32)
    total = total + jnp.einsum(
        "gcbt,gts->gcbs", earlier_blocks, circ_past, preferred_element_type=jnp.float32
    )
    return total.reshape(field.shape)


def anti_long(grad, circ_now, circ_past):
    group_count, taps = (circ_now.shape[0], circ_now.shape[2])
    blocks = as_groups(grad, group_count, taps)
    later_blocks = jnp.concatenate([blocks[:, :, 1:], jnp.zeros_like(blocks[:, :, :1])], axis=2)
    total = jnp.einsum("gcbs,gts->gcbt", blocks, circ_now, preferred_element_type=jnp.float32)
    total = total + jnp.einsum(
        "gcbs,gts->gcbt", later_blocks, circ_past, preferred_element_type=jnp.float32
    )
    return total.reshape(grad.shape)


def lag_grad(values, grad, group_count, taps):
    value_blocks = as_groups(values, group_count, taps)
    grad_blocks = as_groups(grad, group_count, taps)
    earlier_blocks = jnp.concatenate(
        [jnp.zeros_like(value_blocks[:, :, :1]), value_blocks[:, :, :-1]], axis=2
    )
    pairs_now = jnp.einsum(
        "gcbt,gcbs->gts", value_blocks, grad_blocks, preferred_element_type=jnp.float32
    )
    pairs_past = jnp.einsum(
        "gcbt,gcbs->gts", earlier_blocks, grad_blocks, preferred_element_type=jnp.float32
    )
    row_pos = jnp.arange(taps, dtype=jnp.int32)[:, None]
    col_pos = jnp.arange(taps, dtype=jnp.int32)[None, :]
    joined = jnp.where(row_pos <= col_pos, pairs_now, pairs_past)
    doubled = jnp.concatenate([joined, joined], axis=2).reshape(group_count, 2 * taps * taps)
    padded = jnp.concatenate([doubled, jnp.zeros((group_count, taps), jnp.float32)], axis=1)
    skewed = padded.reshape(group_count, taps, 2 * taps + 1)[:, :, :taps]
    return jnp.sum(skewed, axis=1)


def short_mix(field, taps_row):
    tap_count = taps_row.shape[0]
    extra = tap_count - 1
    row_count = field.shape[1]
    padded = jnp.concatenate([jnp.zeros((field.shape[0], extra), field.dtype), field], axis=1)
    total = jnp.zeros(field.shape, jnp.float32)
    for tap_index in range(tap_count):
        start = extra - tap_index
        total = total + taps_row[tap_index].astype(jnp.float32)[:, None] * padded[
            :, start : start + row_count
        ].astype(jnp.float32)
    return total


def short_back(field, taps_row):
    tap_count = taps_row.shape[0]
    extra = tap_count - 1
    row_count = field.shape[1]
    padded = jnp.concatenate([field, jnp.zeros((field.shape[0], extra), field.dtype)], axis=1)
    total = jnp.zeros(field.shape, jnp.float32)
    for tap_index in range(tap_count):
        total = total + taps_row[tap_index].astype(jnp.float32)[:, None] * padded[
            :, tap_index : tap_index + row_count
        ].astype(jnp.float32)
    return total


def short_corr(grad, field, tap_count):
    extra = tap_count - 1
    row_count = field.shape[1]
    padded = jnp.concatenate([jnp.zeros((field.shape[0], extra), field.dtype), field], axis=1)
    grad_wide = grad.astype(jnp.float32)
    rows_out = []
    for tap_index in range(tap_count):
        start = extra - tap_index
        rows_out.append(
            jnp.sum(grad_wide * padded[:, start : start + row_count].astype(jnp.float32), axis=1)
        )
    return jnp.stack(rows_out)


CHUNKS = 2


def chunk_grads(source, top_grad, short_all, long_all):
    group_count, taps = (long_all.shape[1], long_all.shape[2])
    tap_count = short_all.shape[1]
    circ_now, circ_past = circulants(long_all)
    mixed_one = short_mix(source, short_all[0]).astype(jnp.bfloat16)
    long_one = causal_long(mixed_one, circ_now[0], circ_past[0])
    middle = (source.astype(jnp.float32) + long_one).astype(jnp.bfloat16)
    mixed_two = short_mix(middle, short_all[1]).astype(jnp.bfloat16)
    dmix_two = anti_long(top_grad, circ_now[1], circ_past[1]).astype(jnp.bfloat16)
    dlong_two = lag_grad(mixed_two, top_grad, group_count, taps)
    middle_grad = (top_grad.astype(jnp.float32) + short_back(dmix_two, short_all[1])).astype(
        jnp.bfloat16
    )
    dshort_two = short_corr(dmix_two, middle, tap_count)
    dmix_one = anti_long(middle_grad, circ_now[0], circ_past[0]).astype(jnp.bfloat16)
    dlong_one = lag_grad(mixed_one, middle_grad, group_count, taps)
    input_grad = (middle_grad.astype(jnp.float32) + short_back(dmix_one, short_all[0])).astype(
        jnp.bfloat16
    )
    dshort_one = short_corr(dmix_one, source, tap_count)
    return input_grad, jnp.stack([dshort_one, dshort_two]), jnp.stack([dlong_one, dlong_two])


def body(section_input, out_grad, short_filter, long_filter):
    devices = lax.axis_size("dp")
    rows, width = section_input.shape[1], section_input.shape[2]
    both = jnp.stack([section_input[0], out_grad[0]])
    gathered = lax.all_to_all(both, "dp", split_axis=2, concat_axis=1, tiled=True)
    source = gathered[0].T
    top_grad = gathered[1].T
    input_grad, short_grad, long_grad = chunk_grads(source, top_grad, short_filter[0], long_filter[0])
    own = input_grad.shape[0]
    half = own // 2
    passed = []
    for index in range(2):
        piece = input_grad[index * half : (index + 1) * half].T
        own_rows = lax.all_to_all(piece, "dp", split_axis=0, concat_axis=1, tiled=True)
        passed.append(from_behind(own_rows.reshape(rows, devices, half), "pipe", -1))
    passed_grad = jnp.stack(passed, axis=2).reshape(1, rows, width)
    factor = float(rows * devices) ** (-0.5)
    return (passed_grad, short_grad[None] * factor, long_grad[None] * factor)


def solution(mesh):
    in_specs = (
        P("pipe", "dp", None),
        P("pipe", "dp", None),
        P("pipe", None, None, "dp"),
        P("pipe", None, "dp", None),
    )
    out_specs = (P("pipe", "dp", None), P("pipe", None, None, "dp"), P("pipe", None, "dp", None))
    return jax.shard_map(body, mesh=mesh, in_specs=in_specs, out_specs=out_specs, check_vma=False)
```

profile of v0, /device:TPU:6, one launch (start us, length us, event | category | flops | bytes accessed | tf_op | source)
XLA Modules:
  0.0 167.0 jit_solution(4444435746895479789)
XLA Ops:
  0.6 1.7 %pad_maximum_fusion = bf16[2,128,4096]{2,1,0:T(8,128)(2,1)S(1)} fusion(bf16[1,128,4096]{2,1,0:T(8,128)(2,1)} %param.5, bf16[1,128,4096]{2,1,0:T(8,128)(2,1)} %param.4), kind=kLoop, calls=%fused_computation.79 | loop fusion | flops 1048576 | bytes 4194304 | tf_op jit(solution)/shard_map/stack | solution.py:147
  2.4 3.8 %copy.48 = bf16[2,128,4096]{1,0,2:T(2,128)(2,1)} copy(bf16[2,128,4096]{2,1,0:T(8,128)(2,1)S(1)} %pad_maximum_fusion) | data formatting | bytes 4194304 | tf_op jit(solution)/shard_map/stack | solution.py:147
  6.2 10.2 %all-to-all-start = ((bf16[2,128,4096]{1,0,2:T(2,128)(2,1)}), bf16[2,128,4096]{1,0,2:T(2,128)(2,1)S(1)}, u32[]{:S(2)}, u32[]{:S(2)}) async-start(bf16[2,128,4096]{1,0,2:T(2,128)(2,1)} %copy.48), calls=%async_computation | async-start | bytes 4194304 | tf_op jit(solution)/shard_map/all_to_all | solution.py:148
  16.5 0.1 copy.55
  16.6 1.4 fusion.46
  18.0 1.1 broadcast_select_fusion
  19.0 47.6 %all-to-all-done = bf16[2,128,4096]{1,0,2:T(2,128)(2,1)S(1)} async-done(((bf16[2,128,4096]{1,0,2:T(2,128)(2,1)}), bf16[2,128,4096]{1,0,2:T(2,128)(2,1)S(1)}, u32[]{:S(2)}, u32[]{:S(2)}) %all-to-all-start) | async-done | bytes 2097184 | tf_op jit(solution)/shard_map/all_to_all | solution.py:148
  66.7 3.8 %fusion.75 = (bf16[1,32,128,128]{2,0,3,1:T(2,128)(2,1)S(1)}, bf16[1,32,128,128]{2,0,3,1:T(2,128)(2,1)S(1)}) fusion(bf16[2,32,128,128]{2,0,3,1:T(2,128)(2,1)S(1)} %bitcast.274), kind=kLoop, calls=%fused_computation.174 | loop fusion | bytes 4194304 | tf_op jit(solution)/shard_map/slice | solution.py:149
  70.5 1.2 copy.54
  71.7 1.2 copy.49
  72.9 0.5 copy.124
  73.4 0.2 copy.71
  73.7 0.5 slice.275
  74.2 0.2 copy-done.12
  74.4 0.5 fusion.56
  74.9 0.4 copy-done.10
  75.3 0.4 add_convert_fusion.1
  75.7 1.0 copy-done.1
  76.7 0.5 copy.123
  77.2 3.1 %fusion.23 = bf16[128,4096]{1,0:T(8,128)(2,1)S(1)} fusion(bf16[128,4096]{1,0:T(8,128)(2,1)S(1)} %bitcast.290, f32[128]{0:T(128)S(1)} %get-tuple-element.47, f32[128]{0:T(128)S(1)} %get-tuple-element.48, f32[128]{0:T(128)S(1)} %get-tuple-element.49, f32[128]{0:T(128)S(1)} %get-tuple-element.50, f32[128]{0:T(128)S(1)} %get-tuple-element.51, ...), kind=kLoop, calls=%fused_computation.56 | loop fusion | flops 12058624 | bytes 3149312 | tf_op jit(solution)/shard_map/convert_element_type | solution.py:131
  80.3 0.2 copy.73
  80.5 0.5 slice.278
  81.0 0.5 fusion.58
  81.5 0.4 add_convert_fusion
  82.0 0.9 bitcast_bitcast_fusion
  83.0 5.1 %fusion.53 = (bf16[16,8,32,128]{3,1,2,0:T(8,128)(2,1)S(1)}, bf16[128,4096]{1,0:T(8,128)(2,1)S(1)}) fusion(f32[128]{0:T(128)S(1)} %get-tuple-element.54, f32[128]{0:T(128)S(1)} %get-tuple-element.55, f32[128]{0:T(128)S(1)} %get-tuple-element.43, f32[128]{0:T(128)S(1)} %get-tuple-element.44, f32[128]{0:T(128)S(1)} %get-tuple-element.45, ...), kind=kLoop, calls=%fused_computation.110 | loop fusion | flops 23068672 | bytes 5246464
  88.0 0.2 copy.76
  88.3 0.9 slice_bitcast_fusion.1
  89.2 1.0 copy.125
  90.2 6.2 %all-to-all-start.2 = ((bf16[32,128,64]{1,2,0:T(8,128)(2,1)}), bf16[32,128,64]{1,2,0:T(8,128)(2,1)}, u32[]{:S(2)}, u32[]{:S(2)}) async-start(bf16[32,128,64]{1,2,0:T(8,128)(2,1)} %bitcast.294), calls=%async_computation.2 | async-start | bytes 1048576 | tf_op jit(solution)/shard_map/all_to_all | solution.py:157
  96.4 1.5 fusion.57
  97.9 0.5 convolution_add_fusion
  98.4 0.7 copy-done.4
  99.1 0.3 copy-done.6
  99.4 0.3 copy-done.9
  99.8 6.5 %fusion.45 = (f32[128]{0:T(128)S(1)}, f32[128]{0:T(128)S(1)}, f32[128]{0:T(128)S(1)}, f32[128]{0:T(128)S(1)}, f32[128]{0:T(128)S(1)}, /*index=5*/f32[128]{0:T(128)S(1)}, f32[128]{0:T(128)S(1)}, bf16[128,4096]{1,0:T(8,128)(2,1)S(1)}) fusion(bf16[128,4096]{1,0:T(8,128)(2,1)S(1)} %copy-done.9, bf16[16,8,32,128]{3,2,1,0:T(8,128)(2,1)S(1)} %bitcast.280, ...), kind=kLoop, calls=%fused_computation.78 | loop fusion | flops 12582016 | bytes 6295040 | tf_op jit(solution)/shard_map/reduce_sum | solution.py:113
  106.3 1.0 copy.126
  107.2 5.9 %fusion.30 = (f32[128]{0:T(128)S(1)}, f32[128]{0:T(128)S(1)}, f32[128]{0:T(128)S(1)}, f32[128]{0:T(128)S(1)}, f32[128]{0:T(128)S(1)}, /*index=5*/f32[128]{0:T(12...) fusion(bf16[128,4096]{1,0:T(8,128)(2,1)S(1)} %get-tuple-element.35, bf16[16,8,32,128]{3,2,1,0:T(8,128)(2,1)S(1)} %bitcast.276, ...), kind=kLoop, calls=%fused_computation.63 | loop fusion | flops 22019200 | bytes 3152896 | tf_op jit(solution)/shard_map/reduce_sum | solution.py:113
  113.1 1.2 copy.79
  114.4 9.9 %all-to-all-start.1 = ((bf16[32,128,64]{1,2,0:T(8,128)(2,1)}), bf16[32,128,64]{1,2,0:T(8,128)(2,1)}, u32[]{:S(2)}, u32[]{:S(2)}) async-start(bf16[32,128,64]{1,2,0:T(8,128)(2,1)} %bitcast.293), calls=%async_computation.1 | async-start | bytes 1048576 | tf_op jit(solution)/shard_map/all_to_all | solution.py:157
  124.3 0.7 convolution_bitcast_fusion.2
  124.9 0.5 fusion.47
  125.5 0.1 pad_maximum_fusion.2
  125.6 0.6 copy-done.7
  126.2 0.6 convolution_bitcast_fusion
  126.8 1.3 fusion.48
  128.1 11.2 %collective-permute-start.1 = (bf16[128,32,64]{0,2,1:T(8,128)(2,1)}, bf16[128,32,64]{0,2,1:T(8,128)(2,1)}, u32[]{:S(2)}, u32[]{:S(2)}) collective-permute-start(bf16[128,32,64]{0,2,1:T(8,128)(2,1)} %bitcast.38), channel_id=1, source_target_pairs={{32,0},{64,32},{96,64},{128,96},{160,128},{192,160},{224,192},{256... | collective-permute-start | bytes 1572872 | tf_op jit(solution)/shard_map/ppermute | solution.py:10
  139.3 2.7 %all-to-all-done.1 = bf16[32,128,64]{1,2,0:T(8,128)(2,1)} async-done(((bf16[32,128,64]{1,2,0:T(8,128)(2,1)}), bf16[32,128,64]{1,2,0:T(8,128)(2,1)}, u32[]{:S(2)}, u32[]{:S(2)}) %all-to-all-start.1) | async-done | bytes 524320 | tf_op jit(solution)/shard_map/all_to_all | solution.py:157
  142.0 11.2 %collective-permute-start = (bf16[128,32,64]{0,2,1:T(8,128)(2,1)}, bf16[128,32,64]{0,2,1:T(8,128)(2,1)}, u32[]{:S(2)}, u32[]{:S(2)}) collective-permute-start(bf16[128,32,64]{0,2,1:T(8,128)(2,1)} %bitcast.35), channel_id=1, source_target_pairs={{32,0},{64,32},{96,64},{128,96},{160,128},{192,160},{224,192},{256... | collective-permute-start | bytes 1572872 | tf_op jit(solution)/shard_map/ppermute | solution.py:10
  153.2 0.3 copy.56
  153.6 0.6 copy.78
  154.2 0.1 concatenate.61
  154.3 2.4 %reshape.290 = f32[8,128,257]{2,1,0:T(8,128)} reshape(f32[8,32896]{1,0:T(8,128)S(1)} %concatenate.61) | data formatting | bytes 2105344 | tf_op jit(solution)/shard_map/reshape | solution.py:73
  156.7 0.6 copy.59
  157.3 0.1 pad_maximum_fusion.3
  157.4 0.3 copy.57
  157.7 0.6 copy.80
  158.4 2.4 %reshape.293 = f32[8,128,257]{2,1,0:T(8,128)} reshape(f32[8,32896]{1,0:T(8,128)S(1)} %concatenate.64) | data formatting | bytes 2105344 | tf_op jit(solution)/shard_map/reshape | solution.py:73
  160.8 1.1 slice_reduce_fusion.1
  161.9 1.1 slice_reduce_fusion
  163.0 0.6 maximum_multiply_fusion.1
  163.6 0.8 collective-permute-done
  164.4 1.3 pad_maximum_fusion.1
  165.7 1.3 copy.58
  (34 shorter events, 0.3 us)
Async XLA Ops:
  0.6 16.0 %copy-start = (bf16[1,2,8,128]{3,2,1,0:T(8,128)(2,1)S(1)}, bf16[1,2,8,128]{3,2,1,0:T(8,128)(2,1)}, u32[]{:S(2)}) copy-start(bf16[1,2,8,128]{3,2,1,0:T(8,128)(2,1)} %param.7) | copy-start | bytes 12292
  6.2 60.5 %all-to-all-start = ((bf16[2,128,4096]{1,0,2:T(2,128)(2,1)}), bf16[2,128,4096]{1,0,2:T(2,128)(2,1)S(1)}, u32[]{:S(2)}, u32[]{:S(2)}) async-start(bf16[2,128,4096]{1,0,2:T(2,128)(2,1)} %copy.48), calls=%async_computation | async-start | bytes 4194304 | tf_op jit(solution)/shard_map/all_to_all | solution.py:148
  16.4 1.6 copy-start.15
  71.7 10.2 %copy-start.3 = (bf16[1,32,128,128]{2,1,3,0:T(8,128)(2,1)}, bf16[1,32,128,128]{2,1,3,0:T(8,128)(2,1)S(1)}, u32[]{:S(2)}) copy-start(bf16[1,32,128,128]{2,1,3,0:T(8,128)(2,1)S(1)} %copy.54) | copy-start | bytes 3145732
  73.4 1.0 copy-start.12
  74.2 1.1 copy-start.10
  75.7 1.0 copy-start.1
  81.9 1.0 copy-start.5
  83.0 5.1 %copy-start.8 = (bf16[128,4096]{1,0:T(8,128)(2,1)}, bf16[128,4096]{1,0:T(8,128)(2,1)S(1)}, u32[]{:S(2)}) copy-start(bf16[128,4096]{1,0:T(8,128)(2,1)S(1)} %get-tuple-element.56) | copy-start | bytes 3145732
  90.2 24.2 %all-to-all-start.2 = ((bf16[32,128,64]{1,2,0:T(8,128)(2,1)}), bf16[32,128,64]{1,2,0:T(8,128)(2,1)}, u32[]{:S(2)}, u32[]{:S(2)}) async-start(bf16[32,128,64]{1,2,0:T(8,128)(2,1)} %bitcast.294), calls=%async_computation.2 | async-start | bytes 1048576 | tf_op jit(solution)/shard_map/all_to_all | solution.py:157
  96.4 1.5 copy-start.11
  97.9 1.2 copy-start.4
  97.9 1.5 copy-start.6
  97.9 1.8 %copy-start.9 = (bf16[128,4096]{1,0:T(8,128)(2,1)S(1)}, bf16[128,4096]{1,0:T(8,128)(2,1)}, u32[]{:S(2)}) copy-start(bf16[128,4096]{1,0:T(8,128)(2,1)} %copy-done.8) | copy-start | bytes 3145732
  99.8 6.5 %copy-start.14 = (bf16[8,32,8,128]{3,2,1,0:T(8,128)(2,1)S(1)}, bf16[8,32,8,128]{3,2,1,0:T(8,128)(2,1)}, u32[]{:S(2)}) copy-start(bf16[8,32,8,128]{3,2,1,0:T(8,128)(2,1)} %get-tuple-element.36) | copy-start | bytes 1572868
  99.8 7.5 %copy-start.2 = (bf16[8,16,32,128]{3,2,1,0:T(8,128)(2,1)S(1)}, bf16[8,16,32,128]{3,2,1,0:T(8,128)(2,1)}, u32[]{:S(2)}) copy-start(bf16[8,16,32,128]{3,2,1,0:T(8,128)(2,1)} %copy-done.1) | copy-start | bytes 3145732
  114.4 27.6 %all-to-all-start.1 = ((bf16[32,128,64]{1,2,0:T(8,128)(2,1)}), bf16[32,128,64]{1,2,0:T(8,128)(2,1)}, u32[]{:S(2)}, u32[]{:S(2)}) async-start(bf16[32,128,64]{1,2,0:T(8,128)(2,1)} %bitcast.293), calls=%async_computation.1 | async-start | bytes 1048576 | tf_op jit(solution)/shard_map/all_to_all | solution.py:157
  124.9 1.2 copy-start.7
  128.1 35.5 %collective-permute-start.1 = (bf16[128,32,64]{0,2,1:T(8,128)(2,1)}, bf16[128,32,64]{0,2,1:T(8,128)(2,1)}, u32[]{:S(2)}, u32[]{:S(2)}) collective-permute-start(bf16[128,32,64]{0,2,1:T(8,128)(2,1)} %bitcast.38), channel_id=1, source_target_pairs={{32,0},{64,32},{96,64},{128,96},{160,128},{192,160},{224,192},{256... | collective-permute-start | bytes 1572872 | tf_op jit(solution)/shard_map/ppermute | solution.py:10
  142.0 22.4 %collective-permute-start = (bf16[128,32,64]{0,2,1:T(8,128)(2,1)}, bf16[128,32,64]{0,2,1:T(8,128)(2,1)}, u32[]{:S(2)}, u32[]{:S(2)}) collective-permute-start(bf16[128,32,64]{0,2,1:T(8,128)(2,1)} %bitcast.35), channel_id=1, source_target_pairs={{32,0},{64,32},{96,64},{128,96},{160,128},{192,160},{224,192},{256... | collective-permute-start | bytes 1572872 | tf_op jit(solution)/shard_map/ppermute | solution.py:10
  154.2 3.1 %copy-start.13 = (f32[8,128,128]{1,2,0:T(8,128)S(1)}, f32[8,128,128]{1,2,0:T(8,128)}, u32[]{:S(2)}) copy-start(f32[8,128,128]{1,2,0:T(8,128)} %fusion.48) | copy-start | bytes 1572868
where the time goes:
time: 168 us; the launch traced here: 167 us
  waiting for transfers between devices  51.1 us (30%)
  starting transfers between devices  48.7 us (29%)
  local copies, waits for them, and re-layouts  30.2 us (18%)
  other arithmetic  27.6 us (16%)
  matrix products  8.26 us (5%)
    all_to_all x1, waiting for transfers between devices, body(): lax.all_to_all(both, 'dp', split_axis=2, concat_axis=1, tiled=True)  47.6 us
    ppermute x2, starting transfers between devices, from_behind(): return lax.ppermute(shard, axis, pairs)  22.4 us
    all_to_all x2, starting transfers between devices, body(): lax.all_to_all(piece, 'dp', split_axis=0, concat_axis=1, tiled=True)  16.1 us
    reduce_sum x2, other arithmetic, short_corr(): jnp.sum(grad_wide * padded[:, start:start + row_count].astype(jnp.float32...  12.4 us
    unnamed x43, local copies, waits for them, and re-layouts  10.5 us
    all_to_all x1, starting transfers between devices, body(): lax.all_to_all(both, 'dp', split_axis=2, concat_axis=1, tiled=True)  10.2 us
    unnamed x1, other arithmetic  5.07 us
    slice x2, local copies, waits for them, and re-layouts, body(): source = gathered[0].T  5.03 us
  transfers between devices with their start and end apart: 5, of which 3 were waited for; matrix products, arithmetic and copies ran while one was open for 20% of the time, Pallas kernels for 0%

commit v1 on v0

--- a/solution.py
+++ b/solution.py
@@ -118,37 +118,26 @@
 CHUNKS = 2
 
 
-def chunk_grads(source, top_grad, short_all, long_all):
+def body(section_input, out_grad, short_filter, long_filter):
+    devices = lax.axis_size("dp")
+    rows, width = section_input.shape[1], section_input.shape[2]
+    short_all = short_filter[0]
+    long_all = long_filter[0]
     group_count, taps = (long_all.shape[1], long_all.shape[2])
     tap_count = short_all.shape[1]
     circ_now, circ_past = circulants(long_all)
-    mixed_one = short_mix(source, short_all[0]).astype(jnp.bfloat16)
-    long_one = causal_long(mixed_one, circ_now[0], circ_past[0])
-    middle = (source.astype(jnp.float32) + long_one).astype(jnp.bfloat16)
-    mixed_two = short_mix(middle, short_all[1]).astype(jnp.bfloat16)
+    grad_rows = lax.all_to_all(out_grad[0], "dp", split_axis=1, concat_axis=0, tiled=True)
+    grad_rows, later_input = lax.optimization_barrier((grad_rows, section_input[0]))
+    input_rows = lax.all_to_all(later_input, "dp", split_axis=1, concat_axis=0, tiled=True)
+    top_grad = grad_rows.T
     dmix_two = anti_long(top_grad, circ_now[1], circ_past[1]).astype(jnp.bfloat16)
-    dlong_two = lag_grad(mixed_two, top_grad, group_count, taps)
     middle_grad = (top_grad.astype(jnp.float32) + short_back(dmix_two, short_all[1])).astype(
         jnp.bfloat16
     )
-    dshort_two = short_corr(dmix_two, middle, tap_count)
     dmix_one = anti_long(middle_grad, circ_now[0], circ_past[0]).astype(jnp.bfloat16)
-    dlong_one = lag_grad(mixed_one, middle_grad, group_count, taps)
     input_grad = (middle_grad.astype(jnp.float32) + short_back(dmix_one, short_all[0])).astype(
         jnp.bfloat16
     )
-    dshort_one = short_corr(dmix_one, source, tap_count)
-    return input_grad, jnp.stack([dshort_one, dshort_two]), jnp.stack([dlong_one, dlong_two])
-
-
-def body(section_input, out_grad, short_filter, long_filter):
-    devices = lax.axis_size("dp")
-    rows, width = section_input.shape[1], section_input.shape[2]
-    both = jnp.stack([section_input[0], out_grad[0]])
-    gathered = lax.all_to_all(both, "dp", split_axis=2, concat_axis=1, tiled=True)
-    source = gathered[0].T
-    top_grad = gathered[1].T
-    input_grad, short_grad, long_grad = chunk_grads(source, top_grad, short_filter[0], long_filter[0])
     own = input_grad.shape[0]
     half = own // 2
     passed = []
@@ -157,8 +146,19 @@
         own_rows = lax.all_to_all(piece, "dp", split_axis=0, concat_axis=1, tiled=True)
         passed.append(from_behind(own_rows.reshape(rows, devices, half), "pipe", -1))
     passed_grad = jnp.stack(passed, axis=2).reshape(1, rows, width)
+    source = input_rows.T
+    mixed_one = short_mix(source, short_all[0]).astype(jnp.bfloat16)
+    long_one = causal_long(mixed_one, circ_now[0], circ_past[0])
+    middle = (source.astype(jnp.float32) + long_one).astype(jnp.bfloat16)
+    mixed_two = short_mix(middle, short_all[1]).astype(jnp.bfloat16)
+    dlong_two = lag_grad(mixed_two, top_grad, group_count, taps)
+    dshort_two = short_corr(dmix_two, middle, tap_count)
+    dlong_one = lag_grad(mixed_one, middle_grad, group_count, taps)
+    dshort_one = short_corr(dmix_one, source, tap_count)
     factor = float(rows * devices) ** (-0.5)
-    return (passed_grad, short_grad[None] * factor, long_grad[None] * factor)
+    short_grad = jnp.stack([dshort_one, dshort_two])[None] * factor
+    long_grad = jnp.stack([dlong_one, dlong_two])[None] * factor
+    return (passed_grad, short_grad, long_grad)
 
 
 def solution(mesh):

time: 168 us -> 170 us (1.012)
  other arithmetic: 27.6 us -> 31 us
  waiting for transfers between devices: 51.1 us -> 47.8 us
  starting transfers between devices: 48.7 us -> 51.6 us
    unnamed x1, other arithmetic: 5.07 us -> 11.6 us
    slice x3 -> x0, local copies, waits for them, and re-layouts: 6.25 us -> none  [the longest x2 5.03 us: body(): source = gathered[0].T]
    unnamed x43 -> x47, local copies, waits for them, and re-layouts: 10.5 us -> 15.8 us
    all_to_all x1 -> x2, starting transfers between devices: 10.2 us -> 15.2 us  [the longest x1 10.2 us: body(): lax.all_to_all(out_grad[0], 'dp', split_axis=1, concat_axis=0, tiled=True)]
    all_to_all x1 -> x2, waiting for transfers between devices: 47.6 us -> 43.4 us  [the longest x1 25.6 us: body(): lax.all_to_all(out_grad[0], 'dp', split_axis=1, concat_axis=0, tiled=True)]
    all_to_all x0 -> x3, local copies, waits for them, and re-layouts: none -> 4.11 us  [the longest x2 2.79 us: body(): lax.all_to_all(later_input, 'dp', split_axis=1, concat_axis=0, tiled=True)]
    another operation x1 -> x0, local copies, waits for them, and re-layouts: 3.8 us -> none  [body(): both = jnp.stack([section_input[0], out_grad[0]])]
    all_to_all x2, starting transfers between devices: 16.1 us -> 13.7 us  [body(): lax.all_to_all(piece, 'dp', split_axis=0, concat_axis=1, tiled=True)]
  transfers between devices with their start and end apart: 5 -> 6, of which waited for: 3 -> 5; matrix products, arithmetic and copies ran while one was open for 20% -> 24% of each run, Pallas kernels for 0% -> 0%
where the time goes in v1:
time: 170 us; the launch traced here: 169 us
  starting transfers between devices  51.6 us (30%)
  waiting for transfers between devices  47.8 us (28%)
  other arithmetic  31 us (18%)
  local copies, waits for them, and re-layouts  29.2 us (17%)
  matrix products  8.24 us (5%)
    all_to_all x1, waiting for transfers between devices, body(): lax.all_to_all(out_grad[0], 'dp', split_axis=1, concat_axis=0, tiled=True)  25.6 us
    ppermute x2, starting transfers between devices, from_behind(): return lax.ppermute(shard, axis, pairs)  22.7 us
    all_to_all x1, waiting for transfers between devices, body(): lax.all_to_all(later_input, 'dp', split_axis=1, concat_axis=0, tiled=True)  17.8 us
    unnamed x47, local copies, waits for them, and re-layouts  15.8 us
    all_to_all x2, starting transfers between devices, body(): lax.all_to_all(piece, 'dp', split_axis=0, concat_axis=1, tiled=True)  13.7 us
    unnamed x1, other arithmetic  11.6 us
    reduce_sum x2, other arithmetic, short_corr(): jnp.sum(grad_wide * padded[:, start:start + row_count].astype(jnp.float32...  11.3 us
    all_to_all x1, starting transfers between devices, body(): lax.all_to_all(out_grad[0], 'dp', split_axis=1, concat_axis=0, tiled=True)  10.2 us
  transfers between devices with their start and end apart: 6, of which 5 were waited for; matrix products, arithmetic and copies ran while one was open for 24% of the time, Pallas kernels for 0%

profile of v1, /device:TPU:6, one launch (start us, length us, event | category | flops | bytes accessed | tf_op | source)
XLA Modules:
  0.0 168.9 jit_solution(5339665502270865047)
XLA Ops:
  0.6 1.6 copy.46
  2.3 1.3 copy.47
  3.6 10.2 %all-to-all-start = ((bf16[128,32,128]{2,0,1:T(8,128)(2,1)}), bf16[128,32,128]{2,0,1:T(8,128)(2,1)S(1)}, u32[]{:S(2)}, u32[]{:S(2)}) async-start(bf16[128,32,128]{2,0,1:T(8,128)(2,1)} %copy.47), calls=%async_computation | async-start | bytes 2097152 | tf_op jit(solution)/shard_map/all_to_all | solution.py:129
  14.0 0.7 copy.48
  14.7 1.4 fusion.46
  16.1 1.1 broadcast_select_fusion
  17.1 25.6 %all-to-all-done = bf16[128,32,128]{2,0,1:T(8,128)(2,1)S(1)} async-done(((bf16[128,32,128]{2,0,1:T(8,128)(2,1)}), bf16[128,32,128]{2,0,1:T(8,128)(2,1)S(1)}, u32[]{:S(2)}, u32[]{:S(2)}) %all-to-all-start) | async-done | bytes 1048608 | tf_op jit(solution)/shard_map/all_to_all | solution.py:129
  42.8 0.5 copy.49
  43.3 1.3 copy.54
  44.6 5.0 %all-to-all-start.3 = ((bf16[128,32,128]{2,0,1:T(8,128)(2,1)}), bf16[128,32,128]{2,0,1:T(8,128)(2,1)S(1)}, u32[]{:S(2)}, u32[]{:S(2)}) async-start(bf16[128,32,128]{2,0,1:T(8,128)(2,1)} %copy.54), calls=%async_computation.3 | async-start | bytes 2097152 | tf_op jit(solution)/shard_map/all_to_all | solution.py:131
  49.6 0.2 copy.71
  49.9 0.8 copy-done.12
  50.7 0.5 fusion.56
  51.1 0.5 slice.264
  51.7 0.4 add_convert_fusion.1
  52.1 1.0 copy-done.5
  53.1 0.5 copy.116
  53.6 2.8 %fusion.23 = bf16[128,4096]{1,0:T(8,128)(2,1)S(1)} fusion(bf16[128,4096]{1,0:T(8,128)(2,1)S(1)} %bitcast.271, bf16[4096,128]{0,1:T(8,128)(2,1)S(1)} %copy.49, f32[128]{0:T(128)S(1)} %get-tuple-element.49, f32[128]{0:T(128)S(1)} %get-tuple-element.50, f32[128]{0:T(128)S(1)} %get-tuple-element.51, f32[128]{0:T(128)S(1)} %get-tuple-element.52, ...), kind=kLoop, calls=%fused_computation.56 | loop fusion | flops 12058624 | bytes 3149312 | tf_op jit(solution)/shard_map/convert_element_type | solution.py:134
  56.4 0.2 copy.73
  56.7 0.5 slice.267
  57.2 0.2 copy-done.8
  57.4 0.5 fusion.58
  57.9 0.4 add_convert_fusion
  58.3 1.0 copy-done.3
  59.3 1.4 copy.115
  60.8 17.8 %all-to-all-done.3 = bf16[128,32,128]{2,0,1:T(8,128)(2,1)S(1)} async-done(((bf16[128,32,128]{2,0,1:T(8,128)(2,1)}), bf16[128,32,128]{2,0,1:T(8,128)(2,1)S(1)}, u32[]{:S(2)}, u32[]{:S(2)}) %all-to-all-start.3) | async-done | bytes 1048608 | tf_op jit(solution)/shard_map/all_to_all | solution.py:131
  78.5 1.0 copy-done.9
  79.5 1.5 copy.55
  81.0 11.6 %fusion.53 = (bf16[16,8,32,128]{3,1,2,0:T(8,128)(2,1)S(1)}, bf16[128,4096]{1,0:T(8,128)(2,1)S(1)}) fusion(f32[128]{0:T(128)S(1)} %get-tuple-element.56, f32[128]{0:T(128)S(1)} %get-tuple-element.57, f32[128]{0:T(128)S(1)} %get-tuple-element.45, f32[128]{0:T(128)S(1)} %get-tuple-element.46, f32[128]{0:T(128)S(1)} %get-tuple-element.47, ...), kind=kLoop, calls=%fused_computation.106 | loop fusion | flops 23068672 | bytes 5246464
  92.6 0.2 copy.75
  92.8 0.9 slice_bitcast_fusion.1
  93.7 1.0 copy.117
  94.7 5.1 %all-to-all-start.2 = ((bf16[32,128,64]{1,2,0:T(8,128)(2,1)}), bf16[32,128,64]{1,2,0:T(8,128)(2,1)}, u32[]{:S(2)}, u32[]{:S(2)}) async-start(bf16[32,128,64]{1,2,0:T(8,128)(2,1)} %bitcast.277), calls=%async_computation.2 | async-start | bytes 1048576 | tf_op jit(solution)/shard_map/all_to_all | solution.py:146
  99.8 1.5 fusion.57
  101.3 0.5 convolution_add_fusion
  101.8 0.7 copy-done.2
  102.5 0.3 copy-done.4
  102.8 5.4 %fusion.45 = (f32[128]{0:T(128)S(1)}, f32[128]{0:T(128)S(1)}, f32[128]{0:T(128)S(1)}, f32[128]{0:T(128)S(1)}, f32[128]{0:T(128)S(1)}, /*index=5*/f32[128]{0:T(128)S(1)}, f32[128]{0:T(128)S(1)}, bf16[128,4096]{1,0:T(8,128)(2,1)S(1)}) fusion(bf16[128,4096]{1,0:T(8,128)(2,1)S(1)} %bitcast.255, bf16[16,8,32,128]{3,2,1,0:T(8,128)(2,1)S(1)} %bitcast.257, ...), kind=kLoop, calls=%fused_computation.78 | loop fusion | flops 12582016 | bytes 6295040 | tf_op jit(solution)/shard_map/reduce_sum | solution.py:113
  108.2 1.0 copy.118
  109.2 5.9 %fusion.30 = (f32[128]{0:T(128)S(1)}, f32[128]{0:T(128)S(1)}, f32[128]{0:T(128)S(1)}, f32[128]{0:T(128)S(1)}, f32[128]{0:T(128)S(1)}, /*index=5*/f32[128]{0:T(12...) fusion(bf16[128,4096]{1,0:T(8,128)(2,1)S(1)} %get-tuple-element.37, bf16[16,8,32,128]{3,2,1,0:T(8,128)(2,1)S(1)} %bitcast.259, ...), kind=kLoop, calls=%fused_computation.63 | loop fusion | flops 22019200 | bytes 3152896 | tf_op jit(solution)/shard_map/reduce_sum | solution.py:113
  115.1 1.2 copy.78
  116.3 1.2 all-to-all-done.2
  117.5 8.7 %all-to-all-start.1 = ((bf16[32,128,64]{1,2,0:T(8,128)(2,1)}), bf16[32,128,64]{1,2,0:T(8,128)(2,1)}, u32[]{:S(2)}, u32[]{:S(2)}) async-start(bf16[32,128,64]{1,2,0:T(8,128)(2,1)} %bitcast.276), calls=%async_computation.1 | async-start | bytes 1048576 | tf_op jit(solution)/shard_map/all_to_all | solution.py:146
  126.2 0.7 convolution_bitcast_fusion.2
  126.8 0.5 fusion.47
  127.5 0.6 copy-done.7
  128.1 0.6 convolution_bitcast_fusion
  128.7 1.3 fusion.48
  130.0 11.2 %collective-permute-start.1 = (bf16[128,32,64]{0,2,1:T(8,128)(2,1)}, bf16[128,32,64]{0,2,1:T(8,128)(2,1)}, u32[]{:S(2)}, u32[]{:S(2)}) collective-permute-start(bf16[128,32,64]{0,2,1:T(8,128)(2,1)} %bitcast.40), channel_id=1, source_target_pairs={{32,0},{64,32},{96,64},{128,96},{160,128},{192,160},{224,192},{256... | collective-permute-start | bytes 1572872 | tf_op jit(solution)/shard_map/ppermute | solution.py:10
  141.2 2.7 %all-to-all-done.1 = bf16[32,128,64]{1,2,0:T(8,128)(2,1)} async-done(((bf16[32,128,64]{1,2,0:T(8,128)(2,1)}), bf16[32,128,64]{1,2,0:T(8,128)(2,1)}, u32[]{:S(2)}, u32[]{:S(2)}) %all-to-all-start.1) | async-done | bytes 524320 | tf_op jit(solution)/shard_map/all_to_all | solution.py:146
  143.9 11.5 %collective-permute-start = (bf16[128,32,64]{0,2,1:T(8,128)(2,1)}, bf16[128,32,64]{0,2,1:T(8,128)(2,1)}, u32[]{:S(2)}, u32[]{:S(2)}) collective-permute-start(bf16[128,32,64]{0,2,1:T(8,128)(2,1)} %bitcast.37), channel_id=1, source_target_pairs={{32,0},{64,32},{96,64},{128,96},{160,128},{192,160},{224,192},{256... | collective-permute-start | bytes 1572872 | tf_op jit(solution)/shard_map/ppermute | solution.py:10
  155.4 0.3 copy.57
  155.7 0.6 copy.77
  156.5 2.4 %reshape.293 = f32[8,128,257]{2,1,0:T(8,128)} reshape(f32[8,32896]{1,0:T(8,128)S(1)} %concatenate.61) | data formatting | bytes 2105344 | tf_op jit(solution)/shard_map/reshape | solution.py:73
  158.9 0.6 copy.60
  159.6 0.3 copy.58
  159.9 0.6 copy.79
  160.6 2.4 %reshape.296 = f32[8,128,257]{2,1,0:T(8,128)} reshape(f32[8,32896]{1,0:T(8,128)S(1)} %concatenate.64) | data formatting | bytes 2105344 | tf_op jit(solution)/shard_map/reshape | solution.py:73
  163.0 1.1 slice_reduce_fusion.1
  164.1 1.1 slice_reduce_fusion
  165.2 0.6 maximum_multiply_fusion.1
  165.8 0.5 collective-permute-done
  166.3 1.3 pad_maximum_fusion
  167.6 1.3 copy.59
  (38 shorter events, 0.7 us)
Async XLA Ops:
  0.6 14.1 %copy-start = (bf16[1,2,8,128]{3,2,1,0:T(8,128)(2,1)S(1)}, bf16[1,2,8,128]{3,2,1,0:T(8,128)(2,1)}, u32[]{:S(2)}) copy-start(bf16[1,2,8,128]{3,2,1,0:T(8,128)(2,1)} %param.7) | copy-start | bytes 12292
  2.3 11.7 %copy-start.15 = (bf16[1,128,4096]{2,1,0:T(8,128)(2,1)S(1)}, bf16[1,128,4096]{2,1,0:T(8,128)(2,1)}, u32[]{:S(2)}) copy-start(bf16[1,128,4096]{2,1,0:T(8,128)(2,1)} %param.4) | copy-start | bytes 3145732
  3.6 39.2 %all-to-all-start = ((bf16[128,32,128]{2,0,1:T(8,128)(2,1)}), bf16[128,32,128]{2,0,1:T(8,128)(2,1)S(1)}, u32[]{:S(2)}, u32[]{:S(2)}) async-start(bf16[128,32,128]{2,0,1:T(8,128)(2,1)} %copy.47), calls=%async_computation | async-start | bytes 2097152 | tf_op jit(solution)/shard_map/all_to_all | solution.py:129
  14.6 1.4 copy-start.16
  44.6 33.9 %all-to-all-start.3 = ((bf16[128,32,128]{2,0,1:T(8,128)(2,1)}), bf16[128,32,128]{2,0,1:T(8,128)(2,1)S(1)}, u32[]{:S(2)}, u32[]{:S(2)}) async-start(bf16[128,32,128]{2,0,1:T(8,128)(2,1)} %copy.54), calls=%async_computation.3 | async-start | bytes 2097152 | tf_op jit(solution)/shard_map/all_to_all | solution.py:131
  49.6 1.0 copy-start.12
  50.7 1.0 copy-start.10
  52.1 1.0 copy-start.5
  56.4 1.0 copy-start.8
  58.3 1.0 copy-start.3
  78.5 1.0 copy-start.9
  81.0 11.6 %copy-start.1 = (bf16[4096,128]{0,1:T(8,128)(2,1)}, bf16[4096,128]{0,1:T(8,128)(2,1)S(1)}, u32[]{:S(2)}) copy-start(bf16[4096,128]{0,1:T(8,128)(2,1)S(1)} %copy.55) | copy-start | bytes 3145732
  94.7 22.8 %all-to-all-start.2 = ((bf16[32,128,64]{1,2,0:T(8,128)(2,1)}), bf16[32,128,64]{1,2,0:T(8,128)(2,1)}, u32[]{:S(2)}, u32[]{:S(2)}) async-start(bf16[32,128,64]{1,2,0:T(8,128)(2,1)} %bitcast.277), calls=%async_computation.2 | async-start | bytes 1048576 | tf_op jit(solution)/shard_map/all_to_all | solution.py:146
  99.7 1.5 copy-start.11
  101.3 1.2 copy-start.2
  101.3 1.5 copy-start.4
  102.8 5.4 %copy-start.14 = (bf16[8,32,8,128]{3,2,1,0:T(8,128)(2,1)S(1)}, bf16[8,32,8,128]{3,2,1,0:T(8,128)(2,1)}, u32[]{:S(2)}) copy-start(bf16[8,32,8,128]{3,2,1,0:T(8,128)(2,1)} %get-tuple-element.38) | copy-start | bytes 1572868
  102.8 6.3 %copy-start.6 = (bf16[8,16,32,128]{3,2,1,0:T(8,128)(2,1)S(1)}, bf16[8,16,32,128]{3,2,1,0:T(8,128)(2,1)}, u32[]{:S(2)}) copy-start(bf16[8,16,32,128]{3,2,1,0:T(8,128)(2,1)} %copy-done.5) | copy-start | bytes 3145732
  117.5 26.4 %all-to-all-start.1 = ((bf16[32,128,64]{1,2,0:T(8,128)(2,1)}), bf16[32,128,64]{1,2,0:T(8,128)(2,1)}, u32[]{:S(2)}, u32[]{:S(2)}) async-start(bf16[32,128,64]{1,2,0:T(8,128)(2,1)} %bitcast.276), calls=%async_computation.1 | async-start | bytes 1048576 | tf_op jit(solution)/shard_map/all_to_all | solution.py:146
  126.8 1.2 copy-start.7
  130.0 35.8 %collective-permute-start.1 = (bf16[128,32,64]{0,2,1:T(8,128)(2,1)}, bf16[128,32,64]{0,2,1:T(8,128)(2,1)}, u32[]{:S(2)}, u32[]{:S(2)}) collective-permute-start(bf16[128,32,64]{0,2,1:T(8,128)(2,1)} %bitcast.40), channel_id=1, source_target_pairs={{32,0},{64,32},{96,64},{128,96},{160,128},{192,160},{224,192},{256... | collective-permute-start | bytes 1572872 | tf_op jit(solution)/shard_map/ppermute | solution.py:10
  143.9 22.4 %collective-permute-start = (bf16[128,32,64]{0,2,1:T(8,128)(2,1)}, bf16[128,32,64]{0,2,1:T(8,128)(2,1)}, u32[]{:S(2)}, u32[]{:S(2)}) collective-permute-start(bf16[128,32,64]{0,2,1:T(8,128)(2,1)} %bitcast.37), channel_id=1, source_target_pairs={{32,0},{64,32},{96,64},{128,96},{160,128},{192,160},{224,192},{256... | collective-permute-start | bytes 1572872 | tf_op jit(solution)/shard_map/ppermute | solution.py:10
  156.4 3.1 %copy-start.13 = (f32[8,128,128]{1,2,0:T(8,128)S(1)}, f32[8,128,128]{1,2,0:T(8,128)}, u32[]{:S(2)}) copy-start(f32[8,128,128]{1,2,0:T(8,128)} %fusion.48) | copy-start | bytes 1572868

commit v2 on v1

--- a/solution.py
+++ b/solution.py
@@ -138,14 +138,10 @@
     input_grad = (middle_grad.astype(jnp.float32) + short_back(dmix_one, short_all[0])).astype(
         jnp.bfloat16
     )
-    own = input_grad.shape[0]
-    half = own // 2
-    passed = []
-    for index in range(2):
-        piece = input_grad[index * half : (index + 1) * half].T
-        own_rows = lax.all_to_all(piece, "dp", split_axis=0, concat_axis=1, tiled=True)
-        passed.append(from_behind(own_rows.reshape(rows, devices, half), "pipe", -1))
-    passed_grad = jnp.stack(passed, axis=2).reshape(1, rows, width)
+    input_rows, input_grad = lax.optimization_barrier((input_rows, input_grad))
+    behind = from_behind(input_grad, "pipe", -1)
+    own_rows = lax.all_to_all(behind.T, "dp", split_axis=0, concat_axis=1, tiled=True)
+    passed_grad = own_rows[None]
     source = input_rows.T
     mixed_one = short_mix(source, short_all[0]).astype(jnp.bfloat16)
     long_one = causal_long(mixed_one, circ_now[0], circ_past[0])

time: 170 us -> 159 us (0.935)
  starting transfers between devices: 51.6 us -> 32.6 us
  waiting for transfers between devices: 47.8 us -> 53.6 us
  other arithmetic: 31 us -> 33.8 us
    ppermute x2 -> x1, waiting for transfers between devices: 0.52 us -> 12.2 us  [from_behind(): return lax.ppermute(shard, axis, pairs)]
    ppermute x2 -> x1, starting transfers between devices: 22.7 us -> 11.4 us  [from_behind(): return lax.ppermute(shard, axis, pairs)]
    reduce_sum x2, other arithmetic: 11.3 us -> 20.8 us  [short_corr(): jnp.sum(grad_wide * padded[:, start:start + row_count].astype(jnp.float32...]
    unnamed x1, other arithmetic: 11.6 us -> 2.53 us
    all_to_all x2 -> x1, starting transfers between devices: 13.7 us -> 5.98 us  [body(): lax.all_to_all(behind.T, 'dp', split_axis=0, concat_axis=1, tiled=True)]
    convert_element_type x0 -> x1, other arithmetic: none -> 3.61 us  [body(): (middle_grad.astype(jnp.float32) + short_back(dmix_one, short_all[0])).as...]
    all_to_all x2 -> x1, waiting for transfers between devices: 3.86 us -> 0.63 us  [body(): lax.all_to_all(behind.T, 'dp', split_axis=0, concat_axis=1, tiled=True)]
    all_to_all x1, waiting for transfers between devices: 17.8 us -> 15.1 us  [body(): lax.all_to_all(later_input, 'dp', split_axis=1, concat_axis=0, tiled=True)]
  transfers between devices with their start and end apart: 6 -> 4, of which waited for: 5 -> 4; matrix products, arithmetic and copies ran while one was open for 24% -> 32% of each run, Pallas kernels for 0% -> 0%
where the time goes in v2:
time: 159 us
  waiting for transfers between devices  53.6 us (34%)
  other arithmetic  33.8 us (21%)
  starting transfers between devices  32.6 us (21%)
  local copies, waits for them, and re-layouts  29.2 us (18%)
  matrix products  8.34 us (5%)
    all_to_all x1, waiting for transfers between devices, body(): lax.all_to_all(out_grad[0], 'dp', split_axis=1, concat_axis=0, tiled=True)  25.6 us
    reduce_sum x2, other arithmetic, short_corr(): jnp.sum(grad_wide * padded[:, start:start + row_count].astype(jnp.float32...  20.8 us
    all_to_all x1, waiting for transfers between devices, body(): lax.all_to_all(later_input, 'dp', split_axis=1, concat_axis=0, tiled=True)  15.1 us
    unnamed x44, local copies, waits for them, and re-layouts  13.8 us
    ppermute x1, waiting for transfers between devices, from_behind(): return lax.ppermute(shard, axis, pairs)  12.2 us
    ppermute x1, starting transfers between devices, from_behind(): return lax.ppermute(shard, axis, pairs)  11.4 us
    all_to_all x1, starting transfers between devices, body(): lax.all_to_all(out_grad[0], 'dp', split_axis=1, concat_axis=0, tiled=True)  10.2 us
    all_to_all x1, starting transfers between devices, body(): lax.all_to_all(behind.T, 'dp', split_axis=0, concat_axis=1, tiled=True)  5.98 us
  transfers between devices with their start and end apart: 4, of which 4 were waited for; matrix products, arithmetic and copies ran while one was open for 32% of the time, Pallas kernels for 0%

profile of v2, /device:TPU:6, one launch (start us, length us, event | category | flops | bytes accessed | tf_op | source)
XLA Modules:
  0.0 158.7 jit_solution(148689372701018584)
XLA Ops:
  0.6 1.6 %copy.32 = bf16[1,128,4096]{1,2,0:T(8,128)(2,1)S(1)} copy(bf16[1,128,4096]{2,1,0:T(8,128)(2,1)} %param.5) | data formatting | bytes 2097152 | tf_op args[1]
  2.3 1.3 copy.33
  3.6 10.2 %all-to-all-start = ((bf16[128,32,128]{2,0,1:T(8,128)(2,1)}), bf16[128,32,128]{2,0,1:T(8,128)(2,1)S(1)}, u32[]{:S(2)}, u32[]{:S(2)}) async-start(bf16[128,32,128]{2,0,1:T(8,128)(2,1)} %copy.33), calls=%async_computation | async-start | bytes 2097152 | tf_op jit(solution)/shard_map/all_to_all | solution.py:129
  13.8 0.1 copy.42
  14.0 0.7 copy.34
  14.7 1.4 fusion.46
  16.1 1.1 broadcast_select_fusion
  17.2 25.6 %all-to-all-done = bf16[128,32,128]{2,0,1:T(8,128)(2,1)S(1)} async-done(((bf16[128,32,128]{2,0,1:T(8,128)(2,1)}), bf16[128,32,128]{2,0,1:T(8,128)(2,1)S(1)}, u32[]{:S(2)}, u32[]{:S(2)}) %all-to-all-start) | async-done | bytes 1048608 | tf_op jit(solution)/shard_map/all_to_all | solution.py:129
  42.8 1.3 copy.35
  44.1 5.0 %all-to-all-start.1 = ((bf16[128,32,128]{2,0,1:T(8,128)(2,1)}), bf16[128,32,128]{2,0,1:T(8,128)(2,1)S(1)}, u32[]{:S(2)}, u32[]{:S(2)}) async-start(bf16[128,32,128]{2,0,1:T(8,128)(2,1)} %copy.35), calls=%async_computation.1 | async-start | bytes 2097152 | tf_op jit(solution)/shard_map/all_to_all | solution.py:131
  49.1 0.5 copy.36
  49.6 0.2 copy.55
  49.9 0.5 slice.256
  50.4 0.2 copy-done.10
  50.7 0.5 fusion.56
  51.1 0.4 copy-done.8
  51.5 0.4 add_convert_fusion.1
  52.0 1.0 copy-done.5
  52.9 0.5 copy.98
  53.4 2.8 %fusion.23 = bf16[128,4096]{1,0:T(8,128)(2,1)S(1)} fusion(bf16[128,4096]{1,0:T(8,128)(2,1)S(1)} %bitcast.260, bf16[4096,128]{0,1:T(8,128)(2,1)S(1)} %copy.36, f32[128]{0:T(128)S(1)} %get-tuple-element.46, f32[128]{0:T(128)S(1)} %get-tuple-element.47, f32[128]{0:T(128)S(1)} %get-tuple-element.48, f32[128]{0:T(128)S(1)} %get-tuple-element.49, ...), kind=kLoop, calls=%fused_computation.56 | loop fusion | flops 12058624 | bytes 3149312 | tf_op jit(solution)/shard_map/convert_element_type | solution.py:134
  56.2 0.2 copy.57
  56.4 0.5 slice.259
  56.9 0.5 fusion.58
  57.4 0.4 add_convert_fusion
  57.9 1.0 copy-done.3
  58.8 0.5 copy.97
  59.3 3.6 %fusion.38 = bf16[128,4096]{1,0:T(8,128)(2,1)} fusion(bf16[128,4096]{1,0:T(8,128)(2,1)S(1)} %bitcast.259, bf16[128,4096]{1,0:T(8,128)(2,1)S(1)} %fusion.23, f32[128]{0:T(128)S(1)} %get-tuple-element.53, f32[128]{0:T(128)S(1)} %get-tuple-element.54, f32[128]{0:T(128)S(1)} %get-tuple-element.42, f32[128]{0:T(128)S(1)} %get-tuple-element.43, ...), kind=kLoop, calls=%fused_computation.71 | loop fusion | flops 12058624 | bytes 3149312 | tf_op jit(solution)/shard_map/convert_element_type | solution.py:138
  62.9 15.1 %all-to-all-done.1 = bf16[128,32,128]{2,0,1:T(8,128)(2,1)S(1)} async-done(((bf16[128,32,128]{2,0,1:T(8,128)(2,1)}), bf16[128,32,128]{2,0,1:T(8,128)(2,1)S(1)}, u32[]{:S(2)}, u32[]{:S(2)}) %all-to-all-start.1) | async-done | bytes 1048608 | tf_op jit(solution)/shard_map/all_to_all | solution.py:131
  78.0 1.0 copy-done.7
  79.0 1.5 copy.41
  80.5 1.0 copy-done.1
  81.5 2.5 %fusion.53 = bf16[16,8,32,128]{3,1,2,0:T(8,128)(2,1)S(1)} fusion(f32[128]{0:T(128)S(1)} %get-tuple-element.53, f32[128]{0:T(128)S(1)} %get-tuple-element.54, f32[128]{0:T(128)S(1)} %get-tuple-element.42, f32[128]{0:T(128)S(1)} %get-tuple-element.43, f32[128]{0:T(128)S(1)} %get-tuple-element.44, f32[128]{0:T(128)S(1)} %get-tuple-element.45, ...), kind=kLoop, calls=%fused_computation.105 | loop fusion | flops 11010048 | bytes 2100736
  84.0 0.2 copy.59
  84.3 11.4 %collective-permute-start = (bf16[128,4096]{1,0:T(8,128)(2,1)S(1)}, bf16[128,4096]{1,0:T(8,128)(2,1)S(1)}, u32[]{:S(2)}, u32[]{:S(2)}) collective-permute-start(bf16[128,4096]{1,0:T(8,128)(2,1)S(1)} %copy-done.13), channel_id=1, source_target_pairs={{32,0},{64,32},{96,64},{128,96},{160,128},{192,160},{224,192},{256... | collective-permute-start | bytes 3145736 | tf_op jit(solution)/shard_map/ppermute | solution.py:10
  95.7 0.4 fusion.57
  96.2 1.5 convolution_bitcast_fusion.2
  97.6 0.5 convolution_add_fusion
  98.1 0.8 copy-done.2
  98.9 0.3 copy-done.4
  99.2 6.1 %fusion.45 = (f32[128]{0:T(128)S(1)}, f32[128]{0:T(128)S(1)}, f32[128]{0:T(128)S(1)}, f32[128]{0:T(128)S(1)}, f32[128]{0:T(128)S(1)}, /*index=5*/f32[128]{0:T(128)S(1)}, f32[128]{0:T(128)S(1)}, bf16[128,4096]{1,0:T(8,128)(2,1)}) fusion(bf16[128,4096]{1,0:T(8,128)(2,1)S(1)} %bitcast.243, bf16[16,8,32,128]{3,2,1,0:T(8,128)(2,1)S(1)} %bitcast.245, ...), kind=kLoop, calls=%fused_computation.78 | loop fusion | flops 12582016 | bytes 6295040 | tf_op jit(solution)/shard_map/reduce_sum | solution.py:113
  105.3 12.2 %collective-permute-done = bf16[128,4096]{1,0:T(8,128)(2,1)S(1)} collective-permute-done((bf16[128,4096]{1,0:T(8,128)(2,1)S(1)}, bf16[128,4096]{1,0:T(8,128)(2,1)S(1)}, u32[]{:S(2)}, u32[]{:S(2)}) %collective-permute-start) | collective-permute-done | bytes 1048608 | tf_op jit(solution)/shard_map/ppermute | solution.py:10
  117.5 1.0 copy-done.14
  118.5 2.3 %copy.39 = bf16[4096,128]{1,0:T(8,128)(2,1)} copy(bf16[4096,128]{0,1:T(8,128)(2,1)} %bitcast.265) | data formatting | bytes 2097152 | tf_op jit(solution)/shard_map/transpose | solution.py:143
  120.8 6.0 %all-to-all-start.2 = ((bf16[32,128,128]{2,1,0:T(8,128)(2,1)}), bf16[32,128,128]{2,1,0:T(8,128)(2,1)}, u32[]{:S(2)}, u32[]{:S(2)}) async-start(bf16[32,128,128]{2,1,0:T(8,128)(2,1)} %bitcast.255), calls=%async_computation.2 | async-start | bytes 2097152 | tf_op jit(solution)/shard_map/all_to_all | solution.py:143
  126.7 1.7 %fusion.47 = f32[8,128,128]{1,2,0:T(8,128)S(1)} fusion(f32[8,128,128]{1,2,0:T(8,128)} %convolution_bitcast_fusion.2, pred[128,128]{0,1:T(8,128)(4,1)S(1)} %copy.42, bf16[8,16,32,128]{3,2,1,0:T(8,128)(2,1)S(1)} %bitcast.241, bf16[8,16,32,128]{3,2,1,0:T(8,128)(2,1)S(1)} %bitcast.237), kind=kOutput, calls=%fused_computation.87 | convolution fusion | flops 134348800 | bytes 3162112 | tf_op jit(solution)/shard_map/gcbt,gcbs->gts/dot_general | solution.py:62
  128.4 0.1 pad_maximum_fusion
  128.5 0.3 copy.43
  128.8 0.6 copy.61
  129.6 2.4 %reshape.283 = f32[8,128,257]{2,1,0:T(8,128)} reshape(f32[8,32896]{1,0:T(8,128)S(1)} %concatenate.61) | data formatting | bytes 2105344 | tf_op jit(solution)/shard_map/reshape | solution.py:73
  132.0 14.7 %fusion.30 = (f32[128]{0:T(128)S(1)}, f32[128]{0:T(128)S(1)}, f32[128]{0:T(128)S(1)}, f32[128]{0:T(128)S(1)}, f32[128]{0:T(128)S(1)}, /*index=5*/f32[128]{0:T(12...) fusion(bf16[128,4096]{1,0:T(8,128)(2,1)} %get-tuple-element.38, bf16[16,8,32,128]{3,2,1,0:T(8,128)(2,1)S(1)} %bitcast.247, ...), kind=kLoop, calls=%fused_computation.63 | loop fusion | flops 22019200 | bytes 3152896 | tf_op jit(solution)/shard_map/reduce_sum | solution.py:113
  146.8 0.6 copy.46
  147.4 0.2 copy.62
  147.6 0.6 convolution_bitcast_fusion
  148.3 0.5 fusion.48
  148.8 0.1 pad_maximum_fusion.1
  148.9 0.3 copy.44
  149.2 0.6 copy.63
  149.9 2.4 %reshape.286 = f32[8,128,257]{2,1,0:T(8,128)} reshape(f32[8,32896]{1,0:T(8,128)S(1)} %concatenate.64) | data formatting | bytes 2105344 | tf_op jit(solution)/shard_map/reshape | solution.py:73
  152.3 1.1 slice_reduce_fusion.1
  153.4 1.1 slice_reduce_fusion
  154.5 0.6 maximum_multiply_fusion.1
  155.1 0.6 all-to-all-done.2
  155.7 1.6 %copy.40 = bf16[32,128,128]{1,2,0:T(8,128)(2,1)S(1)} copy(bf16[32,128,128]{2,1,0:T(8,128)(2,1)} %all-to-all-done.2) | data formatting | bytes 2097152 | tf_op jit(solution)/shard_map/all_to_all | solution.py:143
  157.4 1.3 copy.45
  (31 shorter events, 0.3 us)
Async XLA Ops:
  0.6 14.1 %copy-start = (bf16[1,2,8,128]{3,2,1,0:T(8,128)(2,1)S(1)}, bf16[1,2,8,128]{3,2,1,0:T(8,128)(2,1)}, u32[]{:S(2)}) copy-start(bf16[1,2,8,128]{3,2,1,0:T(8,128)(2,1)} %param.7) | copy-start | bytes 12292
  2.3 11.7 %copy-start.12 = (bf16[1,128,4096]{2,1,0:T(8,128)(2,1)S(1)}, bf16[1,128,4096]{2,1,0:T(8,128)(2,1)}, u32[]{:S(2)}) copy-start(bf16[1,128,4096]{2,1,0:T(8,128)(2,1)} %param.4) | copy-start | bytes 3145732
  3.6 39.2 %all-to-all-start = ((bf16[128,32,128]{2,0,1:T(8,128)(2,1)}), bf16[128,32,128]{2,0,1:T(8,128)(2,1)S(1)}, u32[]{:S(2)}, u32[]{:S(2)}) async-start(bf16[128,32,128]{2,0,1:T(8,128)(2,1)} %copy.33), calls=%async_computation | async-start | bytes 2097152 | tf_op jit(solution)/shard_map/all_to_all | solution.py:129
  14.6 1.4 copy-start.15
  44.1 33.9 %all-to-all-start.1 = ((bf16[128,32,128]{2,0,1:T(8,128)(2,1)}), bf16[128,32,128]{2,0,1:T(8,128)(2,1)S(1)}, u32[]{:S(2)}, u32[]{:S(2)}) async-start(bf16[128,32,128]{2,0,1:T(8,128)(2,1)} %copy.35), calls=%async_computation.1 | async-start | bytes 2097152 | tf_op jit(solution)/shard_map/all_to_all | solution.py:131
  49.6 1.0 copy-start.10
  50.4 1.1 copy-start.8
  51.9 1.0 copy-start.5
  57.9 1.0 copy-start.3
  78.0 1.0 copy-start.7
  80.5 1.0 copy-start.1
  81.5 2.8 %copy-start.13 = (bf16[128,4096]{1,0:T(8,128)(2,1)S(1)}, bf16[128,4096]{1,0:T(8,128)(2,1)}, u32[]{:S(2)}) copy-start(bf16[128,4096]{1,0:T(8,128)(2,1)} %fusion.38) | copy-start | bytes 3145732
  81.5 14.2 %copy-start.11 = (bf16[2,8,128,128]{3,2,1,0:T(8,128)(2,1)S(1)}, bf16[2,8,128,128]{3,2,1,0:T(8,128)(2,1)}, u32[]{:S(2)}) copy-start(bf16[2,8,128,128]{3,2,1,0:T(8,128)(2,1)} %get-tuple-element.40) | copy-start | bytes 1572868
  84.3 33.2 %collective-permute-start = (bf16[128,4096]{1,0:T(8,128)(2,1)S(1)}, bf16[128,4096]{1,0:T(8,128)(2,1)S(1)}, u32[]{:S(2)}, u32[]{:S(2)}) collective-permute-start(bf16[128,4096]{1,0:T(8,128)(2,1)S(1)} %copy-done.13), channel_id=1, source_target_pairs={{32,0},{64,32},{96,64},{128,96},{160,128},{192,160},{224,192},{256... | collective-permute-start | bytes 3145736 | tf_op jit(solution)/shard_map/ppermute | solution.py:10
  96.2 1.5 copy-start.9
  97.6 1.2 copy-start.2
  97.6 1.5 copy-start.4
  117.5 1.0 copy-start.14
  120.8 35.0 %all-to-all-start.2 = ((bf16[32,128,128]{2,1,0:T(8,128)(2,1)}), bf16[32,128,128]{2,1,0:T(8,128)(2,1)}, u32[]{:S(2)}, u32[]{:S(2)}) async-start(bf16[32,128,128]{2,1,0:T(8,128)(2,1)} %bitcast.255), calls=%async_computation.2 | async-start | bytes 2097152 | tf_op jit(solution)/shard_map/all_to_all | solution.py:143
  129.5 2.5 %copy-start.6 = (bf16[8,16,32,128]{3,2,1,0:T(8,128)(2,1)S(1)}, bf16[8,16,32,128]{3,2,1,0:T(8,128)(2,1)}, u32[]{:S(2)}) copy-start(bf16[8,16,32,128]{3,2,1,0:T(8,128)(2,1)} %copy-done.5) | copy-start | bytes 3145732

commit v3 on v2

--- a/solution.py
+++ b/solution.py
@@ -130,16 +130,36 @@
     grad_rows, later_input = lax.optimization_barrier((grad_rows, section_input[0]))
     input_rows = lax.all_to_all(later_input, "dp", split_axis=1, concat_axis=0, tiled=True)
     top_grad = grad_rows.T
-    dmix_two = anti_long(top_grad, circ_now[1], circ_past[1]).astype(jnp.bfloat16)
-    middle_grad = (top_grad.astype(jnp.float32) + short_back(dmix_two, short_all[1])).astype(
-        jnp.bfloat16
-    )
-    dmix_one = anti_long(middle_grad, circ_now[0], circ_past[0]).astype(jnp.bfloat16)
-    input_grad = (middle_grad.astype(jnp.float32) + short_back(dmix_one, short_all[0])).astype(
-        jnp.bfloat16
-    )
-    input_rows, input_grad = lax.optimization_barrier((input_rows, input_grad))
-    behind = from_behind(input_grad, "pipe", -1)
+    own = top_grad.shape[0]
+    half = own // 2
+    group_half = group_count // 2
+    dmix_twos, middle_grads, dmix_ones, behinds = [], [], [], []
+    for index in range(2):
+        rows_of = slice(index * half, (index + 1) * half)
+        groups_of = slice(index * group_half, (index + 1) * group_half)
+        grad_half = top_grad[rows_of]
+        if index:
+            grad_half, input_grad_h = lax.optimization_barrier((grad_half, input_grad_h))
+            behinds.append(from_behind(input_grad_h, "pipe", -1))
+        short_half = short_all[:, :, rows_of]
+        dmix_two_h = anti_long(grad_half, circ_now[1, groups_of], circ_past[1, groups_of]).astype(jnp.bfloat16)
+        middle_grad_h = (
+            grad_half.astype(jnp.float32) + short_back(dmix_two_h, short_half[1])
+        ).astype(jnp.bfloat16)
+        dmix_one_h = anti_long(middle_grad_h, circ_now[0, groups_of], circ_past[0, groups_of]).astype(
+            jnp.bfloat16
+        )
+        input_grad_h = (
+            middle_grad_h.astype(jnp.float32) + short_back(dmix_one_h, short_half[0])
+        ).astype(jnp.bfloat16)
+        dmix_twos.append(dmix_two_h)
+        middle_grads.append(middle_grad_h)
+        dmix_ones.append(dmix_one_h)
+    behinds.append(from_behind(input_grad_h, "pipe", -1))
+    dmix_two = jnp.concatenate(dmix_twos)
+    middle_grad = jnp.concatenate(middle_grads)
+    dmix_one = jnp.concatenate(dmix_ones)
+    input_rows, behind = lax.optimization_barrier((input_rows, jnp.concatenate(behinds)))
     own_rows = lax.all_to_all(behind.T, "dp", split_axis=0, concat_axis=1, tiled=True)
     passed_grad = own_rows[None]
     source = input_rows.T

time: 159 us -> 150 us (0.943)
  waiting for transfers between devices: 53.6 us -> 44.8 us
  local copies, waits for them, and re-layouts: 29.2 us -> 22.1 us
  starting transfers between devices: 32.6 us -> 38.7 us
    all_to_all x1, waiting for transfers between devices: 15.1 us -> 0.01 us  [body(): lax.all_to_all(later_input, 'dp', split_axis=1, concat_axis=0, tiled=True)]
    ppermute x1 -> x2, waiting for transfers between devices: 12.2 us -> 18.2 us  [from_behind(): return lax.ppermute(shard, axis, pairs)]
    unnamed x44 -> x55, local copies, waits for them, and re-layouts: 13.8 us -> 9.16 us
    all_to_all x1, starting transfers between devices: 5.98 us -> 9.57 us  [body(): lax.all_to_all(behind.T, 'dp', split_axis=0, concat_axis=1, tiled=True)]
    ppermute x1 -> x2, starting transfers between devices: 11.4 us -> 13.8 us  [from_behind(): return lax.ppermute(shard, axis, pairs)]
    convert_element_type x2 -> x5, other arithmetic: 6.38 us -> 7.51 us  [the longest x2 4.57 us: body(): input_grad_h = (middle_grad_h.astype(jnp.float32) + short_back(dmix_one_h...]
  transfers between devices with their start and end apart: 4 -> 5, of which waited for: 4 -> 3; matrix products, arithmetic and copies ran while one was open for 32% -> 36% of each run, Pallas kernels for 0% -> 0%
where the time goes in v3:
time: 150 us; the launch traced here: 149 us
  waiting for transfers between devices  44.8 us (30%)
  starting transfers between devices  38.7 us (26%)
  other arithmetic  34.1 us (23%)
  local copies, waits for them, and re-layouts  22.1 us (15%)
  matrix products  7.96 us (5%)
    all_to_all x1, waiting for transfers between devices, body(): lax.all_to_all(out_grad[0], 'dp', split_axis=1, concat_axis=0, tiled=True)  26.6 us
    reduce_sum x2, other arithmetic, short_corr(): jnp.sum(grad_wide * padded[:, start:start + row_count].astype(jnp.float32...  20.6 us
    ppermute x2, waiting for transfers between devices, from_behind(): return lax.ppermute(shard, axis, pairs)  18.2 us
    ppermute x2, starting transfers between devices, from_behind(): return lax.ppermute(shard, axis, pairs)  13.8 us
    all_to_all x1, starting transfers between devices, body(): lax.all_to_all(out_grad[0], 'dp', split_axis=1, concat_axis=0, tiled=True)  10.2 us
    all_to_all x1, starting transfers between devices, body(): lax.all_to_all(behind.T, 'dp', split_axis=0, concat_axis=1, tiled=True)  9.57 us
    unnamed x55, local copies, waits for them, and re-layouts  9.16 us
    all_to_all x1, starting transfers between devices, body(): lax.all_to_all(later_input, 'dp', split_axis=1, concat_axis=0, tiled=True)  5.04 us
  transfers between devices with their start and end apart: 5, of which 3 were waited for; matrix products, arithmetic and copies ran while one was open for 36% of the time, Pallas kernels for 0%

profile of v3, /device:TPU:6, one launch (start us, length us, event | category | flops | bytes accessed | tf_op | source)
XLA Modules:
  0.0 149.0 jit_solution(1552515325506026310)
XLA Ops:
  0.6 1.6 %copy.32 = bf16[1,128,4096]{1,2,0:T(8,128)(2,1)S(1)} copy(bf16[1,128,4096]{2,1,0:T(8,128)(2,1)} %param.5) | data formatting | bytes 2097152 | tf_op args[1]
  2.3 1.3 copy.33
  3.6 10.2 %all-to-all-start = ((bf16[128,32,128]{2,0,1:T(8,128)(2,1)}), bf16[128,32,128]{2,0,1:T(8,128)(2,1)S(1)}, u32[]{:S(2)}, u32[]{:S(2)}) async-start(bf16[128,32,128]{2,0,1:T(8,128)(2,1)} %copy.33), calls=%async_computation | async-start | bytes 2097152 | tf_op jit(solution)/shard_map/all_to_all | solution.py:129
  13.8 0.7 copy.34
  14.6 1.4 fusion.34
  16.1 26.6 %all-to-all-done = bf16[128,32,128]{2,0,1:T(8,128)(2,1)S(1)} async-done(((bf16[128,32,128]{2,0,1:T(8,128)(2,1)}), bf16[128,32,128]{2,0,1:T(8,128)(2,1)S(1)}, u32[]{:S(2)}, u32[]{:S(2)}) %all-to-all-start) | async-done | bytes 1048608 | tf_op jit(solution)/shard_map/all_to_all | solution.py:129
  42.8 1.3 copy.35
  44.1 5.0 %all-to-all-start.1 = ((bf16[128,32,128]{2,0,1:T(8,128)(2,1)}), bf16[128,32,128]{2,0,1:T(8,128)(2,1)}, u32[]{:S(2)}, u32[]{:S(2)}) async-start(bf16[128,32,128]{2,0,1:T(8,128)(2,1)} %copy.35), calls=%async_computation.1 | async-start | bytes 2097152 | tf_op jit(solution)/shard_map/all_to_all | solution.py:131
  49.1 0.5 copy.36
  49.9 0.2 slice.507
  50.1 0.3 fusion.54
  50.4 0.3 fusion.30
  50.7 0.2 copy.87
  50.9 1.5 add_convert_fusion.3
  52.5 0.2 slice.517
  52.7 0.3 fusion.53
  53.0 0.3 fusion.31
  53.3 0.2 copy.86
  53.5 2.3 %add_convert_fusion.2 = bf16[64,4096]{1,0:T(8,128)(2,1)} fusion(bf16[64,4096]{1,0:T(8,128)(2,1)S(1)} %bitcast.434, bf16[64,4096]{1,0:T(8,128)(2,1)S(1)} %add_convert_fusion.3, f32[64]{0:T(128)S(1)} %get-tuple-element.77, f32[64]{0:T(128)S(1)} %get-tuple-element.78, f32[64]{0:T(128)S(1)} %get-tuple-element.79, f32[64]{0:T(128)S(1)} %get-tuple-element.80, ...), kind=kLoop, calls=%fused_computation.90 | loop fusion | flops 6029312 | bytes 1574656 | tf_op jit(solution)/shard_map/convert_element_type | solution.py:154
  55.9 0.2 slice.527
  56.1 11.4 %collective-permute-start = (bf16[64,4096]{1,0:T(8,128)(2,1)}, bf16[64,4096]{1,0:T(8,128)(2,1)}, u32[]{:S(2)}, u32[]{:S(2)}) collective-permute-start(bf16[64,4096]{1,0:T(8,128)(2,1)} %add_convert_fusion.2), channel_id=1, source_target_pairs={{32,0},{64,32},{96,64},{128,96},{160,128},{192,160},{224,192},{256... | collective-permute-start | bytes 1572872 | tf_op jit(solution)/shard_map/ppermute | solution.py:10
  67.5 0.3 fusion.52
  67.9 0.3 fusion.32
  68.2 0.2 copy.85
  68.4 1.5 add_convert_fusion.1
  70.0 0.2 slice.537
  70.2 0.3 fusion.51
  70.5 1.2 fusion.33
  71.7 0.2 copy.84
  71.9 2.3 %add_convert_fusion = bf16[64,4096]{1,0:T(8,128)(2,1)} fusion(bf16[64,4096]{1,0:T(8,128)(2,1)S(1)} %bitcast.436, bf16[64,4096]{1,0:T(8,128)(2,1)S(1)} %add_convert_fusion.1, f32[64]{0:T(128)S(1)} %get-tuple-element.64, f32[64]{0:T(128)S(1)} %get-tuple-element.65, f32[64]{0:T(128)S(1)} %get-tuple-element.66, f32[64]{0:T(128)S(1)} %get-tuple-element.67, ...), kind=kLoop, calls=%fused_computation.88 | loop fusion | flops 6029312 | bytes 1574656 | tf_op jit(solution)/shard_map/convert_element_type | solution.py:154
  74.2 2.5 %collective-permute-start.1 = (bf16[64,4096]{1,0:T(8,128)(2,1)}, bf16[64,4096]{1,0:T(8,128)(2,1)}, u32[]{:S(2)}, u32[]{:S(2)}) collective-permute-start(bf16[64,4096]{1,0:T(8,128)(2,1)} %add_convert_fusion), channel_id=1, source_target_pairs={{32,0},{64,32},{96,64},{128,96},{160,128},{192,160},{224,192},{256... | collective-permute-start | bytes 1572872 | tf_op jit(solution)/shard_map/ppermute | solution.py:10
  76.8 0.2 copy.74
  77.2 0.2 copy.71
  77.4 7.7 %collective-permute-done = bf16[64,4096]{1,0:T(8,128)(2,1)} collective-permute-done((bf16[64,4096]{1,0:T(8,128)(2,1)}, bf16[64,4096]{1,0:T(8,128)(2,1)}, u32[]{:S(2)}, u32[]{:S(2)}) %collective-permute-start) | collective-permute-done | bytes 524320 | tf_op jit(solution)/shard_map/ppermute | solution.py:10
  85.1 10.4 %collective-permute-done.1 = bf16[64,4096]{1,0:T(8,128)(2,1)} collective-permute-done((bf16[64,4096]{1,0:T(8,128)(2,1)}, bf16[64,4096]{1,0:T(8,128)(2,1)}, u32[]{:S(2)}, u32[]{:S(2)}) %collective-permute-start.1) | collective-permute-done | bytes 524320 | tf_op jit(solution)/shard_map/ppermute | solution.py:10
  95.6 1.3 pad_maximum_fusion
  96.9 1.3 copy.39
  98.2 9.6 %all-to-all-start.2 = ((bf16[32,128,128]{2,1,0:T(8,128)(2,1)}), bf16[32,128,128]{2,1,0:T(8,128)(2,1)}, u32[]{:S(2)}, u32[]{:S(2)}) async-start(bf16[32,128,128]{2,1,0:T(8,128)(2,1)} %bitcast.67), calls=%async_computation.2 | async-start | bytes 2097152 | tf_op jit(solution)/shard_map/all_to_all | solution.py:163
  107.7 1.5 copy.41
  109.2 2.6 %fusion.43 = bf16[16,8,32,128]{3,1,2,0:T(8,128)(2,1)S(1)} fusion(f32[128]{0:T(128)S(1)} %get-tuple-element.54, f32[128]{0:T(128)S(1)} %get-tuple-element.55, f32[128]{0:T(128)S(1)} %get-tuple-element.56, f32[128]{0:T(128)S(1)} %get-tuple-element.57, f32[128]{0:T(128)S(1)} %get-tuple-element.58, f32[128]{0:T(128)S(1)} %get-tuple-element.59, ...), kind=kLoop, calls=%fused_computation.93 | loop fusion | flops 11010048 | bytes 2100736
  111.8 0.2 copy.69
  112.1 0.4 fusion.50
  112.5 0.7 convolution_bitcast_fusion.2
  113.2 0.4 copy-done.12
  113.6 0.5 convolution_add_fusion
  114.1 0.6 copy-done.2
  114.6 0.2 copy-done.5
  115.1 5.9 %fusion.22 = (f32[128]{0:T(128)S(1)}, f32[128]{0:T(128)S(1)}, f32[128]{0:T(128)S(1)}, f32[128]{0:T(128)S(1)}, f32[128]{0:T(128)S(1)}, /*index=5*/f32[128]{0:T(12...) fusion(bf16[128,4096]{1,0:T(8,128)(2,1)S(1)} %bitcast.415, bf16[64,4096]{1,0:T(8,128)(2,1)S(1)} %bitcast.437, ...), kind=kLoop, calls=%fused_computation.53 | loop fusion | flops 17824768 | bytes 7344128 | tf_op jit(solution)/shard_map/reduce_sum | solution.py:113
  120.9 0.5 fusion.35
  121.6 0.3 copy.43
  121.9 0.6 copy.72
  122.6 2.4 %reshape.552 = f32[8,128,257]{2,1,0:T(8,128)} reshape(f32[8,32896]{1,0:T(8,128)S(1)} %concatenate.93) | data formatting | bytes 2105344 | tf_op jit(solution)/shard_map/reshape | solution.py:73
  125.1 14.7 %fusion.29 = (f32[128]{0:T(128)S(1)}, f32[128]{0:T(128)S(1)}, f32[128]{0:T(128)S(1)}, f32[128]{0:T(128)S(1)}, f32[128]{0:T(128)S(1)}, /*index=5*/f32[128]{0:T(128)S(1)}, bf16[16,8,32,128]{3,1,2,0:T(8,128)(2,1)S(1)}) fusion(bf16[128,4096]{1,0:T(8,128)(2,1)} %get-tuple-element.44, bf16[64,4096]{1,0:T(8,128)(2,1)S(1)} %bitcast.431, ...), kind=kLoop, calls=%fused_computation.60 | loop fusion | flops 22543616 | bytes 3152384 | tf_op jit(solution)/shard_map/reduce_sum | solution.py:113
  139.9 0.6 copy.46
  140.5 0.2 copy.73
  140.7 0.7 convolution_bitcast_fusion
  141.4 0.5 fusion.36
  142.0 0.3 copy.44
  142.4 0.6 copy.75
  143.1 1.3 reshape.556
  144.4 1.1 slice_reduce_fusion.1
  145.5 0.6 maximum_multiply_fusion.1
  146.1 1.6 %copy.40 = bf16[32,128,128]{1,2,0:T(8,128)(2,1)S(1)} copy(bf16[32,128,128]{2,1,0:T(8,128)(2,1)} %all-to-all-done.2) | data formatting | bytes 2097152 | tf_op jit(solution)/shard_map/all_to_all | solution.py:163
  147.7 1.3 copy.45
  (56 shorter events, 1.7 us)
Async XLA Ops:
  0.6 13.9 %copy-start = (bf16[1,2,8,128]{3,2,1,0:T(8,128)(2,1)S(1)}, bf16[1,2,8,128]{3,2,1,0:T(8,128)(2,1)}, u32[]{:S(2)}) copy-start(bf16[1,2,8,128]{3,2,1,0:T(8,128)(2,1)} %param.7) | copy-start | bytes 12292
  2.3 11.6 %copy-start.16 = (bf16[1,128,4096]{2,1,0:T(8,128)(2,1)S(1)}, bf16[1,128,4096]{2,1,0:T(8,128)(2,1)}, u32[]{:S(2)}) copy-start(bf16[1,128,4096]{2,1,0:T(8,128)(2,1)} %param.4) | copy-start | bytes 3145732
  3.6 39.2 %all-to-all-start = ((bf16[128,32,128]{2,0,1:T(8,128)(2,1)}), bf16[128,32,128]{2,0,1:T(8,128)(2,1)S(1)}, u32[]{:S(2)}, u32[]{:S(2)}) async-start(bf16[128,32,128]{2,0,1:T(8,128)(2,1)} %copy.33), calls=%async_computation | async-start | bytes 2097152 | tf_op jit(solution)/shard_map/all_to_all | solution.py:129
  14.5 1.4 copy-start.17
  16.1 33.9 %copy-start.13 = (bf16[2,8,128,128]{3,2,1,0:T(8,128)(2,1)}, bf16[2,8,128,128]{3,2,1,0:T(8,128)(2,1)S(1)}, u32[]{:S(2)}) copy-start(bf16[2,8,128,128]{3,2,1,0:T(8,128)(2,1)S(1)} %get-tuple-element.48) | copy-start | bytes 1572868
  16.1 51.7 %copy-start.11 = (bf16[2,8,128,128]{3,2,1,0:T(8,128)(2,1)}, bf16[2,8,128,128]{3,2,1,0:T(8,128)(2,1)S(1)}, u32[]{:S(2)}) copy-start(bf16[2,8,128,128]{3,2,1,0:T(8,128)(2,1)S(1)} %get-tuple-element.47) | copy-start | bytes 1572868
  44.1 52.8 %all-to-all-start.1 = ((bf16[128,32,128]{2,0,1:T(8,128)(2,1)}), bf16[128,32,128]{2,0,1:T(8,128)(2,1)}, u32[]{:S(2)}, u32[]{:S(2)}) async-start(bf16[128,32,128]{2,0,1:T(8,128)(2,1)} %copy.35), calls=%async_computation.1 | async-start | bytes 2097152 | tf_op jit(solution)/shard_map/all_to_all | solution.py:131
  50.9 2.1 %copy-start.1 = (bf16[8,8,32,128]{3,1,2,0:T(8,128)(2,1)}, bf16[8,8,32,128]{3,1,2,0:T(8,128)(2,1)S(1)}, u32[]{:S(2)}) copy-start(bf16[8,8,32,128]{3,1,2,0:T(8,128)(2,1)S(1)} %copy.87) | copy-start | bytes 1572868
  50.9 1.8 %copy-start.14 = (bf16[2,8,128,128]{3,2,1,0:T(8,128)(2,1)S(1)}, bf16[2,8,128,128]{3,2,1,0:T(8,128)(2,1)}, u32[]{:S(2)}) copy-start(bf16[2,8,128,128]{3,2,1,0:T(8,128)(2,1)} %copy-done.13) | copy-start | bytes 1572868
  53.5 14.3 %copy-start.7 = (bf16[8,8,32,128]{3,1,2,0:T(8,128)(2,1)}, bf16[8,8,32,128]{3,1,2,0:T(8,128)(2,1)S(1)}, u32[]{:S(2)}) copy-start(bf16[8,8,32,128]{3,1,2,0:T(8,128)(2,1)S(1)} %copy.86) | copy-start | bytes 1572868
  56.1 29.0 %collective-permute-start = (bf16[64,4096]{1,0:T(8,128)(2,1)}, bf16[64,4096]{1,0:T(8,128)(2,1)}, u32[]{:S(2)}, u32[]{:S(2)}) collective-permute-start(bf16[64,4096]{1,0:T(8,128)(2,1)} %add_convert_fusion.2), channel_id=1, source_target_pairs={{32,0},{64,32},{96,64},{128,96},{160,128},{192,160},{224,192},{256... | collective-permute-start | bytes 1572872 | tf_op jit(solution)/shard_map/ppermute | solution.py:10
  68.4 2.1 %copy-start.4 = (bf16[8,8,32,128]{3,1,2,0:T(8,128)(2,1)}, bf16[8,8,32,128]{3,1,2,0:T(8,128)(2,1)S(1)}, u32[]{:S(2)}) copy-start(bf16[8,8,32,128]{3,1,2,0:T(8,128)(2,1)S(1)} %copy.85) | copy-start | bytes 1572868
  71.9 4.9 %copy-start.9 = (bf16[8,8,32,128]{3,1,2,0:T(8,128)(2,1)}, bf16[8,8,32,128]{3,1,2,0:T(8,128)(2,1)S(1)}, u32[]{:S(2)}) copy-start(bf16[8,8,32,128]{3,1,2,0:T(8,128)(2,1)S(1)} %copy.84) | copy-start | bytes 1572868
  74.2 21.4 %collective-permute-start.1 = (bf16[64,4096]{1,0:T(8,128)(2,1)}, bf16[64,4096]{1,0:T(8,128)(2,1)}, u32[]{:S(2)}, u32[]{:S(2)}) collective-permute-start(bf16[64,4096]{1,0:T(8,128)(2,1)} %add_convert_fusion), channel_id=1, source_target_pairs={{32,0},{64,32},{96,64},{128,96},{160,128},{192,160},{224,192},{256... | collective-permute-start | bytes 1572872 | tf_op jit(solution)/shard_map/ppermute | solution.py:10
  98.2 47.9 %all-to-all-start.2 = ((bf16[32,128,128]{2,1,0:T(8,128)(2,1)}), bf16[32,128,128]{2,1,0:T(8,128)(2,1)}, u32[]{:S(2)}, u32[]{:S(2)}) async-start(bf16[32,128,128]{2,1,0:T(8,128)(2,1)} %bitcast.67), calls=%async_computation.2 | async-start | bytes 2097152 | tf_op jit(solution)/shard_map/all_to_all | solution.py:163
  109.2 2.8 %copy-start.15 = (bf16[2,8,128,128]{3,2,1,0:T(8,128)(2,1)S(1)}, bf16[2,8,128,128]{3,2,1,0:T(8,128)(2,1)}, u32[]{:S(2)}) copy-start(bf16[2,8,128,128]{3,2,1,0:T(8,128)(2,1)} %copy-done.13) | copy-start | bytes 1572868
  112.5 1.0 copy-start.12
  113.6 1.0 copy-start.2
  113.6 1.2 copy-start.5
  113.6 1.4 copy-start.8
  113.6 1.5 %copy-start.10 = (bf16[8,8,32,128]{3,1,2,0:T(8,128)(2,1)S(1)}, bf16[8,8,32,128]{3,1,2,0:T(8,128)(2,1)}, u32[]{:S(2)}) copy-start(bf16[8,8,32,128]{3,1,2,0:T(8,128)(2,1)} %copy-done.9) | copy-start | bytes 1572868
  122.5 2.5 %copy-start.3 = (bf16[8,8,32,128]{3,1,2,0:T(8,128)(2,1)S(1)}, bf16[8,8,32,128]{3,1,2,0:T(8,128)(2,1)}, u32[]{:S(2)}) copy-start(bf16[8,8,32,128]{3,1,2,0:T(8,128)(2,1)} %copy-done.1) | copy-start | bytes 1572868
  122.5 2.5 %copy-start.6 = (bf16[8,8,32,128]{3,1,2,0:T(8,128)(2,1)S(1)}, bf16[8,8,32,128]{3,1,2,0:T(8,128)(2,1)}, u32[]{:S(2)}) copy-start(bf16[8,8,32,128]{3,1,2,0:T(8,128)(2,1)} %copy-done.4) | copy-start | bytes 1572868

commit v4 on v3

--- a/solution.py
+++ b/solution.py
@@ -155,11 +155,12 @@
         dmix_twos.append(dmix_two_h)
         middle_grads.append(middle_grad_h)
         dmix_ones.append(dmix_one_h)
-    behinds.append(from_behind(input_grad_h, "pipe", -1))
     dmix_two = jnp.concatenate(dmix_twos)
     middle_grad = jnp.concatenate(middle_grads)
     dmix_one = jnp.concatenate(dmix_ones)
-    input_rows, behind = lax.optimization_barrier((input_rows, jnp.concatenate(behinds)))
+    input_rows, input_grad_h = lax.optimization_barrier((input_rows, input_grad_h))
+    behinds.append(from_behind(input_grad_h, "pipe", -1))
+    behind = jnp.concatenate(behinds)
     own_rows = lax.all_to_all(behind.T, "dp", split_axis=0, concat_axis=1, tiled=True)
     passed_grad = own_rows[None]
     source = input_rows.T

time: 150 us -> 148 us (0.987)
  waiting for transfers between devices: 44.8 us -> 29.3 us
  local copies, waits for them, and re-layouts: 22.1 us -> 27.3 us
  starting transfers between devices: 38.7 us -> 43.1 us
  other arithmetic: 34.1 us -> 37.1 us
    ppermute x2, waiting for transfers between devices: 18.2 us -> 0.01 us  [from_behind(): return lax.ppermute(shard, axis, pairs)]
    ppermute x2, starting transfers between devices: 13.8 us -> 22.6 us  [from_behind(): return lax.ppermute(shard, axis, pairs)]
    all_to_all x1, starting transfers between devices: 9.57 us -> 5.26 us  [body(): lax.all_to_all(behind.T, 'dp', split_axis=0, concat_axis=1, tiled=True)]
    all_to_all x1, waiting for transfers between devices: 0.01 us -> 3.1 us  [body(): lax.all_to_all(later_input, 'dp', split_axis=1, concat_axis=0, tiled=True)]
    unnamed x55 -> x59, local copies, waits for them, and re-layouts: 9.16 us -> 12.1 us
    transpose x0 -> x1, other arithmetic: none -> 2.26 us  [body(): own_rows = lax.all_to_all(behind.T, 'dp', split_axis=0, concat_axis=1, ti...]
  transfers between devices with their start and end apart: 5 -> 5, of which waited for: 3 -> 3; matrix products, arithmetic and copies ran while one was open for 36% -> 39% of each run, Pallas kernels for 0% -> 0%
where the time goes in v4:
time: 148 us; the launch traced here: 147 us
  starting transfers between devices  43.1 us (29%)
  other arithmetic  37.1 us (25%)
  waiting for transfers between devices  29.3 us (20%)
  local copies, waits for them, and re-layouts  27.3 us (18%)
  matrix products  8.99 us (6%)
    all_to_all x1, waiting for transfers between devices, body(): lax.all_to_all(out_grad[0], 'dp', split_axis=1, concat_axis=0, tiled=True)  25.5 us
    ppermute x2, starting transfers between devices, from_behind(): return lax.ppermute(shard, axis, pairs)  22.6 us
    reduce_sum x2, other arithmetic, short_corr(): jnp.sum(grad_wide * padded[:, start:start + row_count].astype(jnp.float32...  20.5 us
    unnamed x59, local copies, waits for them, and re-layouts  12.1 us
    all_to_all x1, starting transfers between devices, body(): lax.all_to_all(out_grad[0], 'dp', split_axis=1, concat_axis=0, tiled=True)  10.2 us
    all_to_all x1, starting transfers between devices, body(): lax.all_to_all(behind.T, 'dp', split_axis=0, concat_axis=1, tiled=True)  5.26 us
    all_to_all x1, starting transfers between devices, body(): lax.all_to_all(later_input, 'dp', split_axis=1, concat_axis=0, tiled=True)  4.98 us
    reshape x2, local copies, waits for them, and re-layouts, lag_grad(): skewed = padded.reshape(group_count, taps, 2 * taps + 1)[:, :, :taps]  4.83 us
  transfers between devices with their start and end apart: 5, of which 3 were waited for; matrix products, arithmetic and copies ran while one was open for 39% of the time, Pallas kernels for 0%

profile of v4, /device:TPU:6, one launch (start us, length us, event | category | flops | bytes accessed | tf_op | source)
XLA Modules:
  0.0 147.0 jit_solution(16067943922656243584)
XLA Ops:
  0.6 1.6 %copy.32 = bf16[1,128,4096]{1,2,0:T(8,128)(2,1)S(1)} copy(bf16[1,128,4096]{2,1,0:T(8,128)(2,1)} %param.5) | data formatting | bytes 2097152 | tf_op args[1]
  2.3 1.3 copy.33
  3.6 10.2 %all-to-all-start = ((bf16[128,32,128]{2,0,1:T(8,128)(2,1)}), bf16[128,32,128]{2,0,1:T(8,128)(2,1)S(1)}, u32[]{:S(2)}, u32[]{:S(2)}) async-start(bf16[128,32,128]{2,0,1:T(8,128)(2,1)} %copy.33), calls=%async_computation | async-start | bytes 2097152 | tf_op jit(solution)/shard_map/all_to_all | solution.py:129
  14.0 0.7 copy.34
  14.7 1.4 fusion.34
  16.2 1.1 broadcast_select_fusion
  17.2 25.5 %all-to-all-done = bf16[128,32,128]{2,0,1:T(8,128)(2,1)S(1)} async-done(((bf16[128,32,128]{2,0,1:T(8,128)(2,1)}), bf16[128,32,128]{2,0,1:T(8,128)(2,1)S(1)}, u32[]{:S(2)}, u32[]{:S(2)}) %all-to-all-start) | async-done | bytes 1048608 | tf_op jit(solution)/shard_map/all_to_all | solution.py:129
  42.8 0.5 copy.35
  43.3 1.3 copy.38
  44.6 5.0 %all-to-all-start.1 = ((bf16[128,32,128]{2,0,1:T(8,128)(2,1)}), bf16[128,32,128]{2,0,1:T(8,128)(2,1)S(1)}, u32[]{:S(2)}, u32[]{:S(2)}) async-start(bf16[128,32,128]{2,0,1:T(8,128)(2,1)} %copy.38), calls=%async_computation.1 | async-start | bytes 2097152 | tf_op jit(solution)/shard_map/all_to_all | solution.py:131
  49.6 0.2 copy.74
  50.0 0.2 slice.507
  50.2 0.7 copy-done.16
  50.9 0.3 fusion.54
  51.2 0.3 fusion.30
  51.5 0.2 copy.87
  51.8 1.5 add_convert_fusion.3
  53.5 0.3 fusion.53
  53.8 0.3 fusion.31
  54.1 0.2 copy.86
  54.4 2.3 %add_convert_fusion.2 = bf16[64,4096]{1,0:T(8,128)(2,1)} fusion(bf16[64,4096]{1,0:T(8,128)(2,1)S(1)} %bitcast.435, bf16[64,4096]{1,0:T(8,128)(2,1)S(1)} %add_convert_fusion.3, f32[64]{0:T(128)S(1)} %get-tuple-element.77, f32[64]{0:T(128)S(1)} %get-tuple-element.78, f32[64]{0:T(128)S(1)} %get-tuple-element.79, f32[64]{0:T(128)S(1)} %get-tuple-element.80, ...), kind=kLoop, calls=%fused_computation.90 | loop fusion | flops 6029312 | bytes 1574656 | tf_op jit(solution)/shard_map/convert_element_type | solution.py:154
  56.9 11.4 %collective-permute-start = (bf16[64,4096]{1,0:T(8,128)(2,1)}, bf16[64,4096]{1,0:T(8,128)(2,1)}, u32[]{:S(2)}, u32[]{:S(2)}) collective-permute-start(bf16[64,4096]{1,0:T(8,128)(2,1)} %add_convert_fusion.2), channel_id=1, source_target_pairs={{32,0},{64,32},{96,64},{128,96},{160,128},{192,160},{224,192},{256... | collective-permute-start | bytes 1572872 | tf_op jit(solution)/shard_map/ppermute | solution.py:10
  68.3 0.3 fusion.52
  68.7 0.3 fusion.32
  69.0 0.2 copy.85
  69.2 1.5 add_convert_fusion.1
  71.1 1.2 copy.71
  72.3 0.3 fusion.51
  72.6 0.3 fusion.33
  72.9 0.2 copy.84
  73.1 2.3 %add_convert_fusion = bf16[64,4096]{1,0:T(8,128)(2,1)} fusion(bf16[64,4096]{1,0:T(8,128)(2,1)S(1)} %bitcast.437, bf16[64,4096]{1,0:T(8,128)(2,1)S(1)} %add_convert_fusion.1, f32[64]{0:T(128)S(1)} %get-tuple-element.64, f32[64]{0:T(128)S(1)} %get-tuple-element.65, f32[64]{0:T(128)S(1)} %get-tuple-element.66, f32[64]{0:T(128)S(1)} %get-tuple-element.67, ...), kind=kLoop, calls=%fused_computation.88 | loop fusion | flops 6029312 | bytes 1574656 | tf_op jit(solution)/shard_map/convert_element_type | solution.py:154
  75.4 3.1 %all-to-all-done.1 = bf16[128,32,128]{2,0,1:T(8,128)(2,1)S(1)} async-done(((bf16[128,32,128]{2,0,1:T(8,128)(2,1)}), bf16[128,32,128]{2,0,1:T(8,128)(2,1)S(1)}, u32[]{:S(2)}, u32[]{:S(2)}) %all-to-all-start.1) | async-done | bytes 1048608 | tf_op jit(solution)/shard_map/all_to_all | solution.py:131
  78.5 1.0 copy-done.13
  79.5 11.2 %collective-permute-start.1 = (bf16[64,4096]{1,0:T(8,128)(2,1)}, bf16[64,4096]{1,0:T(8,128)(2,1)}, u32[]{:S(2)}, u32[]{:S(2)}) collective-permute-start(bf16[64,4096]{1,0:T(8,128)(2,1)} %add_convert_fusion), channel_id=1, source_target_pairs={{32,0},{64,32},{96,64},{128,96},{160,128},{192,160},{224,192},{256... | collective-permute-start | bytes 1572872 | tf_op jit(solution)/shard_map/ppermute | solution.py:10
  90.7 1.5 %copy.41 = bf16[4096,128]{0,1:T(8,128)(2,1)S(1)} copy(bf16[4096,128]{1,0:T(8,128)(2,1)} %bitcast.450) | data formatting | bytes 2097152 | tf_op jit(solution)/shard_map/optimization_barrier | solution.py:161
  92.2 2.6 %fusion.43 = bf16[16,8,32,128]{3,1,2,0:T(8,128)(2,1)S(1)} fusion(f32[128]{0:T(128)S(1)} %get-tuple-element.54, f32[128]{0:T(128)S(1)} %get-tuple-element.55, f32[128]{0:T(128)S(1)} %get-tuple-element.56, f32[128]{0:T(128)S(1)} %get-tuple-element.57, f32[128]{0:T(128)S(1)} %get-tuple-element.58, f32[128]{0:T(128)S(1)} %get-tuple-element.59, ...), kind=kLoop, calls=%fused_computation.93 | loop fusion | flops 11010048 | bytes 2100736
  94.8 0.2 copy.69
  95.1 0.4 fusion.50
  95.5 0.8 copy-done.1
  96.3 1.5 %convolution_bitcast_fusion.2 = f32[8,128,128]{1,2,0:T(8,128)} fusion(bf16[8,16,31,128]{3,2,1,0:T(8,128)(2,1)S(1)} %bitcast.412, bf16[8,16,32,128]{3,2,1,0:T(8,128)(2,1)S(1)} %bitcast.422), kind=kOutput, calls=%fused_computation.73 | convolution fusion | flops 134217728 | bytes 2588672 | tf_op jit(solution)/shard_map/gcbt,gcbs->gts/dot_general | solution.py:65
  97.8 0.5 convolution_add_fusion
  98.2 0.5 copy-done.4
  99.3 5.8 %fusion.22 = (f32[128]{0:T(128)S(1)}, f32[128]{0:T(128)S(1)}, f32[128]{0:T(128)S(1)}, f32[128]{0:T(128)S(1)}, f32[128]{0:T(128)S(1)}, /*index=5*/f32[128]{0:T(12...) fusion(bf16[128,4096]{1,0:T(8,128)(2,1)S(1)} %bitcast.416, bf16[64,4096]{1,0:T(8,128)(2,1)S(1)} %bitcast.438, ...), kind=kLoop, calls=%fused_computation.53 | loop fusion | flops 17824768 | bytes 7344128 | tf_op jit(solution)/shard_map/reduce_sum | solution.py:113
  105.1 2.3 %maximum_bitcast_fusion = bf16[4096,128]{0,1:T(8,128)(2,1)} fusion(bf16[64,4096]{1,0:T(8,128)(2,1)} %collective-permute-done.1, bf16[64,4096]{1,0:T(8,128)(2,1)} %collective-permute-done), kind=kLoop, calls=%fused_computation.81 | loop fusion | flops 2097152 | bytes 2097152 | tf_op jit(solution)/shard_map/transpose | solution.py:164
  107.4 2.4 %copy.39 = bf16[4096,128]{1,0:T(8,128)(2,1)} copy(bf16[4096,128]{0,1:T(8,128)(2,1)} %maximum_bitcast_fusion) | data formatting | bytes 2097152 | tf_op jit(solution)/shard_map/transpose | solution.py:164
  109.8 5.3 %all-to-all-start.2 = ((bf16[32,128,128]{2,1,0:T(8,128)(2,1)}), bf16[32,128,128]{2,1,0:T(8,128)(2,1)}, u32[]{:S(2)}, u32[]{:S(2)}) async-start(bf16[32,128,128]{2,1,0:T(8,128)(2,1)} %bitcast.451), calls=%async_computation.2 | async-start | bytes 2097152 | tf_op jit(solution)/shard_map/all_to_all | solution.py:164
  115.0 1.7 %fusion.35 = f32[8,128,128]{1,2,0:T(8,128)S(1)} fusion(f32[8,128,128]{1,2,0:T(8,128)} %convolution_bitcast_fusion.2, pred[128,128]{0,1:T(8,128)(4,1)S(1)} %copy.42, bf16[8,16,32,128]{3,2,1,0:T(8,128)(2,1)S(1)} %bitcast.423, bf16[8,16,32,128]{3,2,1,0:T(8,128)(2,1)S(1)} %bitcast.414), kind=kOutput, calls=%fused_computation.75 | convolution fusion | flops 134348800 | bytes 3162112 | tf_op jit(solution)/shard_map/gcbt,gcbs->gts/dot_general | solution.py:62
  116.8 0.3 copy.43
  117.1 0.6 copy.72
  117.9 2.4 %reshape.552 = f32[8,128,257]{2,1,0:T(8,128)} reshape(f32[8,32896]{1,0:T(8,128)S(1)} %concatenate.93) | data formatting | bytes 2105344 | tf_op jit(solution)/shard_map/reshape | solution.py:73
  120.3 14.7 %fusion.29 = (f32[128]{0:T(128)S(1)}, f32[128]{0:T(128)S(1)}, f32[128]{0:T(128)S(1)}, f32[128]{0:T(128)S(1)}, f32[128]{0:T(128)S(1)}, /*index=5*/f32[128]{0:T(128)S(1)}, bf16[16,8,32,128]{3,1,2,0:T(8,128)(2,1)S(1)}) fusion(bf16[128,4096]{1,0:T(8,128)(2,1)} %get-tuple-element.44, bf16[64,4096]{1,0:T(8,128)(2,1)S(1)} %bitcast.432, ...), kind=kLoop, calls=%fused_computation.60 | loop fusion | flops 22543616 | bytes 3152384 | tf_op jit(solution)/shard_map/reduce_sum | solution.py:113
  135.0 0.6 copy.46
  135.6 0.2 copy.73
  135.9 0.6 convolution_bitcast_fusion
  136.5 0.5 fusion.36
  137.2 0.3 copy.44
  137.5 0.6 copy.75
  138.2 2.4 %reshape.556 = f32[8,128,257]{2,1,0:T(8,128)} reshape(f32[8,32896]{1,0:T(8,128)S(1)} %concatenate.96) | data formatting | bytes 2105344 | tf_op jit(solution)/shard_map/reshape | solution.py:73
  140.6 1.1 slice_reduce_fusion.1
  141.7 1.1 slice_reduce_fusion
  142.8 0.6 maximum_multiply_fusion.1
  143.4 0.7 all-to-all-done.2
  144.1 1.6 %copy.40 = bf16[32,128,128]{1,2,0:T(8,128)(2,1)S(1)} copy(bf16[32,128,128]{2,1,0:T(8,128)(2,1)} %all-to-all-done.2) | data formatting | bytes 2097152 | tf_op jit(solution)/shard_map/all_to_all | solution.py:164
  145.7 1.3 copy.45
  (60 shorter events, 2.3 us)
Async XLA Ops:
  0.6 14.1 %copy-start = (bf16[1,2,8,128]{3,2,1,0:T(8,128)(2,1)S(1)}, bf16[1,2,8,128]{3,2,1,0:T(8,128)(2,1)}, u32[]{:S(2)}) copy-start(bf16[1,2,8,128]{3,2,1,0:T(8,128)(2,1)} %param.7) | copy-start | bytes 12292
  2.3 11.7 %copy-start.18 = (bf16[1,128,4096]{2,1,0:T(8,128)(2,1)S(1)}, bf16[1,128,4096]{2,1,0:T(8,128)(2,1)}, u32[]{:S(2)}) copy-start(bf16[1,128,4096]{2,1,0:T(8,128)(2,1)} %param.4) | copy-start | bytes 3145732
  3.6 39.2 %all-to-all-start = ((bf16[128,32,128]{2,0,1:T(8,128)(2,1)}), bf16[128,32,128]{2,0,1:T(8,128)(2,1)S(1)}, u32[]{:S(2)}, u32[]{:S(2)}) async-start(bf16[128,32,128]{2,0,1:T(8,128)(2,1)} %copy.33), calls=%async_computation | async-start | bytes 2097152 | tf_op jit(solution)/shard_map/all_to_all | solution.py:129
  14.6 1.4 copy-start.19
  44.6 33.9 %all-to-all-start.1 = ((bf16[128,32,128]{2,0,1:T(8,128)(2,1)}), bf16[128,32,128]{2,0,1:T(8,128)(2,1)S(1)}, u32[]{:S(2)}, u32[]{:S(2)}) async-start(bf16[128,32,128]{2,0,1:T(8,128)(2,1)} %copy.38), calls=%async_computation.1 | async-start | bytes 2097152 | tf_op jit(solution)/shard_map/all_to_all | solution.py:131
  49.8 1.0 copy-start.16
  49.9 1.3 copy-start.14
  51.7 2.1 %copy-start.3 = (bf16[8,8,32,128]{3,1,2,0:T(8,128)(2,1)}, bf16[8,8,32,128]{3,1,2,0:T(8,128)(2,1)S(1)}, u32[]{:S(2)}) copy-start(bf16[8,8,32,128]{3,1,2,0:T(8,128)(2,1)S(1)} %copy.87) | copy-start | bytes 1572868
  54.4 14.3 %copy-start.9 = (bf16[8,8,32,128]{3,1,2,0:T(8,128)(2,1)}, bf16[8,8,32,128]{3,1,2,0:T(8,128)(2,1)S(1)}, u32[]{:S(2)}) copy-start(bf16[8,8,32,128]{3,1,2,0:T(8,128)(2,1)S(1)} %copy.86) | copy-start | bytes 1572868
  56.9 48.2 %collective-permute-start = (bf16[64,4096]{1,0:T(8,128)(2,1)}, bf16[64,4096]{1,0:T(8,128)(2,1)}, u32[]{:S(2)}, u32[]{:S(2)}) collective-permute-start(bf16[64,4096]{1,0:T(8,128)(2,1)} %add_convert_fusion.2), channel_id=1, source_target_pairs={{32,0},{64,32},{96,64},{128,96},{160,128},{192,160},{224,192},{256... | collective-permute-start | bytes 1572872 | tf_op jit(solution)/shard_map/ppermute | solution.py:10
  69.2 1.9 %copy-start.6 = (bf16[8,8,32,128]{3,1,2,0:T(8,128)(2,1)}, bf16[8,8,32,128]{3,1,2,0:T(8,128)(2,1)S(1)}, u32[]{:S(2)}) copy-start(bf16[8,8,32,128]{3,1,2,0:T(8,128)(2,1)S(1)} %copy.85) | copy-start | bytes 1572868
  73.1 19.1 %copy-start.11 = (bf16[8,8,32,128]{3,1,2,0:T(8,128)(2,1)}, bf16[8,8,32,128]{3,1,2,0:T(8,128)(2,1)S(1)}, u32[]{:S(2)}) copy-start(bf16[8,8,32,128]{3,1,2,0:T(8,128)(2,1)S(1)} %copy.84) | copy-start | bytes 1572868
  78.5 1.0 copy-start.13
  79.5 25.6 %collective-permute-start.1 = (bf16[64,4096]{1,0:T(8,128)(2,1)}, bf16[64,4096]{1,0:T(8,128)(2,1)}, u32[]{:S(2)}, u32[]{:S(2)}) collective-permute-start(bf16[64,4096]{1,0:T(8,128)(2,1)} %add_convert_fusion), channel_id=1, source_target_pairs={{32,0},{64,32},{96,64},{128,96},{160,128},{192,160},{224,192},{256... | collective-permute-start | bytes 1572872 | tf_op jit(solution)/shard_map/ppermute | solution.py:10
  92.2 2.8 %copy-start.17 = (bf16[2,8,128,128]{3,2,1,0:T(8,128)(2,1)S(1)}, bf16[2,8,128,128]{3,2,1,0:T(8,128)(2,1)}, u32[]{:S(2)}) copy-start(bf16[2,8,128,128]{3,2,1,0:T(8,128)(2,1)} %get-tuple-element.48) | copy-start | bytes 1572868
  95.0 1.2 copy-start.1
  95.5 2.2 %copy-start.15 = (bf16[2,8,128,128]{3,2,1,0:T(8,128)(2,1)S(1)}, bf16[2,8,128,128]{3,2,1,0:T(8,128)(2,1)}, u32[]{:S(2)}) copy-start(bf16[2,8,128,128]{3,2,1,0:T(8,128)(2,1)} %get-tuple-element.47) | copy-start | bytes 1572868
  97.8 1.0 copy-start.4
  97.8 1.2 copy-start.7
  97.8 1.4 copy-start.10
  97.8 1.5 %copy-start.12 = (bf16[8,8,32,128]{3,1,2,0:T(8,128)(2,1)S(1)}, bf16[8,8,32,128]{3,1,2,0:T(8,128)(2,1)}, u32[]{:S(2)}) copy-start(bf16[8,8,32,128]{3,1,2,0:T(8,128)(2,1)} %copy-done.11) | copy-start | bytes 1572868
  107.4 7.6 %copy-start.2 = (bf16[16,8,32,128]{3,2,1,0:T(8,128)(2,1)S(1)}, bf16[16,8,32,128]{3,2,1,0:T(8,128)(2,1)}, u32[]{:S(2)}) copy-start(bf16[16,8,32,128]{3,2,1,0:T(8,128)(2,1)} %copy.71) | copy-start | bytes 3145732
  109.8 34.3 %all-to-all-start.2 = ((bf16[32,128,128]{2,1,0:T(8,128)(2,1)}), bf16[32,128,128]{2,1,0:T(8,128)(2,1)}, u32[]{:S(2)}, u32[]{:S(2)}) async-start(bf16[32,128,128]{2,1,0:T(8,128)(2,1)} %bitcast.451), calls=%async_computation.2 | async-start | bytes 2097152 | tf_op jit(solution)/shard_map/all_to_all | solution.py:164
  117.8 2.5 %copy-start.5 = (bf16[8,8,32,128]{3,1,2,0:T(8,128)(2,1)S(1)}, bf16[8,8,32,128]{3,1,2,0:T(8,128)(2,1)}, u32[]{:S(2)}) copy-start(bf16[8,8,32,128]{3,1,2,0:T(8,128)(2,1)} %copy-done.3) | copy-start | bytes 1572868
  117.8 2.5 %copy-start.8 = (bf16[8,8,32,128]{3,1,2,0:T(8,128)(2,1)S(1)}, bf16[8,8,32,128]{3,1,2,0:T(8,128)(2,1)}, u32[]{:S(2)}) copy-start(bf16[8,8,32,128]{3,1,2,0:T(8,128)(2,1)} %copy-done.6) | copy-start | bytes 1572868

commit v5 on v4

--- a/solution.py
+++ b/solution.py
@@ -116,6 +116,20 @@
 
 
 CHUNKS = 2
+
+
+def short_corr_rows(grad, field, tap_count):
+    extra = tap_count - 1
+    row_count = field.shape[0]
+    padded = jnp.concatenate([jnp.zeros((extra, field.shape[1]), field.dtype), field], axis=0)
+    grad_wide = grad.astype(jnp.float32)
+    rows_out = []
+    for tap_index in range(tap_count):
+        start = extra - tap_index
+        rows_out.append(
+            jnp.sum(grad_wide * padded[start : start + row_count].astype(jnp.float32), axis=0)
+        )
+    return jnp.stack(rows_out)
 
 
 def body(section_input, out_grad, short_filter, long_filter):
@@ -169,9 +183,9 @@
     middle = (source.astype(jnp.float32) + long_one).astype(jnp.bfloat16)
     mixed_two = short_mix(middle, short_all[1]).astype(jnp.bfloat16)
     dlong_two = lag_grad(mixed_two, top_grad, group_count, taps)
-    dshort_two = short_corr(dmix_two, middle, tap_count)
+    dshort_two = short_corr_rows(dmix_two.T, middle.T, tap_count)
     dlong_one = lag_grad(mixed_one, middle_grad, group_count, taps)
-    dshort_one = short_corr(dmix_one, source, tap_count)
+    dshort_one = short_corr_rows(dmix_one.T, input_rows, tap_count)
     factor = float(rows * devices) ** (-0.5)
     short_grad = jnp.stack([dshort_one, dshort_two])[None] * factor
     long_grad = jnp.stack([dlong_one, dlong_two])[None] * factor

time: 148 us -> 148 us (level)
  other arithmetic: 37.1 us -> 27.8 us
  waiting for transfers between devices: 29.3 us -> 37.4 us
    reduce_sum x2, other arithmetic: 20.5 us -> 8.68 us  [short_corr_rows(): jnp.sum(grad_wide * padded[start:start + row_count].astype(jnp.float32),...]
    all_to_all x1, waiting for transfers between devices: 0.69 us -> 7.83 us  [body(): lax.all_to_all(behind.T, 'dp', split_axis=0, concat_axis=1, tiled=True)]
    unnamed x2 -> x3, other arithmetic: 2.64 us -> 5.16 us
  transfers between devices with their start and end apart: 5 -> 5, of which waited for: 3 -> 3; matrix products, arithmetic and copies ran while one was open for 39% -> 34% of each run, Pallas kernels for 0% -> 0%
where the time goes in v5:
time: 148 us; the launch traced here: 147 us
  starting transfers between devices  43.1 us (29%)
  waiting for transfers between devices  37.4 us (25%)
  local copies, waits for them, and re-layouts  27.9 us (19%)
  other arithmetic  27.8 us (19%)
  matrix products  9.01 us (6%)
    all_to_all x1, waiting for transfers between devices, body(): lax.all_to_all(out_grad[0], 'dp', split_axis=1, concat_axis=0, tiled=True)  25.4 us
    ppermute x2, starting transfers between devices, from_behind(): return lax.ppermute(shard, axis, pairs)  22.6 us
    unnamed x59, local copies, waits for them, and re-layouts  10.7 us
    all_to_all x1, starting transfers between devices, body(): lax.all_to_all(out_grad[0], 'dp', split_axis=1, concat_axis=0, tiled=True)  10.2 us
    reduce_sum x2, other arithmetic, short_corr_rows(): jnp.sum(grad_wide * padded[start:start + row_count].astype(jnp.float32),...  8.68 us
    all_to_all x1, waiting for transfers between devices, body(): lax.all_to_all(behind.T, 'dp', split_axis=0, concat_axis=1, tiled=True)  7.83 us
    reshape x2, local copies, waits for them, and re-layouts, lag_grad(): skewed = padded.reshape(group_count, taps, 2 * taps + 1)[:, :, :taps]  6.02 us
    all_to_all x1, starting transfers between devices, body(): lax.all_to_all(behind.T, 'dp', split_axis=0, concat_axis=1, tiled=True)  5.26 us
  transfers between devices with their start and end apart: 5, of which 3 were waited for; matrix products, arithmetic and copies ran while one was open for 34% of the time, Pallas kernels for 0%

profile of v5, /device:TPU:6, one launch (start us, length us, event | category | flops | bytes accessed | tf_op | source)
XLA Modules:
  0.0 146.6 jit_solution(10879827496515775995)
XLA Ops:
  0.6 1.6 %copy.34 = bf16[1,128,4096]{1,2,0:T(8,128)(2,1)S(1)} copy(bf16[1,128,4096]{2,1,0:T(8,128)(2,1)} %param.5) | data formatting | bytes 2097152 | tf_op args[1]
  2.3 1.3 copy.35
  3.6 10.2 %all-to-all-start = ((bf16[128,32,128]{2,0,1:T(8,128)(2,1)}), bf16[128,32,128]{2,0,1:T(8,128)(2,1)S(1)}, u32[]{:S(2)}, u32[]{:S(2)}) async-start(bf16[128,32,128]{2,0,1:T(8,128)(2,1)} %copy.35), calls=%async_computation | async-start | bytes 2097152 | tf_op jit(solution)/shard_map/all_to_all | solution.py:143
  14.0 0.7 copy.36
  14.7 1.4 fusion.27
  16.2 1.1 broadcast_select_fusion
  17.3 25.4 %all-to-all-done = bf16[128,32,128]{2,0,1:T(8,128)(2,1)S(1)} async-done(((bf16[128,32,128]{2,0,1:T(8,128)(2,1)}), bf16[128,32,128]{2,0,1:T(8,128)(2,1)S(1)}, u32[]{:S(2)}, u32[]{:S(2)}) %all-to-all-start) | async-done | bytes 1048608 | tf_op jit(solution)/shard_map/all_to_all | solution.py:143
  42.8 0.5 copy.37
  43.3 1.3 copy.40
  44.6 5.0 %all-to-all-start.1 = ((bf16[128,32,128]{2,0,1:T(8,128)(2,1)}), bf16[128,32,128]{2,0,1:T(8,128)(2,1)}, u32[]{:S(2)}, u32[]{:S(2)}) async-start(bf16[128,32,128]{2,0,1:T(8,128)(2,1)} %copy.40), calls=%async_computation.1 | async-start | bytes 2097152 | tf_op jit(solution)/shard_map/all_to_all | solution.py:145
  49.7 0.2 copy.78
  50.3 0.6 copy-done.16
  50.9 0.3 fusion.47
  51.3 0.3 fusion.23
  51.6 0.2 copy.91
  51.8 1.5 %add_convert_fusion.4 = bf16[64,4096]{1,0:T(8,128)(2,1)S(1)} fusion(bf16[64,4096]{1,0:T(8,128)(2,1)S(1)} %bitcast.474, f32[64]{0:T(128)S(1)} %get-tuple-element.83, f32[64]{0:T(128)S(1)} %get-tuple-element.84, f32[64]{0:T(128)S(1)} %get-tuple-element.85, f32[64]{0:T(128)S(1)} %get-tuple-element.86, f32[64]{0:T(128)S(1)} %get-tuple-element.87, ...), kind=kLoop, calls=%fused_computation.80 | loop fusion | flops 6029312 | bytes 1574656 | tf_op jit(solution)/shard_map/convert_element_type | solution.py:162
  53.6 0.3 fusion.46
  53.9 0.3 fusion.24
  54.2 0.2 copy.90
  54.4 2.3 %add_convert_fusion.3 = bf16[64,4096]{1,0:T(8,128)(2,1)} fusion(bf16[64,4096]{1,0:T(8,128)(2,1)S(1)} %bitcast.489, bf16[64,4096]{1,0:T(8,128)(2,1)S(1)} %add_convert_fusion.4, f32[64]{0:T(128)S(1)} %get-tuple-element.76, f32[64]{0:T(128)S(1)} %get-tuple-element.77, f32[64]{0:T(128)S(1)} %get-tuple-element.78, f32[64]{0:T(128)S(1)} %get-tuple-element.79, ...), kind=kLoop, calls=%fused_computation.79 | loop fusion | flops 6029312 | bytes 1574656 | tf_op jit(solution)/shard_map/convert_element_type | solution.py:168
  57.0 11.4 %collective-permute-start = (bf16[64,4096]{1,0:T(8,128)(2,1)}, bf16[64,4096]{1,0:T(8,128)(2,1)}, u32[]{:S(2)}, u32[]{:S(2)}) collective-permute-start(bf16[64,4096]{1,0:T(8,128)(2,1)} %add_convert_fusion.3), channel_id=1, source_target_pairs={{32,0},{64,32},{96,64},{128,96},{160,128},{192,160},{224,192},{256... | collective-permute-start | bytes 1572872 | tf_op jit(solution)/shard_map/ppermute | solution.py:10
  68.4 0.3 fusion.45
  68.7 0.3 fusion.25
  69.0 0.2 copy.89
  69.3 1.5 add_convert_fusion.2
  71.1 0.2 copy.75
  71.4 0.3 fusion.44
  71.7 0.3 fusion.26
  72.0 0.2 copy.88
  72.2 2.3 %add_convert_fusion.1 = bf16[64,4096]{1,0:T(8,128)(2,1)} fusion(bf16[64,4096]{1,0:T(8,128)(2,1)S(1)} %bitcast.491, bf16[64,4096]{1,0:T(8,128)(2,1)S(1)} %add_convert_fusion.2, f32[64]{0:T(128)S(1)} %get-tuple-element.63, f32[64]{0:T(128)S(1)} %get-tuple-element.64, f32[64]{0:T(128)S(1)} %get-tuple-element.65, f32[64]{0:T(128)S(1)} %get-tuple-element.66, ...), kind=kLoop, calls=%fused_computation.77 | loop fusion | flops 6029312 | bytes 1574656 | tf_op jit(solution)/shard_map/convert_element_type | solution.py:168
  74.5 4.1 %all-to-all-done.1 = bf16[128,32,128]{2,0,1:T(8,128)(2,1)} async-done(((bf16[128,32,128]{2,0,1:T(8,128)(2,1)}), bf16[128,32,128]{2,0,1:T(8,128)(2,1)}, u32[]{:S(2)}, u32[]{:S(2)}) %all-to-all-start.1) | async-done | bytes 1048608 | tf_op jit(solution)/shard_map/all_to_all | solution.py:145
  78.6 11.2 %collective-permute-start.1 = (bf16[64,4096]{1,0:T(8,128)(2,1)}, bf16[64,4096]{1,0:T(8,128)(2,1)}, u32[]{:S(2)}, u32[]{:S(2)}) collective-permute-start(bf16[64,4096]{1,0:T(8,128)(2,1)} %add_convert_fusion.1), channel_id=1, source_target_pairs={{32,0},{64,32},{96,64},{128,96},{160,128},{192,160},{224,192},{256... | collective-permute-start | bytes 1572872 | tf_op jit(solution)/shard_map/ppermute | solution.py:10
  89.9 1.5 %copy.43 = bf16[4096,128]{0,1:T(8,128)(2,1)S(1)} copy(bf16[4096,128]{1,0:T(8,128)(2,1)} %bitcast.39) | data formatting | bytes 2097152 | tf_op jit(solution)/shard_map/optimization_barrier | solution.py:175
  91.4 1.0 copy-done.2
  92.3 2.5 %fusion.36 = bf16[16,8,32,128]{3,1,2,0:T(8,128)(2,1)S(1)} fusion(f32[128]{0:T(128)S(1)} %get-tuple-element.53, bf16[128,4096]{1,0:T(8,128)(2,1)S(1)} %bitcast.470, f32[128]{0:T(128)S(1)} %get-tuple-element.54, f32[128]{0:T(128)S(1)} %get-tuple-element.55, f32[128]{0:T(128)S(1)} %get-tuple-element.56, f32[128]{0:T(128)S(1)} %get-tuple-element.57, ...), kind=kLoop, calls=%fused_computation.82 | loop fusion | flops 11010048 | bytes 2100736
  94.9 0.2 copy.73
  95.1 0.4 fusion.43
  95.6 1.5 %convolution_bitcast_fusion.2 = f32[8,128,128]{1,2,0:T(8,128)} fusion(bf16[8,16,31,128]{3,2,1,0:T(8,128)(2,1)S(1)} %bitcast.457, bf16[8,16,32,128]{3,2,1,0:T(8,128)(2,1)S(1)} %bitcast.465), kind=kOutput, calls=%fused_computation.54 | convolution fusion | flops 134217728 | bytes 2588672 | tf_op jit(solution)/shard_map/gcbt,gcbs->gts/dot_general | solution.py:65
  97.1 0.5 convolution_add_fusion
  97.6 0.7 copy-done.3
  98.9 5.9 %fusion.22 = (f32[128]{0:T(128)S(1)}, f32[128]{0:T(128)S(1)}, f32[128]{0:T(128)S(1)}, f32[128]{0:T(128)S(1)}, f32[128]{0:T(128)S(1)}, /*index=5*/f32[128]{0:T(12...) fusion(bf16[4096,128]{0,1:T(8,128)(2,1)S(1)} %copy-done.3, bf16[64,4096]{1,0:T(8,128)(2,1)S(1)} %bitcast.492, ...), kind=kLoop, calls=%fused_computation.40 | loop fusion | flops 18349056 | bytes 6295552 | tf_op jit(solution)/shard_map/reduce_sum | solution.py:130
  104.8 2.3 %maximum_bitcast_fusion = bf16[4096,128]{0,1:T(8,128)(2,1)} fusion(bf16[64,4096]{1,0:T(8,128)(2,1)} %collective-permute-done.1, bf16[64,4096]{1,0:T(8,128)(2,1)} %collective-permute-done), kind=kLoop, calls=%fused_computation.62 | loop fusion | flops 2097152 | bytes 2097152 | tf_op jit(solution)/shard_map/transpose | solution.py:178
  107.0 2.3 %copy.41 = bf16[4096,128]{1,0:T(8,128)(2,1)} copy(bf16[4096,128]{0,1:T(8,128)(2,1)} %maximum_bitcast_fusion) | data formatting | bytes 2097152 | tf_op jit(solution)/shard_map/transpose | solution.py:178
  109.3 5.3 %all-to-all-start.2 = ((bf16[32,128,128]{2,1,0:T(8,128)(2,1)}), bf16[32,128,128]{2,1,0:T(8,128)(2,1)}, u32[]{:S(2)}, u32[]{:S(2)}) async-start(bf16[32,128,128]{2,1,0:T(8,128)(2,1)} %bitcast.495), calls=%async_computation.2 | async-start | bytes 2097152 | tf_op jit(solution)/shard_map/all_to_all | solution.py:178
  114.6 1.7 %fusion.28 = f32[8,128,128]{1,2,0:T(8,128)S(1)} fusion(f32[8,128,128]{1,2,0:T(8,128)} %convolution_bitcast_fusion.2, pred[128,128]{0,1:T(8,128)(4,1)S(1)} %copy.46, bf16[8,16,32,128]{3,2,1,0:T(8,128)(2,1)S(1)} %bitcast.466, bf16[8,16,32,128]{3,2,1,0:T(8,128)(2,1)S(1)} %bitcast.459), kind=kOutput, calls=%fused_computation.56 | convolution fusion | flops 134348800 | bytes 3162112 | tf_op jit(solution)/shard_map/gcbt,gcbs->gts/dot_general | solution.py:62
  116.4 0.3 copy.47
  116.7 0.6 copy.76
  117.3 1.0 concatenate.98
  118.4 3.6 %reshape.552 = f32[8,128,257]{2,1,0:T(8,128)} reshape(f32[8,32896]{1,0:T(8,128)} %concatenate.98) | data formatting | bytes 2105344 | tf_op jit(solution)/shard_map/reshape | solution.py:73
  122.1 2.8 %fusion.15 = (f32[128]{0:T(128)S(1)}, f32[128]{0:T(128)S(1)}, f32[128]{0:T(128)S(1)}, f32[128]{0:T(128)S(1)}, f32[128]{0:T(128)S(1)}, /*index=5*/f32[128]{0:T(128)S(1)}) fusion(bf16[4096,128]{0,1:T(8,128)(2,1)S(1)} %bitcast.469, bf16[64,4096]{1,0:T(8,128)(2,1)S(1)} %bitcast.479, bf16[64,4096]{1,0:T(8,128)(2,1)S(1)} %bitcast.476), kind=kLoop, calls=%fused_computation.26 | loop fusion | flops 11533568 | bytes 2100224 | tf_op jit(solution)/shard_map/reduce_sum | solution.py:130
  124.9 0.6 copy.50
  125.5 2.5 %fusion.35 = bf16[16,8,32,128]{3,1,2,0:T(8,128)(2,1)S(1)} fusion(f32[128]{0:T(128)S(1)} %get-tuple-element.60, bf16[128,4096]{1,0:T(8,128)(2,1)S(1)} %copy-done.1, f32[128]{0:T(128)S(1)} %get-tuple-element.61, f32[128]{0:T(128)S(1)} %get-tuple-element.49, f32[128]{0:T(128)S(1)} %get-tuple-element.50, f32[128]{0:T(128)S(1)} %get-tuple-element.51, ...), kind=kLoop, calls=%fused_computation.81 | loop fusion | flops 11010048 | bytes 2100736
  128.1 0.2 copy.77
  128.3 0.6 convolution_bitcast_fusion
  129.0 0.5 fusion.29
  129.6 0.3 copy.48
  129.9 0.6 copy.79
  130.6 2.4 %reshape.556 = f32[8,128,257]{2,1,0:T(8,128)} reshape(f32[8,32896]{1,0:T(8,128)S(1)} %concatenate.102) | data formatting | bytes 2105344 | tf_op jit(solution)/shard_map/reshape | solution.py:73
  133.1 1.1 slice_reduce_fusion.1
  134.1 1.1 slice_reduce_fusion
  135.2 0.6 maximum_multiply_fusion.1
  135.8 7.8 %all-to-all-done.2 = bf16[32,128,128]{2,1,0:T(8,128)(2,1)} async-done(((bf16[32,128,128]{2,1,0:T(8,128)(2,1)}), bf16[32,128,128]{2,1,0:T(8,128)(2,1)}, u32[]{:S(2)}, u32[]{:S(2)}) %all-to-all-start.2) | async-done | bytes 1048608 | tf_op jit(solution)/shard_map/all_to_all | solution.py:178
  143.7 1.6 %copy.42 = bf16[32,128,128]{1,2,0:T(8,128)(2,1)S(1)} copy(bf16[32,128,128]{2,1,0:T(8,128)(2,1)} %all-to-all-done.2) | data formatting | bytes 2097152 | tf_op jit(solution)/shard_map/all_to_all | solution.py:178
  145.3 1.3 copy.49
  (61 shorter events, 2.6 us)
Async XLA Ops:
  0.6 14.1 %copy-start = (bf16[1,2,8,128]{3,2,1,0:T(8,128)(2,1)S(1)}, bf16[1,2,8,128]{3,2,1,0:T(8,128)(2,1)}, u32[]{:S(2)}) copy-start(bf16[1,2,8,128]{3,2,1,0:T(8,128)(2,1)} %param.7) | copy-start | bytes 12292
  2.3 11.7 %copy-start.18 = (bf16[1,128,4096]{2,1,0:T(8,128)(2,1)S(1)}, bf16[1,128,4096]{2,1,0:T(8,128)(2,1)}, u32[]{:S(2)}) copy-start(bf16[1,128,4096]{2,1,0:T(8,128)(2,1)} %param.4) | copy-start | bytes 3145732
  3.6 39.2 %all-to-all-start = ((bf16[128,32,128]{2,0,1:T(8,128)(2,1)}), bf16[128,32,128]{2,0,1:T(8,128)(2,1)S(1)}, u32[]{:S(2)}, u32[]{:S(2)}) async-start(bf16[128,32,128]{2,0,1:T(8,128)(2,1)} %copy.35), calls=%async_computation | async-start | bytes 2097152 | tf_op jit(solution)/shard_map/all_to_all | solution.py:143
  14.6 1.4 copy-start.19
  44.6 34.0 %all-to-all-start.1 = ((bf16[128,32,128]{2,0,1:T(8,128)(2,1)}), bf16[128,32,128]{2,0,1:T(8,128)(2,1)}, u32[]{:S(2)}, u32[]{:S(2)}) async-start(bf16[128,32,128]{2,0,1:T(8,128)(2,1)} %copy.40), calls=%async_computation.1 | async-start | bytes 2097152 | tf_op jit(solution)/shard_map/all_to_all | solution.py:145
  49.9 1.0 copy-start.16
  50.0 1.3 copy-start.14
  51.8 2.1 %copy-start.4 = (bf16[8,8,32,128]{3,1,2,0:T(8,128)(2,1)}, bf16[8,8,32,128]{3,1,2,0:T(8,128)(2,1)S(1)}, u32[]{:S(2)}) copy-start(bf16[8,8,32,128]{3,1,2,0:T(8,128)(2,1)S(1)} %copy.91) | copy-start | bytes 1572868
  54.4 14.3 %copy-start.10 = (bf16[8,8,32,128]{3,1,2,0:T(8,128)(2,1)}, bf16[8,8,32,128]{3,1,2,0:T(8,128)(2,1)S(1)}, u32[]{:S(2)}) copy-start(bf16[8,8,32,128]{3,1,2,0:T(8,128)(2,1)S(1)} %copy.90) | copy-start | bytes 1572868
  57.0 47.8 %collective-permute-start = (bf16[64,4096]{1,0:T(8,128)(2,1)}, bf16[64,4096]{1,0:T(8,128)(2,1)}, u32[]{:S(2)}, u32[]{:S(2)}) collective-permute-start(bf16[64,4096]{1,0:T(8,128)(2,1)} %add_convert_fusion.3), channel_id=1, source_target_pairs={{32,0},{64,32},{96,64},{128,96},{160,128},{192,160},{224,192},{256... | collective-permute-start | bytes 1572872 | tf_op jit(solution)/shard_map/ppermute | solution.py:10
  69.3 1.9 %copy-start.7 = (bf16[8,8,32,128]{3,1,2,0:T(8,128)(2,1)}, bf16[8,8,32,128]{3,1,2,0:T(8,128)(2,1)S(1)}, u32[]{:S(2)}) copy-start(bf16[8,8,32,128]{3,1,2,0:T(8,128)(2,1)S(1)} %copy.89) | copy-start | bytes 1572868
  72.2 6.4 %copy-start.12 = (bf16[8,8,32,128]{3,1,2,0:T(8,128)(2,1)}, bf16[8,8,32,128]{3,1,2,0:T(8,128)(2,1)S(1)}, u32[]{:S(2)}) copy-start(bf16[8,8,32,128]{3,1,2,0:T(8,128)(2,1)S(1)} %copy.88) | copy-start | bytes 1572868
  78.6 26.1 %collective-permute-start.1 = (bf16[64,4096]{1,0:T(8,128)(2,1)}, bf16[64,4096]{1,0:T(8,128)(2,1)}, u32[]{:S(2)}, u32[]{:S(2)}) collective-permute-start(bf16[64,4096]{1,0:T(8,128)(2,1)} %add_convert_fusion.1), channel_id=1, source_target_pairs={{32,0},{64,32},{96,64},{128,96},{160,128},{192,160},{224,192},{256... | collective-permute-start | bytes 1572872 | tf_op jit(solution)/shard_map/ppermute | solution.py:10
  91.4 1.0 copy-start.2
  92.3 2.8 %copy-start.17 = (bf16[2,8,128,128]{3,2,1,0:T(8,128)(2,1)S(1)}, bf16[2,8,128,128]{3,2,1,0:T(8,128)(2,1)}, u32[]{:S(2)}) copy-start(bf16[2,8,128,128]{3,2,1,0:T(8,128)(2,1)} %get-tuple-element.47) | copy-start | bytes 1572868
  95.6 1.5 %copy-start.15 = (bf16[2,8,128,128]{3,2,1,0:T(8,128)(2,1)S(1)}, bf16[2,8,128,128]{3,2,1,0:T(8,128)(2,1)}, u32[]{:S(2)}) copy-start(bf16[2,8,128,128]{3,2,1,0:T(8,128)(2,1)} %get-tuple-element.46) | copy-start | bytes 1572868
  97.1 1.2 copy-start.3
  97.1 1.4 copy-start.5
  97.1 1.5 %copy-start.8 = (bf16[8,8,32,128]{3,1,2,0:T(8,128)(2,1)S(1)}, bf16[8,8,32,128]{3,1,2,0:T(8,128)(2,1)}, u32[]{:S(2)}) copy-start(bf16[8,8,32,128]{3,1,2,0:T(8,128)(2,1)} %copy-done.7) | copy-start | bytes 1572868
  97.1 1.7 %copy-start.11 = (bf16[8,8,32,128]{3,1,2,0:T(8,128)(2,1)S(1)}, bf16[8,8,32,128]{3,1,2,0:T(8,128)(2,1)}, u32[]{:S(2)}) copy-start(bf16[8,8,32,128]{3,1,2,0:T(8,128)(2,1)} %copy-done.10) | copy-start | bytes 1572868
  97.1 1.8 %copy-start.13 = (bf16[8,8,32,128]{3,1,2,0:T(8,128)(2,1)S(1)}, bf16[8,8,32,128]{3,1,2,0:T(8,128)(2,1)}, u32[]{:S(2)}) copy-start(bf16[8,8,32,128]{3,1,2,0:T(8,128)(2,1)} %copy-done.12) | copy-start | bytes 1572868
  109.3 34.3 %all-to-all-start.2 = ((bf16[32,128,128]{2,1,0:T(8,128)(2,1)}), bf16[32,128,128]{2,1,0:T(8,128)(2,1)}, u32[]{:S(2)}, u32[]{:S(2)}) async-start(bf16[32,128,128]{2,1,0:T(8,128)(2,1)} %bitcast.495), calls=%async_computation.2 | async-start | bytes 2097152 | tf_op jit(solution)/shard_map/all_to_all | solution.py:178
  117.3 4.7 %copy-start.1 = (bf16[128,4096]{1,0:T(8,128)(2,1)S(1)}, bf16[128,4096]{1,0:T(8,128)(2,1)}, u32[]{:S(2)}) copy-start(bf16[128,4096]{1,0:T(8,128)(2,1)} %get-tuple-element.43) | copy-start | bytes 3145732
  117.3 4.7 %copy-start.6 = (bf16[8,8,32,128]{3,1,2,0:T(8,128)(2,1)S(1)}, bf16[8,8,32,128]{3,1,2,0:T(8,128)(2,1)}, u32[]{:S(2)}) copy-start(bf16[8,8,32,128]{3,1,2,0:T(8,128)(2,1)} %copy-done.4) | copy-start | bytes 1572868
  117.3 4.7 %copy-start.9 = (bf16[8,8,32,128]{3,1,2,0:T(8,128)(2,1)S(1)}, bf16[8,8,32,128]{3,1,2,0:T(8,128)(2,1)}, u32[]{:S(2)}) copy-start(bf16[8,8,32,128]{3,1,2,0:T(8,128)(2,1)} %copy-done.7) | copy-start | bytes 1572868

commit v6 on v5

--- a/solution.py
+++ b/solution.py
@@ -172,8 +172,8 @@
     dmix_two = jnp.concatenate(dmix_twos)
     middle_grad = jnp.concatenate(middle_grads)
     dmix_one = jnp.concatenate(dmix_ones)
-    input_rows, input_grad_h = lax.optimization_barrier((input_rows, input_grad_h))
     behinds.append(from_behind(input_grad_h, "pipe", -1))
+    input_rows, _ = lax.optimization_barrier((input_rows, input_grad_h))
     behind = jnp.concatenate(behinds)
     own_rows = lax.all_to_all(behind.T, "dp", split_axis=0, concat_axis=1, tiled=True)
     passed_grad = own_rows[None]

time: 148 us -> 146 us (0.986)
  waiting for transfers between devices: 37.4 us -> 44.7 us
  starting transfers between devices: 43.1 us -> 38.7 us
  other arithmetic: 27.8 us -> 25.3 us
  matrix products: 9.01 us -> 7.06 us
    ppermute x2, waiting for transfers between devices: 0.01 us -> 19.1 us  [from_behind(): return lax.ppermute(shard, axis, pairs)]
    ppermute x2, starting transfers between devices: 22.6 us -> 13.8 us  [from_behind(): return lax.ppermute(shard, axis, pairs)]
    all_to_all x1, waiting for transfers between devices: 7.83 us -> 0.01 us  [body(): lax.all_to_all(behind.T, 'dp', split_axis=0, concat_axis=1, tiled=True)]
    all_to_all x1, starting transfers between devices: 5.26 us -> 9.56 us  [body(): lax.all_to_all(behind.T, 'dp', split_axis=0, concat_axis=1, tiled=True)]
    all_to_all x1, waiting for transfers between devices: 4.12 us -> 0.01 us  [body(): lax.all_to_all(later_input, 'dp', split_axis=1, concat_axis=0, tiled=True)]
    unnamed x59 -> x57, local copies, waits for them, and re-layouts: 10.7 us -> 11.3 us
where the time goes in v6:
time: 146 us; the launch traced here: 145 us
  waiting for transfers between devices  44.7 us (31%)
  starting transfers between devices  38.7 us (27%)
  local copies, waits for them, and re-layouts  27.6 us (19%)
  other arithmetic  25.3 us (17%)
  matrix products  7.06 us (5%)
    all_to_all x1, waiting for transfers between devices, body(): lax.all_to_all(out_grad[0], 'dp', split_axis=1, concat_axis=0, tiled=True)  25.6 us
    ppermute x2, waiting for transfers between devices, from_behind(): return lax.ppermute(shard, axis, pairs)  19.1 us
    ppermute x2, starting transfers between devices, from_behind(): return lax.ppermute(shard, axis, pairs)  13.8 us
    unnamed x57, local copies, waits for them, and re-layouts  11.3 us
    all_to_all x1, starting transfers between devices, body(): lax.all_to_all(out_grad[0], 'dp', split_axis=1, concat_axis=0, tiled=True)  10.2 us
    all_to_all x1, starting transfers between devices, body(): lax.all_to_all(behind.T, 'dp', split_axis=0, concat_axis=1, tiled=True)  9.56 us
    reduce_sum x2, other arithmetic, short_corr_rows(): jnp.sum(grad_wide * padded[start:start + row_count].astype(jnp.float32),...  7.93 us
    unnamed x3, other arithmetic  5.44 us
  transfers between devices with their start and end apart: 5, of which 3 were waited for; matrix products, arithmetic and copies ran while one was open for 34% of the time, Pallas kernels for 0%

profile of v6, /device:TPU:6, one launch (start us, length us, event | category | flops | bytes accessed | tf_op | source)
XLA Modules:
  0.0 144.6 jit_solution(3724898164072475388)
XLA Ops:
  0.6 1.6 %copy.34 = bf16[1,128,4096]{1,2,0:T(8,128)(2,1)S(1)} copy(bf16[1,128,4096]{2,1,0:T(8,128)(2,1)} %param.5) | data formatting | bytes 2097152 | tf_op args[1]
  2.3 1.3 copy.35
  3.6 10.2 %all-to-all-start = ((bf16[128,32,128]{2,0,1:T(8,128)(2,1)}), bf16[128,32,128]{2,0,1:T(8,128)(2,1)S(1)}, u32[]{:S(2)}, u32[]{:S(2)}) async-start(bf16[128,32,128]{2,0,1:T(8,128)(2,1)} %copy.35), calls=%async_computation | async-start | bytes 2097152 | tf_op jit(solution)/shard_map/all_to_all | solution.py:143
  13.8 0.7 copy.36
  14.6 1.4 fusion.27
  16.0 1.1 broadcast_select_fusion
  17.2 25.6 %all-to-all-done = bf16[128,32,128]{2,0,1:T(8,128)(2,1)S(1)} async-done(((bf16[128,32,128]{2,0,1:T(8,128)(2,1)}), bf16[128,32,128]{2,0,1:T(8,128)(2,1)S(1)}, u32[]{:S(2)}, u32[]{:S(2)}) %all-to-all-start) | async-done | bytes 1048608 | tf_op jit(solution)/shard_map/all_to_all | solution.py:143
  42.8 0.5 copy.37
  43.3 1.3 copy.42
  44.6 5.0 %all-to-all-start.2 = ((bf16[128,32,128]{2,0,1:T(8,128)(2,1)}), bf16[128,32,128]{2,0,1:T(8,128)(2,1)}, u32[]{:S(2)}, u32[]{:S(2)}) async-start(bf16[128,32,128]{2,0,1:T(8,128)(2,1)} %copy.42), calls=%async_computation.2 | async-start | bytes 2097152 | tf_op jit(solution)/shard_map/all_to_all | solution.py:145
  50.1 0.7 copy-done.15
  50.7 0.3 fusion.47
  51.0 0.3 fusion.23
  51.3 0.2 copy.91
  51.6 1.5 %add_convert_fusion.4 = bf16[64,4096]{1,0:T(8,128)(2,1)S(1)} fusion(bf16[64,4096]{1,0:T(8,128)(2,1)S(1)} %bitcast.474, f32[64]{0:T(128)S(1)} %get-tuple-element.81, f32[64]{0:T(128)S(1)} %get-tuple-element.82, f32[64]{0:T(128)S(1)} %get-tuple-element.83, f32[64]{0:T(128)S(1)} %get-tuple-element.84, f32[64]{0:T(128)S(1)} %get-tuple-element.85, ...), kind=kLoop, calls=%fused_computation.80 | loop fusion | flops 6029312 | bytes 1574656 | tf_op jit(solution)/shard_map/convert_element_type | solution.py:162
  53.3 0.3 fusion.46
  53.7 0.3 fusion.24
  54.0 0.2 copy.90
  54.2 2.3 %add_convert_fusion.3 = bf16[64,4096]{1,0:T(8,128)(2,1)} fusion(bf16[64,4096]{1,0:T(8,128)(2,1)S(1)} %bitcast.489, bf16[64,4096]{1,0:T(8,128)(2,1)S(1)} %add_convert_fusion.4, f32[64]{0:T(128)S(1)} %get-tuple-element.74, f32[64]{0:T(128)S(1)} %get-tuple-element.75, f32[64]{0:T(128)S(1)} %get-tuple-element.76, f32[64]{0:T(128)S(1)} %get-tuple-element.77, ...), kind=kLoop, calls=%fused_computation.79 | loop fusion | flops 6029312 | bytes 1574656 | tf_op jit(solution)/shard_map/convert_element_type | solution.py:168
  56.6 0.2 slice.563
  56.8 11.4 %collective-permute-start = (bf16[64,4096]{1,0:T(8,128)(2,1)}, bf16[64,4096]{1,0:T(8,128)(2,1)}, u32[]{:S(2)}, u32[]{:S(2)}) collective-permute-start(bf16[64,4096]{1,0:T(8,128)(2,1)} %add_convert_fusion.3), channel_id=1, source_target_pairs={{32,0},{64,32},{96,64},{128,96},{160,128},{192,160},{224,192},{256... | collective-permute-start | bytes 1572872 | tf_op jit(solution)/shard_map/ppermute | solution.py:10
  68.2 0.3 fusion.45
  68.5 0.3 fusion.25
  68.8 0.2 copy.89
  69.0 1.5 %add_convert_fusion.2 = bf16[64,4096]{1,0:T(8,128)(2,1)S(1)} fusion(bf16[64,4096]{1,0:T(8,128)(2,1)S(1)} %bitcast.477, bf16[64,4096]{1,0:T(8,128)(2,1)S(1)} %get-tuple-element.10, f32[64]{0:T(128)S(1)} %get-tuple-element.67, f32[64]{0:T(128)S(1)} %get-tuple-element.68, f32[64]{0:T(128)S(1)} %get-tuple-element.69, f32[64]{0:T(128)S(1)} %get-tuple-element.70, ...), kind=kLoop, calls=%fused_computation.78 | loop fusion | flops 6029312 | bytes 1574656 | tf_op jit(solution)/shard_map/convert_element_type | solution.py:162
  70.8 0.3 fusion.44
  71.1 0.3 fusion.26
  71.4 0.2 copy.88
  71.7 2.3 %add_convert_fusion.1 = bf16[64,4096]{1,0:T(8,128)(2,1)} fusion(bf16[64,4096]{1,0:T(8,128)(2,1)S(1)} %bitcast.491, bf16[64,4096]{1,0:T(8,128)(2,1)S(1)} %add_convert_fusion.2, f32[64]{0:T(128)S(1)} %get-tuple-element.61, f32[64]{0:T(128)S(1)} %get-tuple-element.62, f32[64]{0:T(128)S(1)} %get-tuple-element.63, f32[64]{0:T(128)S(1)} %get-tuple-element.64, ...), kind=kLoop, calls=%fused_computation.77 | loop fusion | flops 6029312 | bytes 1574656 | tf_op jit(solution)/shard_map/convert_element_type | solution.py:168
  73.9 2.5 %collective-permute-start.1 = (bf16[64,4096]{1,0:T(8,128)(2,1)}, bf16[64,4096]{1,0:T(8,128)(2,1)}, u32[]{:S(2)}, u32[]{:S(2)}) collective-permute-start(bf16[64,4096]{1,0:T(8,128)(2,1)} %add_convert_fusion.1), channel_id=1, source_target_pairs={{32,0},{64,32},{96,64},{128,96},{160,128},{192,160},{224,192},{256... | collective-permute-start | bytes 1572872 | tf_op jit(solution)/shard_map/ppermute | solution.py:10
  76.5 0.2 copy.78
  76.9 0.2 copy.75
  77.2 8.6 %collective-permute-done = bf16[64,4096]{1,0:T(8,128)(2,1)} collective-permute-done((bf16[64,4096]{1,0:T(8,128)(2,1)}, bf16[64,4096]{1,0:T(8,128)(2,1)}, u32[]{:S(2)}, u32[]{:S(2)}) %collective-permute-start) | collective-permute-done | bytes 524320 | tf_op jit(solution)/shard_map/ppermute | solution.py:10
  85.8 10.4 %collective-permute-done.1 = bf16[64,4096]{1,0:T(8,128)(2,1)} collective-permute-done((bf16[64,4096]{1,0:T(8,128)(2,1)}, bf16[64,4096]{1,0:T(8,128)(2,1)}, u32[]{:S(2)}, u32[]{:S(2)}) %collective-permute-start.1) | collective-permute-done | bytes 524320 | tf_op jit(solution)/shard_map/ppermute | solution.py:10
  96.2 1.3 maximum_bitcast_fusion
  97.5 1.3 copy.40
  98.8 9.6 %all-to-all-start.1 = ((bf16[32,128,128]{2,1,0:T(8,128)(2,1)}), bf16[32,128,128]{2,1,0:T(8,128)(2,1)}, u32[]{:S(2)}, u32[]{:S(2)}) async-start(bf16[32,128,128]{2,1,0:T(8,128)(2,1)} %bitcast.64), calls=%async_computation.1 | async-start | bytes 2097152 | tf_op jit(solution)/shard_map/all_to_all | solution.py:178
  108.4 1.5 %copy.43 = bf16[4096,128]{0,1:T(8,128)(2,1)S(1)} copy(bf16[4096,128]{1,0:T(8,128)(2,1)} %bitcast.70) | data formatting | bytes 2097152 | tf_op jit(solution)/shard_map/optimization_barrier | solution.py:176
  109.9 2.6 %fusion.36 = bf16[16,8,32,128]{3,1,2,0:T(8,128)(2,1)S(1)} fusion(f32[128]{0:T(128)S(1)} %get-tuple-element.51, bf16[128,4096]{1,0:T(8,128)(2,1)S(1)} %bitcast.470, f32[128]{0:T(128)S(1)} %get-tuple-element.52, f32[128]{0:T(128)S(1)} %get-tuple-element.53, f32[128]{0:T(128)S(1)} %get-tuple-element.54, f32[128]{0:T(128)S(1)} %get-tuple-element.55, ...), kind=kLoop, calls=%fused_computation.82 | loop fusion | flops 11010048 | bytes 2100736
  112.5 0.2 copy.73
  112.8 0.4 fusion.43
  113.2 0.7 convolution_bitcast_fusion.2
  113.9 0.4 copy-done.14
  114.3 0.5 convolution_add_fusion
  114.7 0.7 copy-done.2
  116.1 5.1 %fusion.22 = (f32[128]{0:T(128)S(1)}, f32[128]{0:T(128)S(1)}, f32[128]{0:T(128)S(1)}, f32[128]{0:T(128)S(1)}, f32[128]{0:T(128)S(1)}, /*index=5*/f32[128]{0:T(12...) fusion(bf16[4096,128]{0,1:T(8,128)(2,1)S(1)} %copy-done.2, bf16[64,4096]{1,0:T(8,128)(2,1)S(1)} %bitcast.492, ...), kind=kLoop, calls=%fused_computation.40 | loop fusion | flops 18349056 | bytes 6295552 | tf_op jit(solution)/shard_map/reduce_sum | solution.py:130
  121.2 0.5 fusion.28
  121.8 1.4 copy.47
  123.2 1.8 %copy.76 = f32[1,8,128,256]{3,1,2,0:T(8,128)S(1)} copy(f32[1,8,128,256]{3,2,1,0:T(8,128)} %bitcast.497) | data formatting | bytes 2097152
  125.1 1.1 concatenate.98
  126.2 3.6 %reshape.552 = f32[8,128,257]{2,1,0:T(8,128)} reshape(f32[8,32896]{1,0:T(8,128)} %concatenate.98) | data formatting | bytes 2105344 | tf_op jit(solution)/shard_map/reshape | solution.py:73
  129.8 2.8 %fusion.15 = (f32[128]{0:T(128)S(1)}, f32[128]{0:T(128)S(1)}, f32[128]{0:T(128)S(1)}, f32[128]{0:T(128)S(1)}, f32[128]{0:T(128)S(1)}, /*index=5*/f32[128]{0:T(128)S(1)}) fusion(bf16[4096,128]{0,1:T(8,128)(2,1)S(1)} %bitcast.469, bf16[64,4096]{1,0:T(8,128)(2,1)S(1)} %bitcast.479, bf16[64,4096]{1,0:T(8,128)(2,1)S(1)} %bitcast.476), kind=kLoop, calls=%fused_computation.26 | loop fusion | flops 11533568 | bytes 2100224 | tf_op jit(solution)/shard_map/reduce_sum | solution.py:130
  132.7 0.6 copy.50
  133.3 2.8 %fusion.35 = bf16[16,8,32,128]{3,1,2,0:T(8,128)(2,1)S(1)} fusion(f32[128]{0:T(128)S(1)} %get-tuple-element.58, bf16[128,4096]{1,0:T(8,128)(2,1)S(1)} %get-tuple-element.41, f32[128]{0:T(128)S(1)} %get-tuple-element.59, f32[128]{0:T(128)S(1)} %get-tuple-element.47, f32[128]{0:T(128)S(1)} %get-tuple-element.48, f32[128]{0:T(128)S(1)} %get-tuple-element.49, ...), kind=kLoop, calls=%fused_computation.81 | loop fusion | flops 11010048 | bytes 2100736
  136.1 0.2 copy.77
  136.3 0.7 convolution_bitcast_fusion
  137.0 0.5 fusion.29
  137.6 0.3 copy.48
  137.9 0.6 copy.79
  138.6 1.3 reshape.556
  139.9 1.1 slice_reduce_fusion.1
  141.1 0.6 maximum_multiply_fusion.1
  141.7 1.6 %copy.41 = bf16[32,128,128]{1,2,0:T(8,128)(2,1)S(1)} copy(bf16[32,128,128]{2,1,0:T(8,128)(2,1)} %all-to-all-done.1) | data formatting | bytes 2097152 | tf_op jit(solution)/shard_map/all_to_all | solution.py:178
  143.3 1.3 copy.49
  (59 shorter events, 2.4 us)
Async XLA Ops:
  0.6 13.9 %copy-start = (bf16[1,2,8,128]{3,2,1,0:T(8,128)(2,1)S(1)}, bf16[1,2,8,128]{3,2,1,0:T(8,128)(2,1)}, u32[]{:S(2)}) copy-start(bf16[1,2,8,128]{3,2,1,0:T(8,128)(2,1)} %param.7) | copy-start | bytes 12292
  2.3 11.6 %copy-start.17 = (bf16[1,128,4096]{2,1,0:T(8,128)(2,1)S(1)}, bf16[1,128,4096]{2,1,0:T(8,128)(2,1)}, u32[]{:S(2)}) copy-start(bf16[1,128,4096]{2,1,0:T(8,128)(2,1)} %param.4) | copy-start | bytes 3145732
  3.6 39.2 %all-to-all-start = ((bf16[128,32,128]{2,0,1:T(8,128)(2,1)}), bf16[128,32,128]{2,0,1:T(8,128)(2,1)S(1)}, u32[]{:S(2)}, u32[]{:S(2)}) async-start(bf16[128,32,128]{2,0,1:T(8,128)(2,1)} %copy.35), calls=%async_computation | async-start | bytes 2097152 | tf_op jit(solution)/shard_map/all_to_all | solution.py:143
  14.5 1.4 copy-start.18
  44.6 54.2 %all-to-all-start.2 = ((bf16[128,32,128]{2,0,1:T(8,128)(2,1)}), bf16[128,32,128]{2,0,1:T(8,128)(2,1)}, u32[]{:S(2)}, u32[]{:S(2)}) async-start(bf16[128,32,128]{2,0,1:T(8,128)(2,1)} %copy.42), calls=%async_computation.2 | async-start | bytes 2097152 | tf_op jit(solution)/shard_map/all_to_all | solution.py:145
  49.7 1.0 copy-start.15
  49.8 1.3 copy-start.13
  51.6 2.1 %copy-start.3 = (bf16[8,8,32,128]{3,1,2,0:T(8,128)(2,1)}, bf16[8,8,32,128]{3,1,2,0:T(8,128)(2,1)S(1)}, u32[]{:S(2)}) copy-start(bf16[8,8,32,128]{3,1,2,0:T(8,128)(2,1)S(1)} %copy.91) | copy-start | bytes 1572868
  54.2 2.3 %copy-start.9 = (bf16[8,8,32,128]{3,1,2,0:T(8,128)(2,1)}, bf16[8,8,32,128]{3,1,2,0:T(8,128)(2,1)S(1)}, u32[]{:S(2)}) copy-start(bf16[8,8,32,128]{3,1,2,0:T(8,128)(2,1)S(1)} %copy.90) | copy-start | bytes 1572868
  56.8 29.0 %collective-permute-start = (bf16[64,4096]{1,0:T(8,128)(2,1)}, bf16[64,4096]{1,0:T(8,128)(2,1)}, u32[]{:S(2)}, u32[]{:S(2)}) collective-permute-start(bf16[64,4096]{1,0:T(8,128)(2,1)} %add_convert_fusion.3), channel_id=1, source_target_pairs={{32,0},{64,32},{96,64},{128,96},{160,128},{192,160},{224,192},{256... | collective-permute-start | bytes 1572872 | tf_op jit(solution)/shard_map/ppermute | solution.py:10
  69.0 2.1 %copy-start.6 = (bf16[8,8,32,128]{3,1,2,0:T(8,128)(2,1)}, bf16[8,8,32,128]{3,1,2,0:T(8,128)(2,1)S(1)}, u32[]{:S(2)}) copy-start(bf16[8,8,32,128]{3,1,2,0:T(8,128)(2,1)S(1)} %copy.89) | copy-start | bytes 1572868
  71.7 4.9 %copy-start.11 = (bf16[8,8,32,128]{3,1,2,0:T(8,128)(2,1)}, bf16[8,8,32,128]{3,1,2,0:T(8,128)(2,1)S(1)}, u32[]{:S(2)}) copy-start(bf16[8,8,32,128]{3,1,2,0:T(8,128)(2,1)S(1)} %copy.88) | copy-start | bytes 1572868
  73.9 22.3 %collective-permute-start.1 = (bf16[64,4096]{1,0:T(8,128)(2,1)}, bf16[64,4096]{1,0:T(8,128)(2,1)}, u32[]{:S(2)}, u32[]{:S(2)}) collective-permute-start(bf16[64,4096]{1,0:T(8,128)(2,1)} %add_convert_fusion.1), channel_id=1, source_target_pairs={{32,0},{64,32},{96,64},{128,96},{160,128},{192,160},{224,192},{256... | collective-permute-start | bytes 1572872 | tf_op jit(solution)/shard_map/ppermute | solution.py:10
  98.8 42.8 %all-to-all-start.1 = ((bf16[32,128,128]{2,1,0:T(8,128)(2,1)}), bf16[32,128,128]{2,1,0:T(8,128)(2,1)}, u32[]{:S(2)}, u32[]{:S(2)}) async-start(bf16[32,128,128]{2,1,0:T(8,128)(2,1)} %bitcast.64), calls=%async_computation.1 | async-start | bytes 2097152 | tf_op jit(solution)/shard_map/all_to_all | solution.py:178
  109.9 2.8 %copy-start.1 = (bf16[4096,128]{0,1:T(8,128)(2,1)}, bf16[4096,128]{0,1:T(8,128)(2,1)S(1)}, u32[]{:S(2)}) copy-start(bf16[4096,128]{0,1:T(8,128)(2,1)S(1)} %copy.43) | copy-start | bytes 3145732
  109.9 2.8 %copy-start.16 = (bf16[2,8,128,128]{3,2,1,0:T(8,128)(2,1)S(1)}, bf16[2,8,128,128]{3,2,1,0:T(8,128)(2,1)}, u32[]{:S(2)}) copy-start(bf16[2,8,128,128]{3,2,1,0:T(8,128)(2,1)} %get-tuple-element.45) | copy-start | bytes 1572868
  113.2 1.0 copy-start.14
  114.2 1.2 copy-start.2
  114.2 1.4 copy-start.4
  114.2 1.5 %copy-start.7 = (bf16[8,8,32,128]{3,1,2,0:T(8,128)(2,1)S(1)}, bf16[8,8,32,128]{3,1,2,0:T(8,128)(2,1)}, u32[]{:S(2)}) copy-start(bf16[8,8,32,128]{3,1,2,0:T(8,128)(2,1)} %copy-done.6) | copy-start | bytes 1572868
  114.3 1.7 %copy-start.10 = (bf16[8,8,32,128]{3,1,2,0:T(8,128)(2,1)S(1)}, bf16[8,8,32,128]{3,1,2,0:T(8,128)(2,1)}, u32[]{:S(2)}) copy-start(bf16[8,8,32,128]{3,1,2,0:T(8,128)(2,1)} %copy-done.9) | copy-start | bytes 1572868
  114.3 1.8 %copy-start.12 = (bf16[8,8,32,128]{3,1,2,0:T(8,128)(2,1)S(1)}, bf16[8,8,32,128]{3,1,2,0:T(8,128)(2,1)}, u32[]{:S(2)}) copy-start(bf16[8,8,32,128]{3,1,2,0:T(8,128)(2,1)} %copy-done.11) | copy-start | bytes 1572868
  125.0 4.7 %copy-start.5 = (bf16[8,8,32,128]{3,1,2,0:T(8,128)(2,1)S(1)}, bf16[8,8,32,128]{3,1,2,0:T(8,128)(2,1)}, u32[]{:S(2)}) copy-start(bf16[8,8,32,128]{3,1,2,0:T(8,128)(2,1)} %copy-done.3) | copy-start | bytes 1572868
  125.1 4.7 %copy-start.8 = (bf16[8,8,32,128]{3,1,2,0:T(8,128)(2,1)S(1)}, bf16[8,8,32,128]{3,1,2,0:T(8,128)(2,1)}, u32[]{:S(2)}) copy-start(bf16[8,8,32,128]{3,1,2,0:T(8,128)(2,1)} %copy-done.6) | copy-start | bytes 1572868

commit v7 on v6

--- a/solution.py
+++ b/solution.py
@@ -174,14 +174,15 @@
     dmix_one = jnp.concatenate(dmix_ones)
     behinds.append(from_behind(input_grad_h, "pipe", -1))
     input_rows, _ = lax.optimization_barrier((input_rows, input_grad_h))
-    behind = jnp.concatenate(behinds)
-    own_rows = lax.all_to_all(behind.T, "dp", split_axis=0, concat_axis=1, tiled=True)
-    passed_grad = own_rows[None]
     source = input_rows.T
     mixed_one = short_mix(source, short_all[0]).astype(jnp.bfloat16)
     long_one = causal_long(mixed_one, circ_now[0], circ_past[0])
     middle = (source.astype(jnp.float32) + long_one).astype(jnp.bfloat16)
     mixed_two = short_mix(middle, short_all[1]).astype(jnp.bfloat16)
+    behinds = list(lax.optimization_barrier((*behinds, mixed_two))[:-1])
+    behind = jnp.concatenate(behinds)
+    own_rows = lax.all_to_all(behind.T, "dp", split_axis=0, concat_axis=1, tiled=True)
+    passed_grad = own_rows[None]
     dlong_two = lag_grad(mixed_two, top_grad, group_count, taps)
     dshort_two = short_corr_rows(dmix_two.T, middle.T, tap_count)
     dlong_one = lag_grad(mixed_one, middle_grad, group_count, taps)

time: 146 us -> 143 us (0.979)
  waiting for transfers between devices: 44.7 us -> 37.3 us
  other arithmetic: 25.3 us -> 27.8 us
  matrix products: 7.06 us -> 8.98 us
    ppermute x2, waiting for transfers between devices: 19.1 us -> 2.38 us  [from_behind(): return lax.ppermute(shard, axis, pairs)]
    all_to_all x1, waiting for transfers between devices: 0.01 us -> 7.76 us  [body(): lax.all_to_all(behind.T, 'dp', split_axis=0, concat_axis=1, tiled=True)]
    all_to_all x1, waiting for transfers between devices: 0.01 us -> 1.63 us  [body(): lax.all_to_all(later_input, 'dp', split_axis=1, concat_axis=0, tiled=True)]
    unnamed x57 -> x59, local copies, waits for them, and re-layouts: 11.3 us -> 11.3 us
  transfers between devices with their start and end apart: 5 -> 5, of which waited for: 3 -> 4; matrix products, arithmetic and copies ran while one was open for 34% -> 35% of each run, Pallas kernels for 0% -> 0%
where the time goes in v7:
time: 143 us; the launch traced here: 142 us
  starting transfers between devices  38.6 us (27%)
  waiting for transfers between devices  37.3 us (26%)
  local copies, waits for them, and re-layouts  28.5 us (20%)
  other arithmetic  27.8 us (19%)
  matrix products  8.98 us (6%)
    all_to_all x1, waiting for transfers between devices, body(): lax.all_to_all(out_grad[0], 'dp', split_axis=1, concat_axis=0, tiled=True)  25.5 us
    ppermute x2, starting transfers between devices, from_behind(): return lax.ppermute(shard, axis, pairs)  13.8 us
    unnamed x59, local copies, waits for them, and re-layouts  11.3 us
    all_to_all x1, starting transfers between devices, body(): lax.all_to_all(out_grad[0], 'dp', split_axis=1, concat_axis=0, tiled=True)  10.2 us
    all_to_all x1, starting transfers between devices, body(): lax.all_to_all(behind.T, 'dp', split_axis=0, concat_axis=1, tiled=True)  9.55 us
    reduce_sum x2, other arithmetic, short_corr_rows(): jnp.sum(grad_wide * padded[start:start + row_count].astype(jnp.float32),...  8.68 us
    all_to_all x1, waiting for transfers between devices, body(): lax.all_to_all(behind.T, 'dp', split_axis=0, concat_axis=1, tiled=True)  7.76 us
    reshape x2, local copies, waits for them, and re-layouts, lag_grad(): skewed = padded.reshape(group_count, taps, 2 * taps + 1)[:, :, :taps]  6.02 us
  transfers between devices with their start and end apart: 5, of which 4 were waited for; matrix products, arithmetic and copies ran while one was open for 35% of the time, Pallas kernels for 0%

profile of v7, /device:TPU:6, one launch (start us, length us, event | category | flops | bytes accessed | tf_op | source)
XLA Modules:
  0.0 142.5 jit_solution(2260990801175637756)
XLA Ops:
  0.6 1.6 %copy.34 = bf16[1,128,4096]{1,2,0:T(8,128)(2,1)S(1)} copy(bf16[1,128,4096]{2,1,0:T(8,128)(2,1)} %param.5) | data formatting | bytes 2097152 | tf_op args[1]
  2.3 1.3 copy.35
  3.6 10.2 %all-to-all-start = ((bf16[128,32,128]{2,0,1:T(8,128)(2,1)}), bf16[128,32,128]{2,0,1:T(8,128)(2,1)S(1)}, u32[]{:S(2)}, u32[]{:S(2)}) async-start(bf16[128,32,128]{2,0,1:T(8,128)(2,1)} %copy.35), calls=%async_computation | async-start | bytes 2097152 | tf_op jit(solution)/shard_map/all_to_all | solution.py:143
  14.0 0.7 copy.36
  14.7 1.4 fusion.27
  16.2 1.1 broadcast_select_fusion
  17.3 25.5 %all-to-all-done = bf16[128,32,128]{2,0,1:T(8,128)(2,1)S(1)} async-done(((bf16[128,32,128]{2,0,1:T(8,128)(2,1)}), bf16[128,32,128]{2,0,1:T(8,128)(2,1)S(1)}, u32[]{:S(2)}, u32[]{:S(2)}) %all-to-all-start) | async-done | bytes 1048608 | tf_op jit(solution)/shard_map/all_to_all | solution.py:143
  42.8 0.5 copy.37
  43.3 1.3 copy.40
  44.6 5.0 %all-to-all-start.1 = ((bf16[128,32,128]{2,0,1:T(8,128)(2,1)}), bf16[128,32,128]{2,0,1:T(8,128)(2,1)}, u32[]{:S(2)}, u32[]{:S(2)}) async-start(bf16[128,32,128]{2,0,1:T(8,128)(2,1)} %copy.40), calls=%async_computation.1 | async-start | bytes 2097152 | tf_op jit(solution)/shard_map/all_to_all | solution.py:145
  49.7 0.2 copy.78
  50.3 0.6 copy-done.16
  50.9 0.3 fusion.46
  51.3 0.3 fusion.23
  51.6 0.2 copy.91
  51.8 1.5 %add_convert_fusion.4 = bf16[64,4096]{1,0:T(8,128)(2,1)S(1)} fusion(bf16[64,4096]{1,0:T(8,128)(2,1)S(1)} %bitcast.474, f32[64]{0:T(128)S(1)} %get-tuple-element.85, f32[64]{0:T(128)S(1)} %get-tuple-element.86, f32[64]{0:T(128)S(1)} %get-tuple-element.87, f32[64]{0:T(128)S(1)} %get-tuple-element.88, f32[64]{0:T(128)S(1)} %get-tuple-element.89, ...), kind=kLoop, calls=%fused_computation.80 | loop fusion | flops 6029312 | bytes 1574656 | tf_op jit(solution)/shard_map/convert_element_type | solution.py:162
  53.6 0.3 fusion.45
  53.9 0.3 fusion.24
  54.2 0.2 copy.90
  54.4 2.3 %add_convert_fusion.3 = bf16[64,4096]{1,0:T(8,128)(2,1)} fusion(bf16[64,4096]{1,0:T(8,128)(2,1)S(1)} %bitcast.489, bf16[64,4096]{1,0:T(8,128)(2,1)S(1)} %add_convert_fusion.4, f32[64]{0:T(128)S(1)} %get-tuple-element.78, f32[64]{0:T(128)S(1)} %get-tuple-element.79, f32[64]{0:T(128)S(1)} %get-tuple-element.80, f32[64]{0:T(128)S(1)} %get-tuple-element.81, ...), kind=kLoop, calls=%fused_computation.79 | loop fusion | flops 6029312 | bytes 1574656 | tf_op jit(solution)/shard_map/convert_element_type | solution.py:168
  57.0 11.4 %collective-permute-start = (bf16[64,4096]{1,0:T(8,128)(2,1)}, bf16[64,4096]{1,0:T(8,128)(2,1)}, u32[]{:S(2)}, u32[]{:S(2)}) collective-permute-start(bf16[64,4096]{1,0:T(8,128)(2,1)} %add_convert_fusion.3), channel_id=1, source_target_pairs={{32,0},{64,32},{96,64},{128,96},{160,128},{192,160},{224,192},{256... | collective-permute-start | bytes 1572872 | tf_op jit(solution)/shard_map/ppermute | solution.py:10
  68.4 0.3 fusion.44
  68.8 0.3 fusion.25
  69.3 1.5 %add_convert_fusion.2 = bf16[64,4096]{1,0:T(8,128)(2,1)S(1)} fusion(bf16[64,4096]{1,0:T(8,128)(2,1)S(1)} %bitcast.477, bf16[64,4096]{1,0:T(8,128)(2,1)S(1)} %get-tuple-element.12, f32[64]{0:T(128)S(1)} %get-tuple-element.71, f32[64]{0:T(128)S(1)} %get-tuple-element.72, f32[64]{0:T(128)S(1)} %get-tuple-element.73, f32[64]{0:T(128)S(1)} %get-tuple-element.74, ...), kind=kLoop, calls=%fused_computation.78 | loop fusion | flops 6029312 | bytes 1574656 | tf_op jit(solution)/shard_map/convert_element_type | solution.py:162
  71.2 0.2 copy.75
  71.4 0.3 fusion.43
  71.7 0.3 fusion.26
  72.3 2.3 %add_convert_fusion.1 = bf16[64,4096]{1,0:T(8,128)(2,1)} fusion(bf16[64,4096]{1,0:T(8,128)(2,1)S(1)} %bitcast.491, bf16[64,4096]{1,0:T(8,128)(2,1)S(1)} %add_convert_fusion.2, f32[64]{0:T(128)S(1)} %get-tuple-element.65, f32[64]{0:T(128)S(1)} %get-tuple-element.66, f32[64]{0:T(128)S(1)} %get-tuple-element.67, f32[64]{0:T(128)S(1)} %get-tuple-element.68, ...), kind=kLoop, calls=%fused_computation.77 | loop fusion | flops 6029312 | bytes 1574656 | tf_op jit(solution)/shard_map/convert_element_type | solution.py:168
  74.6 2.4 %collective-permute-start.1 = (bf16[64,4096]{1,0:T(8,128)(2,1)}, bf16[64,4096]{1,0:T(8,128)(2,1)}, u32[]{:S(2)}, u32[]{:S(2)}) collective-permute-start(bf16[64,4096]{1,0:T(8,128)(2,1)} %add_convert_fusion.1), channel_id=1, source_target_pairs={{32,0},{64,32},{96,64},{128,96},{160,128},{192,160},{224,192},{256... | collective-permute-start | bytes 1572872 | tf_op jit(solution)/shard_map/ppermute | solution.py:10
  77.0 1.6 %all-to-all-done.1 = bf16[128,32,128]{2,0,1:T(8,128)(2,1)} async-done(((bf16[128,32,128]{2,0,1:T(8,128)(2,1)}), bf16[128,32,128]{2,0,1:T(8,128)(2,1)}, u32[]{:S(2)}, u32[]{:S(2)}) %all-to-all-start.1) | async-done | bytes 1048608 | tf_op jit(solution)/shard_map/all_to_all | solution.py:145
  78.6 1.5 %copy.41 = bf16[4096,128]{0,1:T(8,128)(2,1)S(1)} copy(bf16[4096,128]{1,0:T(8,128)(2,1)} %bitcast.66) | data formatting | bytes 2097152 | tf_op jit(solution)/shard_map/optimization_barrier | solution.py:176
  80.2 1.0 copy-done.2
  81.1 2.5 %fusion.35 = bf16[16,8,32,128]{3,1,2,0:T(8,128)(2,1)S(1)} fusion(f32[128]{0:T(128)S(1)} %get-tuple-element.55, bf16[128,4096]{1,0:T(8,128)(2,1)S(1)} %bitcast.470, f32[128]{0:T(128)S(1)} %get-tuple-element.56, f32[128]{0:T(128)S(1)} %get-tuple-element.57, f32[128]{0:T(128)S(1)} %get-tuple-element.58, f32[128]{0:T(128)S(1)} %get-tuple-element.59, ...), kind=kLoop, calls=%fused_computation.81 | loop fusion | flops 11010048 | bytes 2100736
  83.7 0.2 copy.73
  83.9 0.4 fusion.42
  84.4 0.6 copy-done.15
  85.0 0.5 convolution_add_fusion
  85.4 0.7 copy-done.3
  86.8 5.9 %fusion.22 = (f32[128]{0:T(128)S(1)}, f32[128]{0:T(128)S(1)}, f32[128]{0:T(128)S(1)}, f32[128]{0:T(128)S(1)}, f32[128]{0:T(128)S(1)}, /*index=5*/f32[128]{0:T(12...) fusion(bf16[4096,128]{0,1:T(8,128)(2,1)S(1)} %copy-done.3, bf16[64,4096]{1,0:T(8,128)(2,1)S(1)} %bitcast.492, ...), kind=kLoop, calls=%fused_computation.40 | loop fusion | flops 18349056 | bytes 6295552 | tf_op jit(solution)/shard_map/reduce_sum | solution.py:130
  92.6 1.5 %convolution_bitcast_fusion.2 = f32[8,128,128]{1,2,0:T(8,128)} fusion(bf16[8,16,31,128]{3,2,1,0:T(8,128)(2,1)S(1)} %bitcast.458, bf16[8,16,32,128]{3,2,1,0:T(8,128)(2,1)S(1)} %bitcast.465), kind=kOutput, calls=%fused_computation.54 | convolution fusion | flops 134217728 | bytes 2588672 | tf_op jit(solution)/shard_map/gcbt,gcbs->gts/dot_general | solution.py:65
  94.1 2.4 %collective-permute-done.1 = bf16[64,4096]{1,0:T(8,128)(2,1)} collective-permute-done((bf16[64,4096]{1,0:T(8,128)(2,1)}, bf16[64,4096]{1,0:T(8,128)(2,1)}, u32[]{:S(2)}, u32[]{:S(2)}) %collective-permute-start.1) | collective-permute-done | bytes 524320 | tf_op jit(solution)/shard_map/ppermute | solution.py:10
  96.5 2.3 %maximum_bitcast_fusion = bf16[4096,128]{0,1:T(8,128)(2,1)} fusion(bf16[64,4096]{1,0:T(8,128)(2,1)} %collective-permute-done.1, bf16[64,4096]{1,0:T(8,128)(2,1)} %collective-permute-done), kind=kLoop, calls=%fused_computation.62 | loop fusion | flops 2097152 | bytes 2097152 | tf_op jit(solution)/shard_map/transpose | solution.py:184
  98.7 2.3 %copy.42 = bf16[4096,128]{1,0:T(8,128)(2,1)} copy(bf16[4096,128]{0,1:T(8,128)(2,1)} %maximum_bitcast_fusion) | data formatting | bytes 2097152 | tf_op jit(solution)/shard_map/transpose | solution.py:184
  101.0 9.5 %all-to-all-start.2 = ((bf16[32,128,128]{2,1,0:T(8,128)(2,1)}), bf16[32,128,128]{2,1,0:T(8,128)(2,1)}, u32[]{:S(2)}, u32[]{:S(2)}) async-start(bf16[32,128,128]{2,1,0:T(8,128)(2,1)} %bitcast.495), calls=%async_computation.2 | async-start | bytes 2097152 | tf_op jit(solution)/shard_map/all_to_all | solution.py:184
  110.6 1.7 %fusion.28 = f32[8,128,128]{1,2,0:T(8,128)S(1)} fusion(f32[8,128,128]{1,2,0:T(8,128)} %convolution_bitcast_fusion.2, pred[128,128]{0,1:T(8,128)(4,1)S(1)} %copy.46, bf16[8,16,32,128]{3,2,1,0:T(8,128)(2,1)S(1)} %bitcast.466, bf16[8,16,32,128]{3,2,1,0:T(8,128)(2,1)S(1)} %bitcast.459), kind=kOutput, calls=%fused_computation.56 | convolution fusion | flops 134348800 | bytes 3162112 | tf_op jit(solution)/shard_map/gcbt,gcbs->gts/dot_general | solution.py:62
  112.3 0.3 copy.47
  112.7 0.6 copy.76
  113.3 1.0 concatenate.99
  114.4 3.6 %reshape.552 = f32[8,128,257]{2,1,0:T(8,128)} reshape(f32[8,32896]{1,0:T(8,128)} %concatenate.99) | data formatting | bytes 2105344 | tf_op jit(solution)/shard_map/reshape | solution.py:73
  118.0 2.8 %fusion.15 = (f32[128]{0:T(128)S(1)}, f32[128]{0:T(128)S(1)}, f32[128]{0:T(128)S(1)}, f32[128]{0:T(128)S(1)}, f32[128]{0:T(128)S(1)}, /*index=5*/f32[128]{0:T(128)S(1)}) fusion(bf16[4096,128]{0,1:T(8,128)(2,1)S(1)} %bitcast.469, bf16[64,4096]{1,0:T(8,128)(2,1)S(1)} %bitcast.479, bf16[64,4096]{1,0:T(8,128)(2,1)S(1)} %bitcast.476), kind=kLoop, calls=%fused_computation.26 | loop fusion | flops 11533568 | bytes 2100224 | tf_op jit(solution)/shard_map/reduce_sum | solution.py:130
  120.9 0.6 copy.50
  121.5 2.5 %fusion.92 = bf16[16,8,32,128]{3,1,2,0:T(8,128)(2,1)S(1)} fusion(f32[128]{0:T(128)S(1)} %get-tuple-element.62, f32[128]{0:T(128)S(1)} %get-tuple-element.63, f32[128]{0:T(128)S(1)} %get-tuple-element.51, f32[128]{0:T(128)S(1)} %get-tuple-element.52, f32[128]{0:T(128)S(1)} %get-tuple-element.53, bf16[128,4096]{1,0:T(8,128)(2,1)S(1)} %copy-done.1, ...), kind=kLoop, calls=%fused_computation.220 | loop fusion | flops 11010048 | bytes 2100736
  124.0 0.2 copy.77
  124.3 0.6 convolution_bitcast_fusion
  125.0 0.5 fusion.29
  125.6 0.3 copy.48
  125.9 0.6 copy.79
  126.6 2.4 %reshape.556 = f32[8,128,257]{2,1,0:T(8,128)} reshape(f32[8,32896]{1,0:T(8,128)S(1)} %concatenate.102) | data formatting | bytes 2105344 | tf_op jit(solution)/shard_map/reshape | solution.py:73
  129.0 1.1 slice_reduce_fusion.1
  130.1 1.1 slice_reduce_fusion
  131.2 0.6 maximum_multiply_fusion.1
  131.8 7.8 %all-to-all-done.2 = bf16[32,128,128]{2,1,0:T(8,128)(2,1)} async-done(((bf16[32,128,128]{2,1,0:T(8,128)(2,1)}), bf16[32,128,128]{2,1,0:T(8,128)(2,1)}, u32[]{:S(2)}, u32[]{:S(2)}) %all-to-all-start.2) | async-done | bytes 1048608 | tf_op jit(solution)/shard_map/all_to_all | solution.py:184
  139.6 1.6 %copy.43 = bf16[32,128,128]{1,2,0:T(8,128)(2,1)S(1)} copy(bf16[32,128,128]{2,1,0:T(8,128)(2,1)} %all-to-all-done.2) | data formatting | bytes 2097152 | tf_op jit(solution)/shard_map/all_to_all | solution.py:184
  141.2 1.3 copy.49
  (61 shorter events, 3.0 us)
Async XLA Ops:
  0.6 14.1 %copy-start = (bf16[1,2,8,128]{3,2,1,0:T(8,128)(2,1)S(1)}, bf16[1,2,8,128]{3,2,1,0:T(8,128)(2,1)}, u32[]{:S(2)}) copy-start(bf16[1,2,8,128]{3,2,1,0:T(8,128)(2,1)} %param.7) | copy-start | bytes 12292
  2.3 11.7 %copy-start.18 = (bf16[1,128,4096]{2,1,0:T(8,128)(2,1)S(1)}, bf16[1,128,4096]{2,1,0:T(8,128)(2,1)}, u32[]{:S(2)}) copy-start(bf16[1,128,4096]{2,1,0:T(8,128)(2,1)} %param.4) | copy-start | bytes 3145732
  3.6 39.2 %all-to-all-start = ((bf16[128,32,128]{2,0,1:T(8,128)(2,1)}), bf16[128,32,128]{2,0,1:T(8,128)(2,1)S(1)}, u32[]{:S(2)}, u32[]{:S(2)}) async-start(bf16[128,32,128]{2,0,1:T(8,128)(2,1)} %copy.35), calls=%async_computation | async-start | bytes 2097152 | tf_op jit(solution)/shard_map/all_to_all | solution.py:143
  14.6 1.4 copy-start.19
  44.6 34.0 %all-to-all-start.1 = ((bf16[128,32,128]{2,0,1:T(8,128)(2,1)}), bf16[128,32,128]{2,0,1:T(8,128)(2,1)}, u32[]{:S(2)}, u32[]{:S(2)}) async-start(bf16[128,32,128]{2,0,1:T(8,128)(2,1)} %copy.40), calls=%async_computation.1 | async-start | bytes 2097152 | tf_op jit(solution)/shard_map/all_to_all | solution.py:145
  49.9 1.0 copy-start.16
  50.0 1.3 copy-start.14
  51.8 2.1 %copy-start.4 = (bf16[8,8,32,128]{3,1,2,0:T(8,128)(2,1)}, bf16[8,8,32,128]{3,1,2,0:T(8,128)(2,1)S(1)}, u32[]{:S(2)}) copy-start(bf16[8,8,32,128]{3,1,2,0:T(8,128)(2,1)S(1)} %copy.91) | copy-start | bytes 1572868
  54.4 14.3 %copy-start.10 = (bf16[8,8,32,128]{3,1,2,0:T(8,128)(2,1)}, bf16[8,8,32,128]{3,1,2,0:T(8,128)(2,1)S(1)}, u32[]{:S(2)}) copy-start(bf16[8,8,32,128]{3,1,2,0:T(8,128)(2,1)S(1)} %copy.90) | copy-start | bytes 1572868
  57.0 37.1 %collective-permute-start = (bf16[64,4096]{1,0:T(8,128)(2,1)}, bf16[64,4096]{1,0:T(8,128)(2,1)}, u32[]{:S(2)}, u32[]{:S(2)}) collective-permute-start(bf16[64,4096]{1,0:T(8,128)(2,1)} %add_convert_fusion.3), channel_id=1, source_target_pairs={{32,0},{64,32},{96,64},{128,96},{160,128},{192,160},{224,192},{256... | collective-permute-start | bytes 1572872 | tf_op jit(solution)/shard_map/ppermute | solution.py:10
  69.3 1.9 %copy-start.7 = (bf16[8,8,32,128]{3,1,2,0:T(8,128)(2,1)}, bf16[8,8,32,128]{3,1,2,0:T(8,128)(2,1)S(1)}, u32[]{:S(2)}) copy-start(bf16[8,8,32,128]{3,1,2,0:T(8,128)(2,1)S(1)} %copy.89) | copy-start | bytes 1572868
  72.3 6.4 %copy-start.12 = (bf16[8,8,32,128]{3,1,2,0:T(8,128)(2,1)}, bf16[8,8,32,128]{3,1,2,0:T(8,128)(2,1)S(1)}, u32[]{:S(2)}) copy-start(bf16[8,8,32,128]{3,1,2,0:T(8,128)(2,1)S(1)} %copy.88) | copy-start | bytes 1572868
  74.6 21.9 %collective-permute-start.1 = (bf16[64,4096]{1,0:T(8,128)(2,1)}, bf16[64,4096]{1,0:T(8,128)(2,1)}, u32[]{:S(2)}, u32[]{:S(2)}) collective-permute-start(bf16[64,4096]{1,0:T(8,128)(2,1)} %add_convert_fusion.1), channel_id=1, source_target_pairs={{32,0},{64,32},{96,64},{128,96},{160,128},{192,160},{224,192},{256... | collective-permute-start | bytes 1572872 | tf_op jit(solution)/shard_map/ppermute | solution.py:10
  80.1 1.0 copy-start.2
  81.1 2.8 %copy-start.17 = (bf16[2,8,128,128]{3,2,1,0:T(8,128)(2,1)S(1)}, bf16[2,8,128,128]{3,2,1,0:T(8,128)(2,1)}, u32[]{:S(2)}) copy-start(bf16[2,8,128,128]{3,2,1,0:T(8,128)(2,1)} %get-tuple-element.49) | copy-start | bytes 1572868
  83.9 1.0 copy-start.15
  85.0 1.2 copy-start.3
  85.0 1.4 copy-start.5
  85.0 1.5 %copy-start.8 = (bf16[8,8,32,128]{3,1,2,0:T(8,128)(2,1)S(1)}, bf16[8,8,32,128]{3,1,2,0:T(8,128)(2,1)}, u32[]{:S(2)}) copy-start(bf16[8,8,32,128]{3,1,2,0:T(8,128)(2,1)} %copy-done.7) | copy-start | bytes 1572868
  85.0 1.7 %copy-start.11 = (bf16[8,8,32,128]{3,1,2,0:T(8,128)(2,1)S(1)}, bf16[8,8,32,128]{3,1,2,0:T(8,128)(2,1)}, u32[]{:S(2)}) copy-start(bf16[8,8,32,128]{3,1,2,0:T(8,128)(2,1)} %copy-done.10) | copy-start | bytes 1572868
  85.0 1.8 %copy-start.13 = (bf16[8,8,32,128]{3,1,2,0:T(8,128)(2,1)S(1)}, bf16[8,8,32,128]{3,1,2,0:T(8,128)(2,1)}, u32[]{:S(2)}) copy-start(bf16[8,8,32,128]{3,1,2,0:T(8,128)(2,1)} %copy-done.12) | copy-start | bytes 1572868
  101.0 38.5 %all-to-all-start.2 = ((bf16[32,128,128]{2,1,0:T(8,128)(2,1)}), bf16[32,128,128]{2,1,0:T(8,128)(2,1)}, u32[]{:S(2)}, u32[]{:S(2)}) async-start(bf16[32,128,128]{2,1,0:T(8,128)(2,1)} %bitcast.495), calls=%async_computation.2 | async-start | bytes 2097152 | tf_op jit(solution)/shard_map/all_to_all | solution.py:184
  113.3 4.7 %copy-start.1 = (bf16[128,4096]{1,0:T(8,128)(2,1)S(1)}, bf16[128,4096]{1,0:T(8,128)(2,1)}, u32[]{:S(2)}) copy-start(bf16[128,4096]{1,0:T(8,128)(2,1)} %get-tuple-element.45) | copy-start | bytes 3145732
  113.3 4.7 %copy-start.6 = (bf16[8,8,32,128]{3,1,2,0:T(8,128)(2,1)S(1)}, bf16[8,8,32,128]{3,1,2,0:T(8,128)(2,1)}, u32[]{:S(2)}) copy-start(bf16[8,8,32,128]{3,1,2,0:T(8,128)(2,1)} %copy-done.4) | copy-start | bytes 1572868
  113.3 4.7 %copy-start.9 = (bf16[8,8,32,128]{3,1,2,0:T(8,128)(2,1)S(1)}, bf16[8,8,32,128]{3,1,2,0:T(8,128)(2,1)}, u32[]{:S(2)}) copy-start(bf16[8,8,32,128]{3,1,2,0:T(8,128)(2,1)} %copy-done.7) | copy-start | bytes 1572868

commit v8 on v6

--- a/solution.py
+++ b/solution.py
@@ -173,7 +173,9 @@
     middle_grad = jnp.concatenate(middle_grads)
     dmix_one = jnp.concatenate(dmix_ones)
     behinds.append(from_behind(input_grad_h, "pipe", -1))
-    input_rows, _ = lax.optimization_barrier((input_rows, input_grad_h))
+    input_rows, _, dmix_two_t, dmix_one_t, middle_grad = lax.optimization_barrier(
+        (input_rows, input_grad_h, dmix_two.T, dmix_one.T, middle_grad)
+    )
     behind = jnp.concatenate(behinds)
     own_rows = lax.all_to_all(behind.T, "dp", split_axis=0, concat_axis=1, tiled=True)
     passed_grad = own_rows[None]
@@ -183,9 +185,9 @@
     middle = (source.astype(jnp.float32) + long_one).astype(jnp.bfloat16)
     mixed_two = short_mix(middle, short_all[1]).astype(jnp.bfloat16)
     dlong_two = lag_grad(mixed_two, top_grad, group_count, taps)
-    dshort_two = short_corr_rows(dmix_two.T, middle.T, tap_count)
+    dshort_two = short_corr_rows(dmix_two_t, middle.T, tap_count)
     dlong_one = lag_grad(mixed_one, middle_grad, group_count, taps)
-    dshort_one = short_corr_rows(dmix_one.T, input_rows, tap_count)
+    dshort_one = short_corr_rows(dmix_one_t, input_rows, tap_count)
     factor = float(rows * devices) ** (-0.5)
     short_grad = jnp.stack([dshort_one, dshort_two])[None] * factor
     long_grad = jnp.stack([dlong_one, dlong_two])[None] * factor

time: 146 us -> 146 us (level)
  other arithmetic: 25.3 us -> 26.8 us
  waiting for transfers between devices: 44.7 us -> 43.2 us
    convert_element_type x0 -> x1, other arithmetic: none -> 1.87 us  [body(): middle = (source.astype(jnp.float32) + long_one).astype(jnp.bfloat16)]
    convert_element_type x2, other arithmetic: 4.56 us -> 2.92 us  [body(): input_grad_h = (middle_grad_h.astype(jnp.float32) + short_back(dmix_one_h...]
    unnamed x57 -> x37, local copies, waits for them, and re-layouts: 11.3 us -> 10.6 us
    unnamed x3 -> x2, other arithmetic: 5.44 us -> 5.11 us
  transfers between devices with their start and end apart: 5 -> 5, of which waited for: 3 -> 3; matrix products, arithmetic and copies ran while one was open for 34% -> 37% of each run, Pallas kernels for 0% -> 0%
where the time goes in v8:
time: 146 us; the launch traced here: 145 us
  waiting for transfers between devices  43.2 us (30%)
  starting transfers between devices  38.8 us (27%)
  local copies, waits for them, and re-layouts  27.1 us (19%)
  other arithmetic  26.8 us (18%)
  matrix products  8.11 us (6%)
    all_to_all x1, waiting for transfers between devices, body(): lax.all_to_all(out_grad[0], 'dp', split_axis=1, concat_axis=0, tiled=True)  25.5 us
    ppermute x2, waiting for transfers between devices, from_behind(): return lax.ppermute(shard, axis, pairs)  17.7 us
    ppermute x2, starting transfers between devices, from_behind(): return lax.ppermute(shard, axis, pairs)  13.9 us
    unnamed x37, local copies, waits for them, and re-layouts  10.6 us
    all_to_all x1, starting transfers between devices, body(): lax.all_to_all(out_grad[0], 'dp', split_axis=1, concat_axis=0, tiled=True)  10.2 us
    all_to_all x1, starting transfers between devices, body(): lax.all_to_all(behind.T, 'dp', split_axis=0, concat_axis=1, tiled=True)  9.71 us
    reduce_sum x2, other arithmetic, short_corr_rows(): jnp.sum(grad_wide * padded[start:start + row_count].astype(jnp.float32),...  7.26 us
    unnamed x2, other arithmetic  5.11 us
  transfers between devices with their start and end apart: 5, of which 3 were waited for; matrix products, arithmetic and copies ran while one was open for 37% of the time, Pallas kernels for 0%

profile of v8, /device:TPU:6, one launch (start us, length us, event | category | flops | bytes accessed | tf_op | source)
XLA Modules:
  0.0 145.2 jit_solution(3795859821888832447)
XLA Ops:
  0.6 1.6 %copy.34 = bf16[1,128,4096]{1,2,0:T(8,128)(2,1)S(1)} copy(bf16[1,128,4096]{2,1,0:T(8,128)(2,1)} %param.5) | data formatting | bytes 2097152 | tf_op args[1]
  2.3 1.3 copy.35
  3.6 10.2 %all-to-all-start = ((bf16[128,32,128]{2,0,1:T(8,128)(2,1)}), bf16[128,32,128]{2,0,1:T(8,128)(2,1)S(1)}, u32[]{:S(2)}, u32[]{:S(2)}) async-start(bf16[128,32,128]{2,0,1:T(8,128)(2,1)} %copy.35), calls=%async_computation | async-start | bytes 2097152 | tf_op jit(solution)/shard_map/all_to_all | solution.py:143
  14.0 0.7 copy.36
  14.7 1.4 fusion.27
  16.2 1.1 broadcast_select_fusion
  17.3 25.5 %all-to-all-done = bf16[128,32,128]{2,0,1:T(8,128)(2,1)S(1)} async-done(((bf16[128,32,128]{2,0,1:T(8,128)(2,1)}), bf16[128,32,128]{2,0,1:T(8,128)(2,1)S(1)}, u32[]{:S(2)}, u32[]{:S(2)}) %all-to-all-start) | async-done | bytes 1048608 | tf_op jit(solution)/shard_map/all_to_all | solution.py:143
  42.8 0.5 copy.37
  43.3 1.3 copy.42
  44.6 5.0 %all-to-all-start.2 = ((bf16[128,32,128]{2,0,1:T(8,128)(2,1)}), bf16[128,32,128]{2,0,1:T(8,128)(2,1)S(1)}, u32[]{:S(2)}, u32[]{:S(2)}) async-start(bf16[128,32,128]{2,0,1:T(8,128)(2,1)} %copy.42), calls=%async_computation.2 | async-start | bytes 2097152 | tf_op jit(solution)/shard_map/all_to_all | solution.py:145
  50.0 0.7 copy-done.6
  50.7 0.3 fusion.47
  51.0 0.3 fusion.23
  51.3 0.2 copy.90
  51.5 1.5 %add_convert_fusion.4 = bf16[64,4096]{1,0:T(8,128)(2,1)S(1)} fusion(bf16[64,4096]{1,0:T(8,128)(2,1)S(1)} %bitcast.440, f32[64]{0:T(128)S(1)} %get-tuple-element.84, f32[64]{0:T(128)S(1)} %get-tuple-element.85, f32[64]{0:T(128)S(1)} %get-tuple-element.86, f32[64]{0:T(128)S(1)} %get-tuple-element.87, f32[64]{0:T(128)S(1)} %get-tuple-element.88, ...), kind=kLoop, calls=%fused_computation.80 | loop fusion | flops 6029312 | bytes 1574656 | tf_op jit(solution)/shard_map/convert_element_type | solution.py:162
  53.3 0.3 fusion.46
  53.6 0.3 fusion.24
  53.9 0.2 copy.89
  54.1 1.5 %add_convert_fusion.3 = bf16[64,4096]{1,0:T(8,128)(2,1)S(1)} fusion(bf16[64,4096]{1,0:T(8,128)(2,1)S(1)} %bitcast.442, bf16[64,4096]{1,0:T(8,128)(2,1)S(1)} %add_convert_fusion.4, f32[64]{0:T(128)S(1)} %get-tuple-element.77, f32[64]{0:T(128)S(1)} %get-tuple-element.78, f32[64]{0:T(128)S(1)} %get-tuple-element.79, f32[64]{0:T(128)S(1)} %get-tuple-element.80, ...), kind=kLoop, calls=%fused_computation.79 | loop fusion | flops 6029312 | bytes 1574656 | tf_op jit(solution)/shard_map/convert_element_type | solution.py:168
  55.9 11.4 %collective-permute-start = (bf16[64,4096]{1,0:T(8,128)(2,1)S(1)}, bf16[64,4096]{1,0:T(8,128)(2,1)S(1)}, u32[]{:S(2)}, u32[]{:S(2)}) collective-permute-start(bf16[64,4096]{1,0:T(8,128)(2,1)S(1)} %add_convert_fusion.3), channel_id=1, source_target_pairs={{32,0},{64,32},{96,64},{128,96},{160,128},{192,160},{224,192},{256... | collective-permute-start | bytes 1572872 | tf_op jit(solution)/shard_map/ppermute | solution.py:10
  67.3 0.3 fusion.45
  67.6 0.3 fusion.25
  67.9 0.2 copy.88
  68.1 1.5 %add_convert_fusion.2 = bf16[64,4096]{1,0:T(8,128)(2,1)S(1)} fusion(bf16[64,4096]{1,0:T(8,128)(2,1)S(1)} %bitcast.444, bf16[64,4096]{1,0:T(8,128)(2,1)S(1)} %get-tuple-element.13, f32[64]{0:T(128)S(1)} %get-tuple-element.70, f32[64]{0:T(128)S(1)} %get-tuple-element.71, f32[64]{0:T(128)S(1)} %get-tuple-element.72, f32[64]{0:T(128)S(1)} %get-tuple-element.73, ...), kind=kLoop, calls=%fused_computation.78 | loop fusion | flops 6029312 | bytes 1574656 | tf_op jit(solution)/shard_map/convert_element_type | solution.py:162
  69.9 0.3 fusion.44
  70.2 0.3 fusion.26
  70.5 0.2 copy.87
  70.7 1.5 %add_convert_fusion.1 = bf16[64,4096]{1,0:T(8,128)(2,1)S(1)} fusion(bf16[64,4096]{1,0:T(8,128)(2,1)S(1)} %bitcast.446, bf16[64,4096]{1,0:T(8,128)(2,1)S(1)} %add_convert_fusion.2, f32[64]{0:T(128)S(1)} %get-tuple-element.64, f32[64]{0:T(128)S(1)} %get-tuple-element.65, f32[64]{0:T(128)S(1)} %get-tuple-element.66, f32[64]{0:T(128)S(1)} %get-tuple-element.67, ...), kind=kLoop, calls=%fused_computation.77 | loop fusion | flops 6029312 | bytes 1574656 | tf_op jit(solution)/shard_map/convert_element_type | solution.py:168
  72.2 2.5 %collective-permute-start.1 = (bf16[64,4096]{1,0:T(8,128)(2,1)S(1)}, bf16[64,4096]{1,0:T(8,128)(2,1)S(1)}, u32[]{:S(2)}, u32[]{:S(2)}) collective-permute-start(bf16[64,4096]{1,0:T(8,128)(2,1)S(1)} %add_convert_fusion.1), channel_id=1, source_target_pairs={{32,0},{64,32},{96,64},{128,96},{160,128},{192,160},{224,192},{256... | collective-permute-start | bytes 1572872 | tf_op jit(solution)/shard_map/ppermute | solution.py:10
  74.6 1.1 pad_maximum_fusion
  75.7 0.2 copy.78
  75.9 1.4 maximum_bitcast_fusion.1
  77.4 7.3 %collective-permute-done = bf16[64,4096]{1,0:T(8,128)(2,1)S(1)} collective-permute-done((bf16[64,4096]{1,0:T(8,128)(2,1)S(1)}, bf16[64,4096]{1,0:T(8,128)(2,1)S(1)}, u32[]{:S(2)}, u32[]{:S(2)}) %collective-permute-start) | collective-permute-done | bytes 524320 | tf_op jit(solution)/shard_map/ppermute | solution.py:10
  84.6 10.4 %collective-permute-done.1 = bf16[64,4096]{1,0:T(8,128)(2,1)S(1)} collective-permute-done((bf16[64,4096]{1,0:T(8,128)(2,1)S(1)}, bf16[64,4096]{1,0:T(8,128)(2,1)S(1)}, u32[]{:S(2)}, u32[]{:S(2)}) %collective-permute-start.1) | collective-permute-done | bytes 524320 | tf_op jit(solution)/shard_map/ppermute | solution.py:10
  95.2 1.3 copy.40
  96.5 9.7 %all-to-all-start.1 = ((bf16[32,128,128]{2,1,0:T(8,128)(2,1)}), bf16[32,128,128]{2,1,0:T(8,128)(2,1)}, u32[]{:S(2)}, u32[]{:S(2)}) async-start(bf16[32,128,128]{2,1,0:T(8,128)(2,1)} %bitcast.64), calls=%async_computation.1 | async-start | bytes 2097152 | tf_op jit(solution)/shard_map/all_to_all | solution.py:180
  106.2 0.5 copy.43
  106.8 2.6 %fusion.36 = bf16[16,8,32,128]{3,1,2,0:T(8,128)(2,1)S(1)} fusion(f32[128]{0:T(128)S(1)} %get-tuple-element.54, bf16[128,4096]{1,0:T(8,128)(2,1)S(1)} %bitcast.417, f32[128]{0:T(128)S(1)} %get-tuple-element.55, f32[128]{0:T(128)S(1)} %get-tuple-element.56, f32[128]{0:T(128)S(1)} %get-tuple-element.57, f32[128]{0:T(128)S(1)} %get-tuple-element.58, ...), kind=kLoop, calls=%fused_computation.82 | loop fusion | flops 11010048 | bytes 2100736
  109.3 0.2 copy.73
  109.6 0.2 copy.75
  109.8 0.7 convolution_bitcast_fusion.2
  110.5 0.5 fusion.28
  111.0 1.1 pad_maximum_fusion.1
  112.1 2.6 %copy.47 = f32[8,128,256]{2,1,0:T(8,128)} copy(f32[8,128,256]{1,2,0:T(8,128)} %pad_maximum_fusion.1) | data formatting | bytes 2097152 | tf_op jit(solution)/shard_map/concatenate | solution.py:71
  114.7 1.8 %copy.76 = f32[1,8,128,256]{3,1,2,0:T(8,128)S(1)} copy(f32[1,8,128,256]{3,2,1,0:T(8,128)} %bitcast.454) | data formatting | bytes 2097152
  116.5 1.1 concatenate.98
  117.6 3.6 %reshape.552 = f32[8,128,257]{2,1,0:T(8,128)} reshape(f32[8,32896]{1,0:T(8,128)} %concatenate.98) | data formatting | bytes 2105344 | tf_op jit(solution)/shard_map/reshape | solution.py:73
  121.2 1.5 %fusion.43 = f32[8,16,32,128]{3,2,1,0:T(8,128)S(1)} fusion(bf16[2,8,128,128]{3,2,1,0:T(8,128)(2,1)} %get-tuple-element.48, bf16[8,16,32,128]{3,2,1,0:T(8,128)(2,1)S(1)} %bitcast.415), kind=kOutput, calls=%fused_computation.116 | convolution fusion | flops 134217728 | bytes 3407872 | tf_op jit(solution)/shard_map/gcbt,gts->gcbs/dot_general | solution.py:38
  122.7 0.5 convolution_add_fusion
  123.2 1.9 %fusion.8 = bf16[128,4096]{1,0:T(8,128)(2,1)S(1)} fusion(f32[16,8,32,128]{3,2,1,0:T(8,128)S(1)} %bitcast.428, bf16[4096,128]{0,1:T(8,128)(2,1)S(1)} %copy.43), kind=kLoop, calls=%fused_computation.26 | loop fusion | flops 1572864 | bytes 4194304 | tf_op jit(solution)/shard_map/convert_element_type | solution.py:185
  125.1 2.6 %fusion.35 = bf16[16,8,32,128]{3,1,2,0:T(8,128)(2,1)S(1)} fusion(f32[128]{0:T(128)S(1)} %get-tuple-element.61, bf16[128,4096]{1,0:T(8,128)(2,1)S(1)} %fusion.8, f32[128]{0:T(128)S(1)} %get-tuple-element.62, f32[128]{0:T(128)S(1)} %get-tuple-element.50, f32[128]{0:T(128)S(1)} %get-tuple-element.51, f32[128]{0:T(128)S(1)} %get-tuple-element.52, ...), kind=kLoop, calls=%fused_computation.81 | loop fusion | flops 11010048 | bytes 2100736
  127.7 1.3 copy.77
  128.9 3.0 %fusion.15 = (f32[128]{0:T(128)S(1)}, f32[128]{0:T(128)S(1)}, f32[128]{0:T(128)S(1)}, f32[128]{0:T(128)S(1)}, f32[128]{0:T(128)S(1)}, /*index=5*/f32[128]{0:T(128)S(1)}, f32[128]{0:T(128)S(1)}) fusion(bf16[4096,128]{0,1:T(8,128)(2,1)S(1)} %copy-done.3, bf16[4096,128]{0,1:T(8,128)(2,1)S(1)} %copy.43), kind=kLoop, calls=%fused_computation.33 | loop fusion | flops 11533440 | bytes 2100736 | tf_op jit(solution)/shard_map/reduce_sum | solution.py:130
  131.9 4.3 %fusion.22 = (f32[128]{0:T(128)S(1)}, f32[128]{0:T(128)S(1)}, f32[128]{0:T(128)S(1)}, f32[128]{0:T(128)S(1)}, f32[128]{0:T(128)S(1)}, /*index=5*/f32[128]{0:T(128)S(1)}, f32[128]{0:T(128)S(1)}) fusion(bf16[4096,128]{0,1:T(8,128)(2,1)} %get-tuple-element.17, bf16[4096,128]{0,1:T(8,128)(2,1)S(1)} %bitcast.418, bf16[128,4096]{1,0:T(8,128)(2,1)S(1)} %fusion.8), kind=kLoop, calls=%fused_computation.40 | loop fusion | flops 11533440 | bytes 3149312 | tf_op jit(solution)/shard_map/reduce_sum | solution.py:130
  136.3 0.6 copy.50
  136.9 0.7 convolution_bitcast_fusion
  137.5 0.5 fusion.29
  138.2 0.3 copy.48
  138.5 0.6 copy.79
  139.2 1.3 reshape.556
  140.5 1.1 slice_reduce_fusion.1
  141.6 0.6 maximum_multiply_fusion.1
  142.2 1.6 %copy.41 = bf16[32,128,128]{1,2,0:T(8,128)(2,1)S(1)} copy(bf16[32,128,128]{2,1,0:T(8,128)(2,1)} %all-to-all-done.1) | data formatting | bytes 2097152 | tf_op jit(solution)/shard_map/all_to_all | solution.py:180
  143.9 1.3 copy.49
  (41 shorter events, 1.8 us)
Async XLA Ops:
  0.6 14.1 %copy-start = (bf16[1,2,8,128]{3,2,1,0:T(8,128)(2,1)S(1)}, bf16[1,2,8,128]{3,2,1,0:T(8,128)(2,1)}, u32[]{:S(2)}) copy-start(bf16[1,2,8,128]{3,2,1,0:T(8,128)(2,1)} %param.7) | copy-start | bytes 12292
  2.3 11.7 %copy-start.7 = (bf16[1,128,4096]{2,1,0:T(8,128)(2,1)S(1)}, bf16[1,128,4096]{2,1,0:T(8,128)(2,1)}, u32[]{:S(2)}) copy-start(bf16[1,128,4096]{2,1,0:T(8,128)(2,1)} %param.4) | copy-start | bytes 3145732
  3.6 39.2 %all-to-all-start = ((bf16[128,32,128]{2,0,1:T(8,128)(2,1)}), bf16[128,32,128]{2,0,1:T(8,128)(2,1)S(1)}, u32[]{:S(2)}, u32[]{:S(2)}) async-start(bf16[128,32,128]{2,0,1:T(8,128)(2,1)} %copy.35), calls=%async_computation | async-start | bytes 2097152 | tf_op jit(solution)/shard_map/all_to_all | solution.py:143
  14.6 1.4 copy-start.8
  44.6 51.9 %all-to-all-start.2 = ((bf16[128,32,128]{2,0,1:T(8,128)(2,1)}), bf16[128,32,128]{2,0,1:T(8,128)(2,1)S(1)}, u32[]{:S(2)}, u32[]{:S(2)}) async-start(bf16[128,32,128]{2,0,1:T(8,128)(2,1)} %copy.42), calls=%async_computation.2 | async-start | bytes 2097152 | tf_op jit(solution)/shard_map/all_to_all | solution.py:145
  49.6 1.0 copy-start.6
  49.7 1.3 copy-start.4
  55.9 28.8 %collective-permute-start = (bf16[64,4096]{1,0:T(8,128)(2,1)S(1)}, bf16[64,4096]{1,0:T(8,128)(2,1)S(1)}, u32[]{:S(2)}, u32[]{:S(2)}) collective-permute-start(bf16[64,4096]{1,0:T(8,128)(2,1)S(1)} %add_convert_fusion.3), channel_id=1, source_target_pairs={{32,0},{64,32},{96,64},{128,96},{160,128},{192,160},{224,192},{256... | collective-permute-start | bytes 1572872 | tf_op jit(solution)/shard_map/ppermute | solution.py:10
  72.2 22.9 %collective-permute-start.1 = (bf16[64,4096]{1,0:T(8,128)(2,1)S(1)}, bf16[64,4096]{1,0:T(8,128)(2,1)S(1)}, u32[]{:S(2)}, u32[]{:S(2)}) collective-permute-start(bf16[64,4096]{1,0:T(8,128)(2,1)S(1)} %add_convert_fusion.1), channel_id=1, source_target_pairs={{32,0},{64,32},{96,64},{128,96},{160,128},{192,160},{224,192},{256... | collective-permute-start | bytes 1572872 | tf_op jit(solution)/shard_map/ppermute | solution.py:10
  96.5 45.8 %all-to-all-start.1 = ((bf16[32,128,128]{2,1,0:T(8,128)(2,1)}), bf16[32,128,128]{2,1,0:T(8,128)(2,1)}, u32[]{:S(2)}, u32[]{:S(2)}) async-start(bf16[32,128,128]{2,1,0:T(8,128)(2,1)} %bitcast.64), calls=%async_computation.1 | async-start | bytes 2097152 | tf_op jit(solution)/shard_map/all_to_all | solution.py:180
  106.7 2.8 %copy-start.2 = (bf16[128,4096]{1,0:T(8,128)(2,1)S(1)}, bf16[128,4096]{1,0:T(8,128)(2,1)}, u32[]{:S(2)}) copy-start(bf16[128,4096]{1,0:T(8,128)(2,1)} %pad_maximum_fusion) | copy-start | bytes 3145732
  121.2 1.5 %copy-start.5 = (bf16[2,8,128,128]{3,2,1,0:T(8,128)(2,1)S(1)}, bf16[2,8,128,128]{3,2,1,0:T(8,128)(2,1)}, u32[]{:S(2)}) copy-start(bf16[2,8,128,128]{3,2,1,0:T(8,128)(2,1)} %get-tuple-element.47) | copy-start | bytes 1572868
  125.1 3.8 %copy-start.3 = (bf16[4096,128]{0,1:T(8,128)(2,1)S(1)}, bf16[4096,128]{0,1:T(8,128)(2,1)}, u32[]{:S(2)}) copy-start(bf16[4096,128]{0,1:T(8,128)(2,1)} %get-tuple-element.15) | copy-start | bytes 3145732
  131.9 5.0 %copy-start.1 = (bf16[16,8,32,128]{3,2,1,0:T(8,128)(2,1)S(1)}, bf16[16,8,32,128]{3,2,1,0:T(8,128)(2,1)}, u32[]{:S(2)}) copy-start(bf16[16,8,32,128]{3,2,1,0:T(8,128)(2,1)} %copy.77) | copy-start | bytes 3145732

commit v9 on v7

--- a/solution.py
+++ b/solution.py
@@ -179,7 +179,7 @@
     long_one = causal_long(mixed_one, circ_now[0], circ_past[0])
     middle = (source.astype(jnp.float32) + long_one).astype(jnp.bfloat16)
     mixed_two = short_mix(middle, short_all[1]).astype(jnp.bfloat16)
-    behinds = list(lax.optimization_barrier((*behinds, mixed_two))[:-1])
+    behinds = list(lax.optimization_barrier((*behinds, middle))[:-1])
     behind = jnp.concatenate(behinds)
     own_rows = lax.all_to_all(behind.T, "dp", split_axis=0, concat_axis=1, tiled=True)
     passed_grad = own_rows[None]

time: 143 us -> 143 us (level)
  no operation moved by 1% of the time
where the time goes in v9:
time: 143 us; the launch traced here: 142 us
  starting transfers between devices  38.6 us (27%)
  waiting for transfers between devices  37.8 us (26%)
  local copies, waits for them, and re-layouts  27.9 us (20%)
  other arithmetic  27.8 us (19%)
  matrix products  9 us (6%)
    all_to_all x1, waiting for transfers between devices, body(): lax.all_to_all(out_grad[0], 'dp', split_axis=1, concat_axis=0, tiled=True)  25.4 us
    ppermute x2, starting transfers between devices, from_behind(): return lax.ppermute(shard, axis, pairs)  13.8 us
    unnamed x59, local copies, waits for them, and re-layouts  10.7 us
    all_to_all x1, starting transfers between devices, body(): lax.all_to_all(out_grad[0], 'dp', split_axis=1, concat_axis=0, tiled=True)  10.2 us
    all_to_all x1, starting transfers between devices, body(): lax.all_to_all(behind.T, 'dp', split_axis=0, concat_axis=1, tiled=True)  9.54 us
    reduce_sum x2, other arithmetic, short_corr_rows(): jnp.sum(grad_wide * padded[start:start + row_count].astype(jnp.float32),...  8.68 us
    all_to_all x1, waiting for transfers between devices, body(): lax.all_to_all(behind.T, 'dp', split_axis=0, concat_axis=1, tiled=True)  7.76 us
    reshape x2, local copies, waits for them, and re-layouts, lag_grad(): skewed = padded.reshape(group_count, taps, 2 * taps + 1)[:, :, :taps]  6.02 us
  transfers between devices with their start and end apart: 5, of which 4 were waited for; matrix products, arithmetic and copies ran while one was open for 35% of the time, Pallas kernels for 0%

profile of v9, /device:TPU:6, one launch (start us, length us, event | category | flops | bytes accessed | tf_op | source)
XLA Modules:
  0.0 142.5 jit_solution(11319698725676027345)
XLA Ops:
  0.6 1.6 %copy.34 = bf16[1,128,4096]{1,2,0:T(8,128)(2,1)S(1)} copy(bf16[1,128,4096]{2,1,0:T(8,128)(2,1)} %param.5) | data formatting | bytes 2097152 | tf_op args[1]
  2.3 1.3 copy.35
  3.6 10.2 %all-to-all-start = ((bf16[128,32,128]{2,0,1:T(8,128)(2,1)}), bf16[128,32,128]{2,0,1:T(8,128)(2,1)S(1)}, u32[]{:S(2)}, u32[]{:S(2)}) async-start(bf16[128,32,128]{2,0,1:T(8,128)(2,1)} %copy.35), calls=%async_computation | async-start | bytes 2097152 | tf_op jit(solution)/shard_map/all_to_all | solution.py:143
  14.0 0.7 copy.36
  14.7 1.4 fusion.27
  16.2 1.1 broadcast_select_fusion
  17.3 25.4 %all-to-all-done = bf16[128,32,128]{2,0,1:T(8,128)(2,1)S(1)} async-done(((bf16[128,32,128]{2,0,1:T(8,128)(2,1)}), bf16[128,32,128]{2,0,1:T(8,128)(2,1)S(1)}, u32[]{:S(2)}, u32[]{:S(2)}) %all-to-all-start) | async-done | bytes 1048608 | tf_op jit(solution)/shard_map/all_to_all | solution.py:143
  42.8 0.5 copy.37
  43.3 1.3 copy.40
  44.6 5.0 %all-to-all-start.1 = ((bf16[128,32,128]{2,0,1:T(8,128)(2,1)}), bf16[128,32,128]{2,0,1:T(8,128)(2,1)}, u32[]{:S(2)}, u32[]{:S(2)}) async-start(bf16[128,32,128]{2,0,1:T(8,128)(2,1)} %copy.40), calls=%async_computation.1 | async-start | bytes 2097152 | tf_op jit(solution)/shard_map/all_to_all | solution.py:145
  49.7 0.2 copy.78
  50.3 0.6 copy-done.16
  50.9 0.3 fusion.47
  51.3 0.3 fusion.23
  51.6 0.2 copy.91
  51.8 1.5 %add_convert_fusion.4 = bf16[64,4096]{1,0:T(8,128)(2,1)S(1)} fusion(bf16[64,4096]{1,0:T(8,128)(2,1)S(1)} %bitcast.474, f32[64]{0:T(128)S(1)} %get-tuple-element.85, f32[64]{0:T(128)S(1)} %get-tuple-element.86, f32[64]{0:T(128)S(1)} %get-tuple-element.87, f32[64]{0:T(128)S(1)} %get-tuple-element.88, f32[64]{0:T(128)S(1)} %get-tuple-element.89, ...), kind=kLoop, calls=%fused_computation.80 | loop fusion | flops 6029312 | bytes 1574656 | tf_op jit(solution)/shard_map/convert_element_type | solution.py:162
  53.6 0.3 fusion.46
  53.9 0.3 fusion.24
  54.2 0.2 copy.90
  54.4 2.3 %add_convert_fusion.3 = bf16[64,4096]{1,0:T(8,128)(2,1)} fusion(bf16[64,4096]{1,0:T(8,128)(2,1)S(1)} %bitcast.489, bf16[64,4096]{1,0:T(8,128)(2,1)S(1)} %add_convert_fusion.4, f32[64]{0:T(128)S(1)} %get-tuple-element.78, f32[64]{0:T(128)S(1)} %get-tuple-element.79, f32[64]{0:T(128)S(1)} %get-tuple-element.80, f32[64]{0:T(128)S(1)} %get-tuple-element.81, ...), kind=kLoop, calls=%fused_computation.79 | loop fusion | flops 6029312 | bytes 1574656 | tf_op jit(solution)/shard_map/convert_element_type | solution.py:168
  57.0 11.4 %collective-permute-start = (bf16[64,4096]{1,0:T(8,128)(2,1)}, bf16[64,4096]{1,0:T(8,128)(2,1)}, u32[]{:S(2)}, u32[]{:S(2)}) collective-permute-start(bf16[64,4096]{1,0:T(8,128)(2,1)} %add_convert_fusion.3), channel_id=1, source_target_pairs={{32,0},{64,32},{96,64},{128,96},{160,128},{192,160},{224,192},{256... | collective-permute-start | bytes 1572872 | tf_op jit(solution)/shard_map/ppermute | solution.py:10
  68.4 0.3 fusion.45
  68.7 0.3 fusion.25
  69.3 1.5 %add_convert_fusion.2 = bf16[64,4096]{1,0:T(8,128)(2,1)S(1)} fusion(bf16[64,4096]{1,0:T(8,128)(2,1)S(1)} %bitcast.477, bf16[64,4096]{1,0:T(8,128)(2,1)S(1)} %get-tuple-element.12, f32[64]{0:T(128)S(1)} %get-tuple-element.71, f32[64]{0:T(128)S(1)} %get-tuple-element.72, f32[64]{0:T(128)S(1)} %get-tuple-element.73, f32[64]{0:T(128)S(1)} %get-tuple-element.74, ...), kind=kLoop, calls=%fused_computation.78 | loop fusion | flops 6029312 | bytes 1574656 | tf_op jit(solution)/shard_map/convert_element_type | solution.py:162
  71.1 0.2 copy.75
  71.4 0.3 fusion.44
  71.7 0.3 fusion.26
  72.0 0.2 copy.88
  72.2 2.3 %add_convert_fusion.1 = bf16[64,4096]{1,0:T(8,128)(2,1)} fusion(bf16[64,4096]{1,0:T(8,128)(2,1)S(1)} %bitcast.491, bf16[64,4096]{1,0:T(8,128)(2,1)S(1)} %add_convert_fusion.2, f32[64]{0:T(128)S(1)} %get-tuple-element.65, f32[64]{0:T(128)S(1)} %get-tuple-element.66, f32[64]{0:T(128)S(1)} %get-tuple-element.67, f32[64]{0:T(128)S(1)} %get-tuple-element.68, ...), kind=kLoop, calls=%fused_computation.77 | loop fusion | flops 6029312 | bytes 1574656 | tf_op jit(solution)/shard_map/convert_element_type | solution.py:168
  74.5 2.4 %collective-permute-start.1 = (bf16[64,4096]{1,0:T(8,128)(2,1)}, bf16[64,4096]{1,0:T(8,128)(2,1)}, u32[]{:S(2)}, u32[]{:S(2)}) collective-permute-start(bf16[64,4096]{1,0:T(8,128)(2,1)} %add_convert_fusion.1), channel_id=1, source_target_pairs={{32,0},{64,32},{96,64},{128,96},{160,128},{192,160},{224,192},{256... | collective-permute-start | bytes 1572872 | tf_op jit(solution)/shard_map/ppermute | solution.py:10
  77.0 1.7 %all-to-all-done.1 = bf16[128,32,128]{2,0,1:T(8,128)(2,1)} async-done(((bf16[128,32,128]{2,0,1:T(8,128)(2,1)}), bf16[128,32,128]{2,0,1:T(8,128)(2,1)}, u32[]{:S(2)}, u32[]{:S(2)}) %all-to-all-start.1) | async-done | bytes 1048608 | tf_op jit(solution)/shard_map/all_to_all | solution.py:145
  78.6 1.5 %copy.41 = bf16[4096,128]{0,1:T(8,128)(2,1)S(1)} copy(bf16[4096,128]{1,0:T(8,128)(2,1)} %bitcast.65) | data formatting | bytes 2097152 | tf_op jit(solution)/shard_map/optimization_barrier | solution.py:176
  80.2 1.0 copy-done.2
  81.1 2.5 %fusion.36 = bf16[16,8,32,128]{3,1,2,0:T(8,128)(2,1)S(1)} fusion(f32[128]{0:T(128)S(1)} %get-tuple-element.55, bf16[128,4096]{1,0:T(8,128)(2,1)S(1)} %bitcast.470, f32[128]{0:T(128)S(1)} %get-tuple-element.56, f32[128]{0:T(128)S(1)} %get-tuple-element.57, f32[128]{0:T(128)S(1)} %get-tuple-element.58, f32[128]{0:T(128)S(1)} %get-tuple-element.59, ...), kind=kLoop, calls=%fused_computation.82 | loop fusion | flops 11010048 | bytes 2100736
  83.7 0.2 copy.73
  83.9 0.4 fusion.43
  84.4 1.5 %convolution_bitcast_fusion.2 = f32[8,128,128]{1,2,0:T(8,128)} fusion(bf16[8,16,31,128]{3,2,1,0:T(8,128)(2,1)S(1)} %bitcast.457, bf16[8,16,32,128]{3,2,1,0:T(8,128)(2,1)S(1)} %bitcast.465), kind=kOutput, calls=%fused_computation.54 | convolution fusion | flops 134217728 | bytes 2588672 | tf_op jit(solution)/shard_map/gcbt,gcbs->gts/dot_general | solution.py:65
  85.9 0.5 convolution_add_fusion
  86.4 0.7 copy-done.3
  87.7 5.9 %fusion.22 = (f32[128]{0:T(128)S(1)}, f32[128]{0:T(128)S(1)}, f32[128]{0:T(128)S(1)}, f32[128]{0:T(128)S(1)}, f32[128]{0:T(128)S(1)}, /*index=5*/f32[128]{0:T(12...) fusion(bf16[4096,128]{0,1:T(8,128)(2,1)S(1)} %copy-done.3, bf16[64,4096]{1,0:T(8,128)(2,1)S(1)} %bitcast.492, ...), kind=kLoop, calls=%fused_computation.40 | loop fusion | flops 18349056 | bytes 6295552 | tf_op jit(solution)/shard_map/reduce_sum | solution.py:130
  93.5 2.9 %collective-permute-done.1 = bf16[64,4096]{1,0:T(8,128)(2,1)} collective-permute-done((bf16[64,4096]{1,0:T(8,128)(2,1)}, bf16[64,4096]{1,0:T(8,128)(2,1)}, u32[]{:S(2)}, u32[]{:S(2)}) %collective-permute-start.1) | collective-permute-done | bytes 524320 | tf_op jit(solution)/shard_map/ppermute | solution.py:10
  96.5 2.3 %maximum_bitcast_fusion = bf16[4096,128]{0,1:T(8,128)(2,1)} fusion(bf16[64,4096]{1,0:T(8,128)(2,1)} %collective-permute-done.1, bf16[64,4096]{1,0:T(8,128)(2,1)} %collective-permute-done), kind=kLoop, calls=%fused_computation.62 | loop fusion | flops 2097152 | bytes 2097152 | tf_op jit(solution)/shard_map/transpose | solution.py:184
  98.7 2.3 %copy.42 = bf16[4096,128]{1,0:T(8,128)(2,1)} copy(bf16[4096,128]{0,1:T(8,128)(2,1)} %maximum_bitcast_fusion) | data formatting | bytes 2097152 | tf_op jit(solution)/shard_map/transpose | solution.py:184
  101.0 9.5 %all-to-all-start.2 = ((bf16[32,128,128]{2,1,0:T(8,128)(2,1)}), bf16[32,128,128]{2,1,0:T(8,128)(2,1)}, u32[]{:S(2)}, u32[]{:S(2)}) async-start(bf16[32,128,128]{2,1,0:T(8,128)(2,1)} %bitcast.495), calls=%async_computation.2 | async-start | bytes 2097152 | tf_op jit(solution)/shard_map/all_to_all | solution.py:184
  110.6 1.7 %fusion.28 = f32[8,128,128]{1,2,0:T(8,128)S(1)} fusion(f32[8,128,128]{1,2,0:T(8,128)} %convolution_bitcast_fusion.2, pred[128,128]{0,1:T(8,128)(4,1)S(1)} %copy.46, bf16[8,16,32,128]{3,2,1,0:T(8,128)(2,1)S(1)} %bitcast.466, bf16[8,16,32,128]{3,2,1,0:T(8,128)(2,1)S(1)} %bitcast.459), kind=kOutput, calls=%fused_computation.56 | convolution fusion | flops 134348800 | bytes 3162112 | tf_op jit(solution)/shard_map/gcbt,gcbs->gts/dot_general | solution.py:62
  112.3 0.3 copy.47
  112.7 0.6 copy.76
  113.3 1.0 concatenate.98
  114.4 3.6 %reshape.552 = f32[8,128,257]{2,1,0:T(8,128)} reshape(f32[8,32896]{1,0:T(8,128)} %concatenate.98) | data formatting | bytes 2105344 | tf_op jit(solution)/shard_map/reshape | solution.py:73
  118.0 2.8 %fusion.15 = (f32[128]{0:T(128)S(1)}, f32[128]{0:T(128)S(1)}, f32[128]{0:T(128)S(1)}, f32[128]{0:T(128)S(1)}, f32[128]{0:T(128)S(1)}, /*index=5*/f32[128]{0:T(128)S(1)}) fusion(bf16[4096,128]{0,1:T(8,128)(2,1)S(1)} %bitcast.469, bf16[64,4096]{1,0:T(8,128)(2,1)S(1)} %bitcast.479, bf16[64,4096]{1,0:T(8,128)(2,1)S(1)} %bitcast.476), kind=kLoop, calls=%fused_computation.26 | loop fusion | flops 11533568 | bytes 2100224 | tf_op jit(solution)/shard_map/reduce_sum | solution.py:130
  120.9 0.6 copy.50
  121.5 2.5 %fusion.35 = bf16[16,8,32,128]{3,1,2,0:T(8,128)(2,1)S(1)} fusion(f32[128]{0:T(128)S(1)} %get-tuple-element.62, bf16[128,4096]{1,0:T(8,128)(2,1)S(1)} %copy-done.1, f32[128]{0:T(128)S(1)} %get-tuple-element.63, f32[128]{0:T(128)S(1)} %get-tuple-element.51, f32[128]{0:T(128)S(1)} %get-tuple-element.52, f32[128]{0:T(128)S(1)} %get-tuple-element.53, ...), kind=kLoop, calls=%fused_computation.81 | loop fusion | flops 11010048 | bytes 2100736
  124.0 0.2 copy.77
  124.3 0.7 convolution_bitcast_fusion
  124.9 0.5 fusion.29
  125.6 0.3 copy.48
  125.9 0.6 copy.79
  126.6 2.4 %reshape.556 = f32[8,128,257]{2,1,0:T(8,128)} reshape(f32[8,32896]{1,0:T(8,128)S(1)} %concatenate.102) | data formatting | bytes 2105344 | tf_op jit(solution)/shard_map/reshape | solution.py:73
  129.0 1.1 slice_reduce_fusion.1
  130.1 1.1 slice_reduce_fusion
  131.2 0.6 maximum_multiply_fusion.1
  131.8 7.8 %all-to-all-done.2 = bf16[32,128,128]{2,1,0:T(8,128)(2,1)} async-done(((bf16[32,128,128]{2,1,0:T(8,128)(2,1)}), bf16[32,128,128]{2,1,0:T(8,128)(2,1)}, u32[]{:S(2)}, u32[]{:S(2)}) %all-to-all-start.2) | async-done | bytes 1048608 | tf_op jit(solution)/shard_map/all_to_all | solution.py:184
  139.5 1.6 %copy.43 = bf16[32,128,128]{1,2,0:T(8,128)(2,1)S(1)} copy(bf16[32,128,128]{2,1,0:T(8,128)(2,1)} %all-to-all-done.2) | data formatting | bytes 2097152 | tf_op jit(solution)/shard_map/all_to_all | solution.py:184
  141.2 1.3 copy.49
  (61 shorter events, 2.8 us)
Async XLA Ops:
  0.6 14.1 %copy-start = (bf16[1,2,8,128]{3,2,1,0:T(8,128)(2,1)S(1)}, bf16[1,2,8,128]{3,2,1,0:T(8,128)(2,1)}, u32[]{:S(2)}) copy-start(bf16[1,2,8,128]{3,2,1,0:T(8,128)(2,1)} %param.7) | copy-start | bytes 12292
  2.3 11.7 %copy-start.18 = (bf16[1,128,4096]{2,1,0:T(8,128)(2,1)S(1)}, bf16[1,128,4096]{2,1,0:T(8,128)(2,1)}, u32[]{:S(2)}) copy-start(bf16[1,128,4096]{2,1,0:T(8,128)(2,1)} %param.4) | copy-start | bytes 3145732
  3.6 39.2 %all-to-all-start = ((bf16[128,32,128]{2,0,1:T(8,128)(2,1)}), bf16[128,32,128]{2,0,1:T(8,128)(2,1)S(1)}, u32[]{:S(2)}, u32[]{:S(2)}) async-start(bf16[128,32,128]{2,0,1:T(8,128)(2,1)} %copy.35), calls=%async_computation | async-start | bytes 2097152 | tf_op jit(solution)/shard_map/all_to_all | solution.py:143
  14.6 1.4 copy-start.19
  44.6 34.0 %all-to-all-start.1 = ((bf16[128,32,128]{2,0,1:T(8,128)(2,1)}), bf16[128,32,128]{2,0,1:T(8,128)(2,1)}, u32[]{:S(2)}, u32[]{:S(2)}) async-start(bf16[128,32,128]{2,0,1:T(8,128)(2,1)} %copy.40), calls=%async_computation.1 | async-start | bytes 2097152 | tf_op jit(solution)/shard_map/all_to_all | solution.py:145
  49.9 1.0 copy-start.16
  50.0 1.3 copy-start.14
  51.8 2.1 %copy-start.4 = (bf16[8,8,32,128]{3,1,2,0:T(8,128)(2,1)}, bf16[8,8,32,128]{3,1,2,0:T(8,128)(2,1)S(1)}, u32[]{:S(2)}) copy-start(bf16[8,8,32,128]{3,1,2,0:T(8,128)(2,1)S(1)} %copy.91) | copy-start | bytes 1572868
  54.4 14.3 %copy-start.10 = (bf16[8,8,32,128]{3,1,2,0:T(8,128)(2,1)}, bf16[8,8,32,128]{3,1,2,0:T(8,128)(2,1)S(1)}, u32[]{:S(2)}) copy-start(bf16[8,8,32,128]{3,1,2,0:T(8,128)(2,1)S(1)} %copy.90) | copy-start | bytes 1572868
  57.0 36.5 %collective-permute-start = (bf16[64,4096]{1,0:T(8,128)(2,1)}, bf16[64,4096]{1,0:T(8,128)(2,1)}, u32[]{:S(2)}, u32[]{:S(2)}) collective-permute-start(bf16[64,4096]{1,0:T(8,128)(2,1)} %add_convert_fusion.3), channel_id=1, source_target_pairs={{32,0},{64,32},{96,64},{128,96},{160,128},{192,160},{224,192},{256... | collective-permute-start | bytes 1572872 | tf_op jit(solution)/shard_map/ppermute | solution.py:10
  69.3 1.9 %copy-start.7 = (bf16[8,8,32,128]{3,1,2,0:T(8,128)(2,1)}, bf16[8,8,32,128]{3,1,2,0:T(8,128)(2,1)S(1)}, u32[]{:S(2)}) copy-start(bf16[8,8,32,128]{3,1,2,0:T(8,128)(2,1)S(1)} %copy.89) | copy-start | bytes 1572868
  72.2 6.4 %copy-start.12 = (bf16[8,8,32,128]{3,1,2,0:T(8,128)(2,1)}, bf16[8,8,32,128]{3,1,2,0:T(8,128)(2,1)S(1)}, u32[]{:S(2)}) copy-start(bf16[8,8,32,128]{3,1,2,0:T(8,128)(2,1)S(1)} %copy.88) | copy-start | bytes 1572868
  74.5 21.9 %collective-permute-start.1 = (bf16[64,4096]{1,0:T(8,128)(2,1)}, bf16[64,4096]{1,0:T(8,128)(2,1)}, u32[]{:S(2)}, u32[]{:S(2)}) collective-permute-start(bf16[64,4096]{1,0:T(8,128)(2,1)} %add_convert_fusion.1), channel_id=1, source_target_pairs={{32,0},{64,32},{96,64},{128,96},{160,128},{192,160},{224,192},{256... | collective-permute-start | bytes 1572872 | tf_op jit(solution)/shard_map/ppermute | solution.py:10
  80.1 1.0 copy-start.2
  81.1 2.8 %copy-start.17 = (bf16[2,8,128,128]{3,2,1,0:T(8,128)(2,1)S(1)}, bf16[2,8,128,128]{3,2,1,0:T(8,128)(2,1)}, u32[]{:S(2)}) copy-start(bf16[2,8,128,128]{3,2,1,0:T(8,128)(2,1)} %get-tuple-element.49) | copy-start | bytes 1572868
  84.4 1.5 %copy-start.15 = (bf16[2,8,128,128]{3,2,1,0:T(8,128)(2,1)S(1)}, bf16[2,8,128,128]{3,2,1,0:T(8,128)(2,1)}, u32[]{:S(2)}) copy-start(bf16[2,8,128,128]{3,2,1,0:T(8,128)(2,1)} %get-tuple-element.48) | copy-start | bytes 1572868
  85.9 1.2 copy-start.3
  85.9 1.4 copy-start.5
  85.9 1.5 %copy-start.8 = (bf16[8,8,32,128]{3,1,2,0:T(8,128)(2,1)S(1)}, bf16[8,8,32,128]{3,1,2,0:T(8,128)(2,1)}, u32[]{:S(2)}) copy-start(bf16[8,8,32,128]{3,1,2,0:T(8,128)(2,1)} %copy-done.7) | copy-start | bytes 1572868
  85.9 1.7 %copy-start.11 = (bf16[8,8,32,128]{3,1,2,0:T(8,128)(2,1)S(1)}, bf16[8,8,32,128]{3,1,2,0:T(8,128)(2,1)}, u32[]{:S(2)}) copy-start(bf16[8,8,32,128]{3,1,2,0:T(8,128)(2,1)} %copy-done.10) | copy-start | bytes 1572868
  85.9 1.8 %copy-start.13 = (bf16[8,8,32,128]{3,1,2,0:T(8,128)(2,1)S(1)}, bf16[8,8,32,128]{3,1,2,0:T(8,128)(2,1)}, u32[]{:S(2)}) copy-start(bf16[8,8,32,128]{3,1,2,0:T(8,128)(2,1)} %copy-done.12) | copy-start | bytes 1572868
  101.0 38.5 %all-to-all-start.2 = ((bf16[32,128,128]{2,1,0:T(8,128)(2,1)}), bf16[32,128,128]{2,1,0:T(8,128)(2,1)}, u32[]{:S(2)}, u32[]{:S(2)}) async-start(bf16[32,128,128]{2,1,0:T(8,128)(2,1)} %bitcast.495), calls=%async_computation.2 | async-start | bytes 2097152 | tf_op jit(solution)/shard_map/all_to_all | solution.py:184
  113.3 4.7 %copy-start.1 = (bf16[128,4096]{1,0:T(8,128)(2,1)S(1)}, bf16[128,4096]{1,0:T(8,128)(2,1)}, u32[]{:S(2)}) copy-start(bf16[128,4096]{1,0:T(8,128)(2,1)} %get-tuple-element.45) | copy-start | bytes 3145732
  113.3 4.7 %copy-start.6 = (bf16[8,8,32,128]{3,1,2,0:T(8,128)(2,1)S(1)}, bf16[8,8,32,128]{3,1,2,0:T(8,128)(2,1)}, u32[]{:S(2)}) copy-start(bf16[8,8,32,128]{3,1,2,0:T(8,128)(2,1)} %copy-done.4) | copy-start | bytes 1572868
  113.3 4.7 %copy-start.9 = (bf16[8,8,32,128]{3,1,2,0:T(8,128)(2,1)S(1)}, bf16[8,8,32,128]{3,1,2,0:T(8,128)(2,1)}, u32[]{:S(2)}) copy-start(bf16[8,8,32,128]{3,1,2,0:T(8,128)(2,1)} %copy-done.7) | copy-start | bytes 1572868

commit v10 on v9

--- a/solution.py
+++ b/solution.py
@@ -154,7 +154,7 @@
         grad_half = top_grad[rows_of]
         if index:
             grad_half, input_grad_h = lax.optimization_barrier((grad_half, input_grad_h))
-            behinds.append(from_behind(input_grad_h, "pipe", -1))
+            behinds.append(from_behind(input_grad_h.T, "pipe", -1))
         short_half = short_all[:, :, rows_of]
         dmix_two_h = anti_long(grad_half, circ_now[1, groups_of], circ_past[1, groups_of]).astype(jnp.bfloat16)
         middle_grad_h = (
@@ -172,7 +172,7 @@
     dmix_two = jnp.concatenate(dmix_twos)
     middle_grad = jnp.concatenate(middle_grads)
     dmix_one = jnp.concatenate(dmix_ones)
-    behinds.append(from_behind(input_grad_h, "pipe", -1))
+    behinds.append(from_behind(input_grad_h.T, "pipe", -1))
     input_rows, _ = lax.optimization_barrier((input_rows, input_grad_h))
     source = input_rows.T
     mixed_one = short_mix(source, short_all[0]).astype(jnp.bfloat16)
@@ -180,8 +180,8 @@
     middle = (source.astype(jnp.float32) + long_one).astype(jnp.bfloat16)
     mixed_two = short_mix(middle, short_all[1]).astype(jnp.bfloat16)
     behinds = list(lax.optimization_barrier((*behinds, middle))[:-1])
-    behind = jnp.concatenate(behinds)
-    own_rows = lax.all_to_all(behind.T, "dp", split_axis=0, concat_axis=1, tiled=True)
+    behind = jnp.concatenate(behinds, axis=1)
+    own_rows = lax.all_to_all(behind, "dp", split_axis=0, concat_axis=1, tiled=True)
     passed_grad = own_rows[None]
     dlong_two = lag_grad(mixed_two, top_grad, group_count, taps)
     dshort_two = short_corr_rows(dmix_two.T, middle.T, tap_count)

time: 143 us -> 143 us (level)
    concatenate x0 -> x1, local copies, waits for them, and re-layouts: none -> 2.28 us  [body(): behind = jnp.concatenate(behinds, axis=1)]
    transpose x1 -> x0, local copies, waits for them, and re-layouts: 2.28 us -> none  [body(): own_rows = lax.all_to_all(behind.T, 'dp', split_axis=0, concat_axis=1, ti...]
    concatenate x0 -> x1, other arithmetic: none -> 2.26 us  [body(): behind = jnp.concatenate(behinds, axis=1)]
    transpose x1 -> x0, other arithmetic: 2.26 us -> none  [body(): own_rows = lax.all_to_all(behind.T, 'dp', split_axis=0, concat_axis=1, ti...]
where the time goes in v10:
time: 143 us; the launch traced here: 142 us
  starting transfers between devices  38.6 us (27%)
  waiting for transfers between devices  37.8 us (26%)
  local copies, waits for them, and re-layouts  27.9 us (20%)
  other arithmetic  27.8 us (19%)
  matrix products  9.01 us (6%)
    all_to_all x1, waiting for transfers between devices, body(): lax.all_to_all(out_grad[0], 'dp', split_axis=1, concat_axis=0, tiled=True)  25.4 us
    ppermute x2, starting transfers between devices, from_behind(): return lax.ppermute(shard, axis, pairs)  13.8 us
    unnamed x59, local copies, waits for them, and re-layouts  10.7 us
    all_to_all x1, starting transfers between devices, body(): lax.all_to_all(out_grad[0], 'dp', split_axis=1, concat_axis=0, tiled=True)  10.2 us
    all_to_all x1, starting transfers between devices, body(): lax.all_to_all(behind, 'dp', split_axis=0, concat_axis=1, tiled=True)  9.55 us
    reduce_sum x2, other arithmetic, short_corr_rows(): jnp.sum(grad_wide * padded[start:start + row_count].astype(jnp.float32),...  8.68 us
    all_to_all x1, waiting for transfers between devices, body(): lax.all_to_all(behind, 'dp', split_axis=0, concat_axis=1, tiled=True)  7.75 us
    reshape x2, local copies, waits for them, and re-layouts, lag_grad(): skewed = padded.reshape(group_count, taps, 2 * taps + 1)[:, :, :taps]  6.02 us
  transfers between devices with their start and end apart: 5, of which 4 were waited for; matrix products, arithmetic and copies ran while one was open for 35% of the time, Pallas kernels for 0%

profile of v10, /device:TPU:6, one launch (start us, length us, event | category | flops | bytes accessed | tf_op | source)
XLA Modules:
  0.0 142.5 jit_solution(8994439053763688653)
XLA Ops:
  0.6 1.6 %copy.34 = bf16[1,128,4096]{1,2,0:T(8,128)(2,1)S(1)} copy(bf16[1,128,4096]{2,1,0:T(8,128)(2,1)} %param.5) | data formatting | bytes 2097152 | tf_op args[1]
  2.3 1.3 copy.35
  3.6 10.2 %all-to-all-start = ((bf16[128,32,128]{2,0,1:T(8,128)(2,1)}), bf16[128,32,128]{2,0,1:T(8,128)(2,1)S(1)}, u32[]{:S(2)}, u32[]{:S(2)}) async-start(bf16[128,32,128]{2,0,1:T(8,128)(2,1)} %copy.35), calls=%async_computation | async-start | bytes 2097152 | tf_op jit(solution)/shard_map/all_to_all | solution.py:143
  14.0 0.7 copy.36
  14.7 1.4 fusion.27
  16.2 1.1 broadcast_select_fusion
  17.3 25.4 %all-to-all-done = bf16[128,32,128]{2,0,1:T(8,128)(2,1)S(1)} async-done(((bf16[128,32,128]{2,0,1:T(8,128)(2,1)}), bf16[128,32,128]{2,0,1:T(8,128)(2,1)S(1)}, u32[]{:S(2)}, u32[]{:S(2)}) %all-to-all-start) | async-done | bytes 1048608 | tf_op jit(solution)/shard_map/all_to_all | solution.py:143
  42.8 0.5 copy.37
  43.3 1.3 copy.40
  44.6 5.0 %all-to-all-start.1 = ((bf16[128,32,128]{2,0,1:T(8,128)(2,1)}), bf16[128,32,128]{2,0,1:T(8,128)(2,1)}, u32[]{:S(2)}, u32[]{:S(2)}) async-start(bf16[128,32,128]{2,0,1:T(8,128)(2,1)} %copy.40), calls=%async_computation.1 | async-start | bytes 2097152 | tf_op jit(solution)/shard_map/all_to_all | solution.py:145
  49.7 0.2 copy.78
  50.3 0.6 copy-done.16
  50.9 0.3 fusion.47
  51.3 0.3 fusion.23
  51.6 0.2 copy.91
  51.8 1.5 %add_convert_fusion.4 = bf16[64,4096]{1,0:T(8,128)(2,1)S(1)} fusion(bf16[64,4096]{1,0:T(8,128)(2,1)S(1)} %bitcast.474, f32[64]{0:T(128)S(1)} %get-tuple-element.85, f32[64]{0:T(128)S(1)} %get-tuple-element.86, f32[64]{0:T(128)S(1)} %get-tuple-element.87, f32[64]{0:T(128)S(1)} %get-tuple-element.88, f32[64]{0:T(128)S(1)} %get-tuple-element.89, ...), kind=kLoop, calls=%fused_computation.80 | loop fusion | flops 6029312 | bytes 1574656 | tf_op jit(solution)/shard_map/convert_element_type | solution.py:162
  53.6 0.3 fusion.46
  53.9 0.3 fusion.24
  54.2 0.2 copy.90
  54.4 2.3 %add_convert_fusion.3 = bf16[64,4096]{1,0:T(8,128)(2,1)} fusion(bf16[64,4096]{1,0:T(8,128)(2,1)S(1)} %bitcast.489, bf16[64,4096]{1,0:T(8,128)(2,1)S(1)} %add_convert_fusion.4, f32[64]{0:T(128)S(1)} %get-tuple-element.78, f32[64]{0:T(128)S(1)} %get-tuple-element.79, f32[64]{0:T(128)S(1)} %get-tuple-element.80, f32[64]{0:T(128)S(1)} %get-tuple-element.81, ...), kind=kLoop, calls=%fused_computation.79 | loop fusion | flops 6029312 | bytes 1574656 | tf_op jit(solution)/shard_map/convert_element_type | solution.py:168
  57.0 11.4 %collective-permute-start = (bf16[4096,64]{0,1:T(8,128)(2,1)}, bf16[4096,64]{0,1:T(8,128)(2,1)}, u32[]{:S(2)}, u32[]{:S(2)}) collective-permute-start(bf16[4096,64]{0,1:T(8,128)(2,1)} %bitcast.37), channel_id=1, source_target_pairs={{32,0},{64,32},{96,64},{128,96},{160,128},{192,160},{224,192},{256... | collective-permute-start | bytes 1572872 | tf_op jit(solution)/shard_map/ppermute | solution.py:10
  68.4 0.3 fusion.45
  68.7 0.3 fusion.25
  69.0 0.2 copy.89
  69.3 1.5 %add_convert_fusion.2 = bf16[64,4096]{1,0:T(8,128)(2,1)S(1)} fusion(bf16[64,4096]{1,0:T(8,128)(2,1)S(1)} %bitcast.477, bf16[64,4096]{1,0:T(8,128)(2,1)S(1)} %get-tuple-element.12, f32[64]{0:T(128)S(1)} %get-tuple-element.71, f32[64]{0:T(128)S(1)} %get-tuple-element.72, f32[64]{0:T(128)S(1)} %get-tuple-element.73, f32[64]{0:T(128)S(1)} %get-tuple-element.74, ...), kind=kLoop, calls=%fused_computation.78 | loop fusion | flops 6029312 | bytes 1574656 | tf_op jit(solution)/shard_map/convert_element_type | solution.py:162
  71.1 0.2 copy.75
  71.4 0.3 fusion.44
  71.7 0.3 fusion.26
  72.2 2.3 %add_convert_fusion.1 = bf16[64,4096]{1,0:T(8,128)(2,1)} fusion(bf16[64,4096]{1,0:T(8,128)(2,1)S(1)} %bitcast.491, bf16[64,4096]{1,0:T(8,128)(2,1)S(1)} %add_convert_fusion.2, f32[64]{0:T(128)S(1)} %get-tuple-element.65, f32[64]{0:T(128)S(1)} %get-tuple-element.66, f32[64]{0:T(128)S(1)} %get-tuple-element.67, f32[64]{0:T(128)S(1)} %get-tuple-element.68, ...), kind=kLoop, calls=%fused_computation.77 | loop fusion | flops 6029312 | bytes 1574656 | tf_op jit(solution)/shard_map/convert_element_type | solution.py:168
  74.5 2.4 %collective-permute-start.1 = (bf16[4096,64]{0,1:T(8,128)(2,1)}, bf16[4096,64]{0,1:T(8,128)(2,1)}, u32[]{:S(2)}, u32[]{:S(2)}) collective-permute-start(bf16[4096,64]{0,1:T(8,128)(2,1)} %bitcast.64), channel_id=1, source_target_pairs={{32,0},{64,32},{96,64},{128,96},{160,128},{192,160},{224,192},{256... | collective-permute-start | bytes 1572872 | tf_op jit(solution)/shard_map/ppermute | solution.py:10
  77.0 1.7 %all-to-all-done.1 = bf16[128,32,128]{2,0,1:T(8,128)(2,1)} async-done(((bf16[128,32,128]{2,0,1:T(8,128)(2,1)}), bf16[128,32,128]{2,0,1:T(8,128)(2,1)}, u32[]{:S(2)}, u32[]{:S(2)}) %all-to-all-start.1) | async-done | bytes 1048608 | tf_op jit(solution)/shard_map/all_to_all | solution.py:145
  78.6 1.5 %copy.41 = bf16[4096,128]{0,1:T(8,128)(2,1)S(1)} copy(bf16[4096,128]{1,0:T(8,128)(2,1)} %bitcast.67) | data formatting | bytes 2097152 | tf_op jit(solution)/shard_map/optimization_barrier | solution.py:176
  80.2 1.0 copy-done.2
  81.1 2.5 %fusion.36 = bf16[16,8,32,128]{3,1,2,0:T(8,128)(2,1)S(1)} fusion(f32[128]{0:T(128)S(1)} %get-tuple-element.55, bf16[128,4096]{1,0:T(8,128)(2,1)S(1)} %bitcast.470, f32[128]{0:T(128)S(1)} %get-tuple-element.56, f32[128]{0:T(128)S(1)} %get-tuple-element.57, f32[128]{0:T(128)S(1)} %get-tuple-element.58, f32[128]{0:T(128)S(1)} %get-tuple-element.59, ...), kind=kLoop, calls=%fused_computation.82 | loop fusion | flops 11010048 | bytes 2100736
  83.7 0.2 copy.73
  83.9 0.4 fusion.43
  84.4 1.5 %convolution_bitcast_fusion.2 = f32[8,128,128]{1,2,0:T(8,128)} fusion(bf16[8,16,31,128]{3,2,1,0:T(8,128)(2,1)S(1)} %bitcast.457, bf16[8,16,32,128]{3,2,1,0:T(8,128)(2,1)S(1)} %bitcast.465), kind=kOutput, calls=%fused_computation.54 | convolution fusion | flops 134217728 | bytes 2588672 | tf_op jit(solution)/shard_map/gcbt,gcbs->gts/dot_general | solution.py:65
  85.9 0.5 convolution_add_fusion
  86.4 0.7 copy-done.3
  87.7 5.9 %fusion.22 = (f32[128]{0:T(128)S(1)}, f32[128]{0:T(128)S(1)}, f32[128]{0:T(128)S(1)}, f32[128]{0:T(128)S(1)}, f32[128]{0:T(128)S(1)}, /*index=5*/f32[128]{0:T(12...) fusion(bf16[4096,128]{0,1:T(8,128)(2,1)S(1)} %copy-done.3, bf16[64,4096]{1,0:T(8,128)(2,1)S(1)} %bitcast.492, ...), kind=kLoop, calls=%fused_computation.40 | loop fusion | flops 18349056 | bytes 6295552 | tf_op jit(solution)/shard_map/reduce_sum | solution.py:130
  93.5 2.9 %collective-permute-done.1 = bf16[4096,64]{0,1:T(8,128)(2,1)} collective-permute-done((bf16[4096,64]{0,1:T(8,128)(2,1)}, bf16[4096,64]{0,1:T(8,128)(2,1)}, u32[]{:S(2)}, u32[]{:S(2)}) %collective-permute-start.1) | collective-permute-done | bytes 524320 | tf_op jit(solution)/shard_map/ppermute | solution.py:10
  96.5 2.3 %pad_maximum_fusion = bf16[4096,128]{0,1:T(8,128)(2,1)} fusion(bf16[4096,64]{0,1:T(8,128)(2,1)} %collective-permute-done.1, bf16[4096,64]{0,1:T(8,128)(2,1)} %collective-permute-done), kind=kLoop, calls=%fused_computation.62 | loop fusion | flops 2097152 | bytes 2097152 | tf_op jit(solution)/shard_map/concatenate | solution.py:183
  98.7 2.3 %copy.42 = bf16[4096,128]{1,0:T(8,128)(2,1)} copy(bf16[4096,128]{0,1:T(8,128)(2,1)} %pad_maximum_fusion) | data formatting | bytes 2097152 | tf_op jit(solution)/shard_map/concatenate | solution.py:183
  101.0 9.5 %all-to-all-start.2 = ((bf16[32,128,128]{2,1,0:T(8,128)(2,1)}), bf16[32,128,128]{2,1,0:T(8,128)(2,1)}, u32[]{:S(2)}, u32[]{:S(2)}) async-start(bf16[32,128,128]{2,1,0:T(8,128)(2,1)} %bitcast.495), calls=%async_computation.2 | async-start | bytes 2097152 | tf_op jit(solution)/shard_map/all_to_all | solution.py:184
  110.6 1.7 %fusion.28 = f32[8,128,128]{1,2,0:T(8,128)S(1)} fusion(f32[8,128,128]{1,2,0:T(8,128)} %convolution_bitcast_fusion.2, pred[128,128]{0,1:T(8,128)(4,1)S(1)} %copy.46, bf16[8,16,32,128]{3,2,1,0:T(8,128)(2,1)S(1)} %bitcast.466, bf16[8,16,32,128]{3,2,1,0:T(8,128)(2,1)S(1)} %bitcast.459), kind=kOutput, calls=%fused_computation.56 | convolution fusion | flops 134348800 | bytes 3162112 | tf_op jit(solution)/shard_map/gcbt,gcbs->gts/dot_general | solution.py:62
  112.3 0.3 copy.47
  112.7 0.6 copy.76
  113.3 1.0 concatenate.98
  114.4 3.6 %reshape.552 = f32[8,128,257]{2,1,0:T(8,128)} reshape(f32[8,32896]{1,0:T(8,128)} %concatenate.98) | data formatting | bytes 2105344 | tf_op jit(solution)/shard_map/reshape | solution.py:73
  118.0 2.8 %fusion.15 = (f32[128]{0:T(128)S(1)}, f32[128]{0:T(128)S(1)}, f32[128]{0:T(128)S(1)}, f32[128]{0:T(128)S(1)}, f32[128]{0:T(128)S(1)}, /*index=5*/f32[128]{0:T(128)S(1)}) fusion(bf16[4096,128]{0,1:T(8,128)(2,1)S(1)} %bitcast.469, bf16[64,4096]{1,0:T(8,128)(2,1)S(1)} %bitcast.479, bf16[64,4096]{1,0:T(8,128)(2,1)S(1)} %bitcast.476), kind=kLoop, calls=%fused_computation.26 | loop fusion | flops 11533568 | bytes 2100224 | tf_op jit(solution)/shard_map/reduce_sum | solution.py:130
  120.9 0.6 copy.50
  121.5 2.5 %fusion.35 = bf16[16,8,32,128]{3,1,2,0:T(8,128)(2,1)S(1)} fusion(f32[128]{0:T(128)S(1)} %get-tuple-element.62, bf16[128,4096]{1,0:T(8,128)(2,1)S(1)} %copy-done.1, f32[128]{0:T(128)S(1)} %get-tuple-element.63, f32[128]{0:T(128)S(1)} %get-tuple-element.51, f32[128]{0:T(128)S(1)} %get-tuple-element.52, f32[128]{0:T(128)S(1)} %get-tuple-element.53, ...), kind=kLoop, calls=%fused_computation.81 | loop fusion | flops 11010048 | bytes 2100736
  124.0 0.2 copy.77
  124.3 0.6 convolution_bitcast_fusion
  124.9 0.5 fusion.29
  125.6 0.3 copy.48
  125.9 0.6 copy.79
  126.6 2.4 %reshape.556 = f32[8,128,257]{2,1,0:T(8,128)} reshape(f32[8,32896]{1,0:T(8,128)S(1)} %concatenate.102) | data formatting | bytes 2105344 | tf_op jit(solution)/shard_map/reshape | solution.py:73
  129.0 1.1 slice_reduce_fusion.1
  130.1 1.1 slice_reduce_fusion
  131.2 0.6 maximum_multiply_fusion.1
  131.8 7.8 %all-to-all-done.2 = bf16[32,128,128]{2,1,0:T(8,128)(2,1)} async-done(((bf16[32,128,128]{2,1,0:T(8,128)(2,1)}), bf16[32,128,128]{2,1,0:T(8,128)(2,1)}, u32[]{:S(2)}, u32[]{:S(2)}) %all-to-all-start.2) | async-done | bytes 1048608 | tf_op jit(solution)/shard_map/all_to_all | solution.py:184
  139.5 1.6 %copy.43 = bf16[32,128,128]{1,2,0:T(8,128)(2,1)S(1)} copy(bf16[32,128,128]{2,1,0:T(8,128)(2,1)} %all-to-all-done.2) | data formatting | bytes 2097152 | tf_op jit(solution)/shard_map/all_to_all | solution.py:184
  141.2 1.3 copy.49
  (61 shorter events, 2.8 us)
Async XLA Ops:
  0.6 14.1 %copy-start = (bf16[1,2,8,128]{3,2,1,0:T(8,128)(2,1)S(1)}, bf16[1,2,8,128]{3,2,1,0:T(8,128)(2,1)}, u32[]{:S(2)}) copy-start(bf16[1,2,8,128]{3,2,1,0:T(8,128)(2,1)} %param.7) | copy-start | bytes 12292
  2.3 11.7 %copy-start.18 = (bf16[1,128,4096]{2,1,0:T(8,128)(2,1)S(1)}, bf16[1,128,4096]{2,1,0:T(8,128)(2,1)}, u32[]{:S(2)}) copy-start(bf16[1,128,4096]{2,1,0:T(8,128)(2,1)} %param.4) | copy-start | bytes 3145732
  3.6 39.2 %all-to-all-start = ((bf16[128,32,128]{2,0,1:T(8,128)(2,1)}), bf16[128,32,128]{2,0,1:T(8,128)(2,1)S(1)}, u32[]{:S(2)}, u32[]{:S(2)}) async-start(bf16[128,32,128]{2,0,1:T(8,128)(2,1)} %copy.35), calls=%async_computation | async-start | bytes 2097152 | tf_op jit(solution)/shard_map/all_to_all | solution.py:143
  14.6 1.4 copy-start.19
  44.6 34.0 %all-to-all-start.1 = ((bf16[128,32,128]{2,0,1:T(8,128)(2,1)}), bf16[128,32,128]{2,0,1:T(8,128)(2,1)}, u32[]{:S(2)}, u32[]{:S(2)}) async-start(bf16[128,32,128]{2,0,1:T(8,128)(2,1)} %copy.40), calls=%async_computation.1 | async-start | bytes 2097152 | tf_op jit(solution)/shard_map/all_to_all | solution.py:145
  49.9 1.0 copy-start.16
  50.0 1.3 copy-start.14
  51.8 2.1 %copy-start.4 = (bf16[8,8,32,128]{3,1,2,0:T(8,128)(2,1)}, bf16[8,8,32,128]{3,1,2,0:T(8,128)(2,1)S(1)}, u32[]{:S(2)}) copy-start(bf16[8,8,32,128]{3,1,2,0:T(8,128)(2,1)S(1)} %copy.91) | copy-start | bytes 1572868
  54.4 14.3 %copy-start.10 = (bf16[8,8,32,128]{3,1,2,0:T(8,128)(2,1)}, bf16[8,8,32,128]{3,1,2,0:T(8,128)(2,1)S(1)}, u32[]{:S(2)}) copy-start(bf16[8,8,32,128]{3,1,2,0:T(8,128)(2,1)S(1)} %copy.90) | copy-start | bytes 1572868
  57.0 36.5 %collective-permute-start = (bf16[4096,64]{0,1:T(8,128)(2,1)}, bf16[4096,64]{0,1:T(8,128)(2,1)}, u32[]{:S(2)}, u32[]{:S(2)}) collective-permute-start(bf16[4096,64]{0,1:T(8,128)(2,1)} %bitcast.37), channel_id=1, source_target_pairs={{32,0},{64,32},{96,64},{128,96},{160,128},{192,160},{224,192},{256... | collective-permute-start | bytes 1572872 | tf_op jit(solution)/shard_map/ppermute | solution.py:10
  69.3 1.9 %copy-start.7 = (bf16[8,8,32,128]{3,1,2,0:T(8,128)(2,1)}, bf16[8,8,32,128]{3,1,2,0:T(8,128)(2,1)S(1)}, u32[]{:S(2)}) copy-start(bf16[8,8,32,128]{3,1,2,0:T(8,128)(2,1)S(1)} %copy.89) | copy-start | bytes 1572868
  72.2 6.4 %copy-start.12 = (bf16[8,8,32,128]{3,1,2,0:T(8,128)(2,1)}, bf16[8,8,32,128]{3,1,2,0:T(8,128)(2,1)S(1)}, u32[]{:S(2)}) copy-start(bf16[8,8,32,128]{3,1,2,0:T(8,128)(2,1)S(1)} %copy.88) | copy-start | bytes 1572868
  74.5 21.9 %collective-permute-start.1 = (bf16[4096,64]{0,1:T(8,128)(2,1)}, bf16[4096,64]{0,1:T(8,128)(2,1)}, u32[]{:S(2)}, u32[]{:S(2)}) collective-permute-start(bf16[4096,64]{0,1:T(8,128)(2,1)} %bitcast.64), channel_id=1, source_target_pairs={{32,0},{64,32},{96,64},{128,96},{160,128},{192,160},{224,192},{256... | collective-permute-start | bytes 1572872 | tf_op jit(solution)/shard_map/ppermute | solution.py:10
  80.1 1.0 copy-start.2
  81.1 2.8 %copy-start.17 = (bf16[2,8,128,128]{3,2,1,0:T(8,128)(2,1)S(1)}, bf16[2,8,128,128]{3,2,1,0:T(8,128)(2,1)}, u32[]{:S(2)}) copy-start(bf16[2,8,128,128]{3,2,1,0:T(8,128)(2,1)} %get-tuple-element.49) | copy-start | bytes 1572868
  84.4 1.5 %copy-start.15 = (bf16[2,8,128,128]{3,2,1,0:T(8,128)(2,1)S(1)}, bf16[2,8,128,128]{3,2,1,0:T(8,128)(2,1)}, u32[]{:S(2)}) copy-start(bf16[2,8,128,128]{3,2,1,0:T(8,128)(2,1)} %get-tuple-element.48) | copy-start | bytes 1572868
  85.9 1.2 copy-start.3
  85.9 1.4 copy-start.5
  85.9 1.5 %copy-start.8 = (bf16[8,8,32,128]{3,1,2,0:T(8,128)(2,1)S(1)}, bf16[8,8,32,128]{3,1,2,0:T(8,128)(2,1)}, u32[]{:S(2)}) copy-start(bf16[8,8,32,128]{3,1,2,0:T(8,128)(2,1)} %copy-done.7) | copy-start | bytes 1572868
  85.9 1.7 %copy-start.11 = (bf16[8,8,32,128]{3,1,2,0:T(8,128)(2,1)S(1)}, bf16[8,8,32,128]{3,1,2,0:T(8,128)(2,1)}, u32[]{:S(2)}) copy-start(bf16[8,8,32,128]{3,1,2,0:T(8,128)(2,1)} %copy-done.10) | copy-start | bytes 1572868
  85.9 1.8 %copy-start.13 = (bf16[8,8,32,128]{3,1,2,0:T(8,128)(2,1)S(1)}, bf16[8,8,32,128]{3,1,2,0:T(8,128)(2,1)}, u32[]{:S(2)}) copy-start(bf16[8,8,32,128]{3,1,2,0:T(8,128)(2,1)} %copy-done.12) | copy-start | bytes 1572868
  101.0 38.5 %all-to-all-start.2 = ((bf16[32,128,128]{2,1,0:T(8,128)(2,1)}), bf16[32,128,128]{2,1,0:T(8,128)(2,1)}, u32[]{:S(2)}, u32[]{:S(2)}) async-start(bf16[32,128,128]{2,1,0:T(8,128)(2,1)} %bitcast.495), calls=%async_computation.2 | async-start | bytes 2097152 | tf_op jit(solution)/shard_map/all_to_all | solution.py:184
  113.3 4.7 %copy-start.1 = (bf16[128,4096]{1,0:T(8,128)(2,1)S(1)}, bf16[128,4096]{1,0:T(8,128)(2,1)}, u32[]{:S(2)}) copy-start(bf16[128,4096]{1,0:T(8,128)(2,1)} %get-tuple-element.45) | copy-start | bytes 3145732
  113.3 4.7 %copy-start.6 = (bf16[8,8,32,128]{3,1,2,0:T(8,128)(2,1)S(1)}, bf16[8,8,32,128]{3,1,2,0:T(8,128)(2,1)}, u32[]{:S(2)}) copy-start(bf16[8,8,32,128]{3,1,2,0:T(8,128)(2,1)} %copy-done.4) | copy-start | bytes 1572868
  113.3 4.7 %copy-start.9 = (bf16[8,8,32,128]{3,1,2,0:T(8,128)(2,1)S(1)}, bf16[8,8,32,128]{3,1,2,0:T(8,128)(2,1)}, u32[]{:S(2)}) copy-start(bf16[8,8,32,128]{3,1,2,0:T(8,128)(2,1)} %copy-done.7) | copy-start | bytes 1572868

commit v11 on v9

--- a/solution.py
+++ b/solution.py
@@ -180,13 +180,15 @@
     middle = (source.astype(jnp.float32) + long_one).astype(jnp.bfloat16)
     mixed_two = short_mix(middle, short_all[1]).astype(jnp.bfloat16)
     behinds = list(lax.optimization_barrier((*behinds, middle))[:-1])
-    behind = jnp.concatenate(behinds)
+    behind, dmix_two_t, dmix_one_t = lax.optimization_barrier(
+        (jnp.concatenate(behinds), dmix_two.T, dmix_one.T)
+    )
     own_rows = lax.all_to_all(behind.T, "dp", split_axis=0, concat_axis=1, tiled=True)
     passed_grad = own_rows[None]
     dlong_two = lag_grad(mixed_two, top_grad, group_count, taps)
-    dshort_two = short_corr_rows(dmix_two.T, middle.T, tap_count)
+    dshort_two = short_corr_rows(dmix_two_t, middle.T, tap_count)
     dlong_one = lag_grad(mixed_one, middle_grad, group_count, taps)
-    dshort_one = short_corr_rows(dmix_one.T, input_rows, tap_count)
+    dshort_one = short_corr_rows(dmix_one_t, input_rows, tap_count)
     factor = float(rows * devices) ** (-0.5)
     short_grad = jnp.stack([dshort_one, dshort_two])[None] * factor
     long_grad = jnp.stack([dlong_one, dlong_two])[None] * factor

time: 143 us -> 149 us (1.042)
  other arithmetic: 27.8 us -> 31.6 us
  local copies, waits for them, and re-layouts: 27.9 us -> 30.1 us
    all_to_all x1, waiting for transfers between devices: 7.76 us -> 12.7 us  [body(): lax.all_to_all(behind.T, 'dp', split_axis=0, concat_axis=1, tiled=True)]
    ppermute x2, waiting for transfers between devices: 2.92 us -> 0.01 us  [from_behind(): return lax.ppermute(shard, axis, pairs)]
    concatenate x0 -> x1, other arithmetic: none -> 2.26 us  [body(): jnp.concatenate(behinds)]
    concatenate x2, local copies, waits for them, and re-layouts: 0.66 us -> 2.91 us  [lag_grad(): jnp.concatenate([joined, joined], axis=2)]
    convert_element_type x0 -> x1, other arithmetic: none -> 1.87 us  [body(): middle = (source.astype(jnp.float32) + long_one).astype(jnp.bfloat16)]
    all_to_all x1, waiting for transfers between devices: 1.67 us -> 0.01 us  [body(): lax.all_to_all(later_input, 'dp', split_axis=1, concat_axis=0, tiled=True)]
    unnamed x59 -> x35, local copies, waits for them, and re-layouts: 10.7 us -> 11.5 us
  transfers between devices with their start and end apart: 5 -> 5, of which waited for: 4 -> 2; matrix products, arithmetic and copies ran while one was open for 35% -> 36% of each run, Pallas kernels for 0% -> 0%
where the time goes in v11:
time: 149 us; the launch traced here: 148 us
  starting transfers between devices  38.9 us (26%)
  waiting for transfers between devices  38.2 us (26%)
  other arithmetic  31.6 us (21%)
  local copies, waits for them, and re-layouts  30.1 us (20%)
  matrix products  8.12 us (5%)
    all_to_all x1, waiting for transfers between devices, body(): lax.all_to_all(out_grad[0], 'dp', split_axis=1, concat_axis=0, tiled=True)  25.5 us
    ppermute x2, starting transfers between devices, from_behind(): return lax.ppermute(shard, axis, pairs)  13.8 us
    all_to_all x1, waiting for transfers between devices, body(): lax.all_to_all(behind.T, 'dp', split_axis=0, concat_axis=1, tiled=True)  12.7 us
    unnamed x35, local copies, waits for them, and re-layouts  11.5 us
    all_to_all x1, starting transfers between devices, body(): lax.all_to_all(out_grad[0], 'dp', split_axis=1, concat_axis=0, tiled=True)  10.2 us
    all_to_all x1, starting transfers between devices, body(): lax.all_to_all(behind.T, 'dp', split_axis=0, concat_axis=1, tiled=True)  9.84 us
    reduce_sum x2, other arithmetic, short_corr_rows(): jnp.sum(grad_wide * padded[start:start + row_count].astype(jnp.float32),...  8.1 us
    reshape x2, local copies, waits for them, and re-layouts, lag_grad(): skewed = padded.reshape(group_count, taps, 2 * taps + 1)[:, :, :taps]  6.05 us
  transfers between devices with their start and end apart: 5, of which 2 were waited for; matrix products, arithmetic and copies ran while one was open for 36% of the time, Pallas kernels for 0%

profile of v11, /device:TPU:6, one launch (start us, length us, event | category | flops | bytes accessed | tf_op | source)
XLA Modules:
  0.0 148.0 jit_solution(9999023932673417951)
XLA Ops:
  0.6 1.6 %copy.34 = bf16[1,128,4096]{1,2,0:T(8,128)(2,1)S(1)} copy(bf16[1,128,4096]{2,1,0:T(8,128)(2,1)} %param.5) | data formatting | bytes 2097152 | tf_op args[1]
  2.3 1.3 copy.35
  3.6 10.2 %all-to-all-start = ((bf16[128,32,128]{2,0,1:T(8,128)(2,1)}), bf16[128,32,128]{2,0,1:T(8,128)(2,1)S(1)}, u32[]{:S(2)}, u32[]{:S(2)}) async-start(bf16[128,32,128]{2,0,1:T(8,128)(2,1)} %copy.35), calls=%async_computation | async-start | bytes 2097152 | tf_op jit(solution)/shard_map/all_to_all | solution.py:143
  14.0 0.7 copy.36
  14.7 1.4 fusion.27
  16.2 1.1 broadcast_select_fusion
  17.3 25.5 %all-to-all-done = bf16[128,32,128]{2,0,1:T(8,128)(2,1)S(1)} async-done(((bf16[128,32,128]{2,0,1:T(8,128)(2,1)}), bf16[128,32,128]{2,0,1:T(8,128)(2,1)S(1)}, u32[]{:S(2)}, u32[]{:S(2)}) %all-to-all-start) | async-done | bytes 1048608 | tf_op jit(solution)/shard_map/all_to_all | solution.py:143
  42.8 0.5 copy.37
  43.3 1.3 copy.40
  44.6 5.0 %all-to-all-start.1 = ((bf16[128,32,128]{2,0,1:T(8,128)(2,1)}), bf16[128,32,128]{2,0,1:T(8,128)(2,1)S(1)}, u32[]{:S(2)}, u32[]{:S(2)}) async-start(bf16[128,32,128]{2,0,1:T(8,128)(2,1)} %copy.40), calls=%async_computation.1 | async-start | bytes 2097152 | tf_op jit(solution)/shard_map/all_to_all | solution.py:145
  49.6 0.2 copy.78
  50.2 0.7 copy-done.5
  50.9 0.3 fusion.47
  51.2 0.3 fusion.23
  51.5 0.2 copy.90
  51.7 1.5 add_convert_fusion.4
  53.5 0.3 fusion.46
  53.8 0.3 fusion.24
  54.1 0.2 copy.89
  54.3 2.3 %add_convert_fusion.3 = bf16[64,4096]{1,0:T(8,128)(2,1)} fusion(bf16[64,4096]{1,0:T(8,128)(2,1)S(1)} %bitcast.442, bf16[64,4096]{1,0:T(8,128)(2,1)S(1)} %add_convert_fusion.4, f32[64]{0:T(128)S(1)} %get-tuple-element.81, f32[64]{0:T(128)S(1)} %get-tuple-element.82, f32[64]{0:T(128)S(1)} %get-tuple-element.83, f32[64]{0:T(128)S(1)} %get-tuple-element.84, ...), kind=kLoop, calls=%fused_computation.79 | loop fusion | flops 6029312 | bytes 1574656 | tf_op jit(solution)/shard_map/convert_element_type | solution.py:168
  56.9 11.4 %collective-permute-start = (bf16[64,4096]{1,0:T(8,128)(2,1)}, bf16[64,4096]{1,0:T(8,128)(2,1)}, u32[]{:S(2)}, u32[]{:S(2)}) collective-permute-start(bf16[64,4096]{1,0:T(8,128)(2,1)} %add_convert_fusion.3), channel_id=1, source_target_pairs={{32,0},{64,32},{96,64},{128,96},{160,128},{192,160},{224,192},{256... | collective-permute-start | bytes 1572872 | tf_op jit(solution)/shard_map/ppermute | solution.py:10
  68.3 0.3 fusion.45
  68.6 0.3 fusion.25
  69.0 0.2 copy.88
  69.2 1.5 add_convert_fusion.2
  71.0 1.2 copy.75
  72.3 0.3 fusion.44
  72.6 0.3 fusion.26
  72.9 0.2 copy.87
  73.1 2.3 %add_convert_fusion.1 = bf16[64,4096]{1,0:T(8,128)(2,1)} fusion(bf16[64,4096]{1,0:T(8,128)(2,1)S(1)} %bitcast.446, bf16[64,4096]{1,0:T(8,128)(2,1)S(1)} %add_convert_fusion.2, f32[64]{0:T(128)S(1)} %get-tuple-element.68, f32[64]{0:T(128)S(1)} %get-tuple-element.69, f32[64]{0:T(128)S(1)} %get-tuple-element.70, f32[64]{0:T(128)S(1)} %get-tuple-element.71, ...), kind=kLoop, calls=%fused_computation.77 | loop fusion | flops 6029312 | bytes 1574656 | tf_op jit(solution)/shard_map/convert_element_type | solution.py:168
  75.4 2.4 %collective-permute-start.1 = (bf16[64,4096]{1,0:T(8,128)(2,1)}, bf16[64,4096]{1,0:T(8,128)(2,1)}, u32[]{:S(2)}, u32[]{:S(2)}) collective-permute-start(bf16[64,4096]{1,0:T(8,128)(2,1)} %add_convert_fusion.1), channel_id=1, source_target_pairs={{32,0},{64,32},{96,64},{128,96},{160,128},{192,160},{224,192},{256... | collective-permute-start | bytes 1572872 | tf_op jit(solution)/shard_map/ppermute | solution.py:10
  77.9 1.5 %maximum_bitcast_fusion = (bf16[4096,128]{0,1:T(8,128)(2,1)}, bf16[4096,128]{0,1:T(8,128)(2,1)}) fusion(bf16[64,4096]{1,0:T(8,128)(2,1)S(1)} %bitcast.445, bf16[64,4096]{1,0:T(8,128)(2,1)S(1)} %bitcast.441, bf16[64,4096]{1,0:T(8,128)(2,1)S(1)} %bitcast.447, bf16[64,4096]{1,0:T(8,128)(2,1)S(1)} %bitcast.443), kind=kLoop, calls=%fused_computation.63 | loop fusion | flops 4194304 | bytes 4194304 | tf_op jit(solution)/shard_map/transpose | solution.py:184
  79.4 0.5 copy.41
  79.9 2.6 %fusion.36 = bf16[16,8,32,128]{3,1,2,0:T(8,128)(2,1)S(1)} fusion(f32[128]{0:T(128)S(1)} %get-tuple-element.58, bf16[128,4096]{1,0:T(8,128)(2,1)S(1)} %bitcast.417, f32[128]{0:T(128)S(1)} %get-tuple-element.59, f32[128]{0:T(128)S(1)} %get-tuple-element.60, f32[128]{0:T(128)S(1)} %get-tuple-element.61, f32[128]{0:T(128)S(1)} %get-tuple-element.62, ...), kind=kLoop, calls=%fused_computation.82 | loop fusion | flops 11010048 | bytes 2100736
  82.5 0.2 copy.73
  82.7 0.7 convolution_bitcast_fusion.2
  83.4 0.5 fusion.28
  83.9 1.1 pad_maximum_fusion.1
  85.0 2.6 %copy.47 = f32[8,128,256]{2,1,0:T(8,128)} copy(f32[8,128,256]{1,2,0:T(8,128)} %pad_maximum_fusion.1) | data formatting | bytes 2097152 | tf_op jit(solution)/shard_map/concatenate | solution.py:71
  87.6 1.8 %copy.76 = f32[1,8,128,256]{3,1,2,0:T(8,128)S(1)} copy(f32[1,8,128,256]{3,2,1,0:T(8,128)} %bitcast.455) | data formatting | bytes 2097152
  89.4 1.0 concatenate.98
  90.5 3.6 %reshape.552 = f32[8,128,257]{2,1,0:T(8,128)} reshape(f32[8,32896]{1,0:T(8,128)} %concatenate.98) | data formatting | bytes 2105344 | tf_op jit(solution)/shard_map/reshape | solution.py:73
  94.1 1.5 %fusion.43 = f32[8,16,32,128]{3,2,1,0:T(8,128)S(1)} fusion(bf16[2,8,128,128]{3,2,1,0:T(8,128)(2,1)} %get-tuple-element.52, bf16[8,16,32,128]{3,2,1,0:T(8,128)(2,1)S(1)} %bitcast.415), kind=kOutput, calls=%fused_computation.116 | convolution fusion | flops 134217728 | bytes 3407872 | tf_op jit(solution)/shard_map/gcbt,gts->gcbs/dot_general | solution.py:38
  95.6 0.5 convolution_add_fusion
  96.1 1.9 %fusion.8 = bf16[128,4096]{1,0:T(8,128)(2,1)S(1)} fusion(f32[16,8,32,128]{3,2,1,0:T(8,128)S(1)} %bitcast.428, bf16[4096,128]{0,1:T(8,128)(2,1)S(1)} %copy.41), kind=kLoop, calls=%fused_computation.26 | loop fusion | flops 1572864 | bytes 4194304 | tf_op jit(solution)/shard_map/convert_element_type | solution.py:180
  98.0 2.3 %pad_maximum_fusion = bf16[128,4096]{1,0:T(8,128)(2,1)} fusion(bf16[64,4096]{1,0:T(8,128)(2,1)} %collective-permute-done.1, bf16[64,4096]{1,0:T(8,128)(2,1)} %collective-permute-done), kind=kLoop, calls=%fused_computation.62 | loop fusion | flops 2097152 | bytes 2097152 | tf_op jit(solution)/shard_map/concatenate | solution.py:184
  100.2 2.3 %copy.42 = bf16[4096,128]{1,0:T(8,128)(2,1)} copy(bf16[4096,128]{0,1:T(8,128)(2,1)} %bitcast.454) | data formatting | bytes 2097152 | tf_op jit(solution)/shard_map/transpose | solution.py:186
  102.5 2.5 %fusion.35 = bf16[16,8,32,128]{3,1,2,0:T(8,128)(2,1)S(1)} fusion(f32[128]{0:T(128)S(1)} %get-tuple-element.65, bf16[128,4096]{1,0:T(8,128)(2,1)S(1)} %fusion.8, f32[128]{0:T(128)S(1)} %get-tuple-element.66, f32[128]{0:T(128)S(1)} %get-tuple-element.54, f32[128]{0:T(128)S(1)} %get-tuple-element.55, f32[128]{0:T(128)S(1)} %get-tuple-element.56, ...), kind=kLoop, calls=%fused_computation.81 | loop fusion | flops 11010048 | bytes 2100736
  105.1 1.2 copy.77
  106.3 9.8 %all-to-all-start.2 = ((bf16[32,128,128]{2,1,0:T(8,128)(2,1)}), bf16[32,128,128]{2,1,0:T(8,128)(2,1)}, u32[]{:S(2)}, u32[]{:S(2)}) async-start(bf16[32,128,128]{2,1,0:T(8,128)(2,1)} %bitcast.451), calls=%async_computation.2 | async-start | bytes 2097152 | tf_op jit(solution)/shard_map/all_to_all | solution.py:186
  116.1 4.0 %fusion.15 = (f32[128]{0:T(128)S(1)}, f32[128]{0:T(128)S(1)}, f32[128]{0:T(128)S(1)}, f32[128]{0:T(128)S(1)}, f32[128]{0:T(128)S(1)}, /*index=5*/f32[128]{0:T(128)S(1)}, f32[128]{0:T(128)S(1)}) fusion(bf16[4096,128]{0,1:T(8,128)(2,1)} %get-tuple-element.21, bf16[4096,128]{0,1:T(8,128)(2,1)S(1)} %copy.41), kind=kLoop, calls=%fused_computation.33 | loop fusion | flops 11533440 | bytes 2100736 | tf_op jit(solution)/shard_map/reduce_sum | solution.py:130
  120.2 4.1 %fusion.22 = (f32[128]{0:T(128)S(1)}, f32[128]{0:T(128)S(1)}, f32[128]{0:T(128)S(1)}, f32[128]{0:T(128)S(1)}, f32[128]{0:T(128)S(1)}, /*index=5*/f32[128]{0:T(128)S(1)}, f32[128]{0:T(128)S(1)}) fusion(bf16[4096,128]{0,1:T(8,128)(2,1)} %get-tuple-element.22, bf16[4096,128]{0,1:T(8,128)(2,1)S(1)} %bitcast.418, bf16[128,4096]{1,0:T(8,128)(2,1)S(1)} %fusion.8), kind=kLoop, calls=%fused_computation.40 | loop fusion | flops 11533440 | bytes 3149312 | tf_op jit(solution)/shard_map/reduce_sum | solution.py:130
  124.3 0.6 copy.50
  124.9 0.7 convolution_bitcast_fusion
  125.6 0.5 fusion.29
  126.2 0.3 copy.48
  126.5 0.6 copy.79
  127.2 2.4 %reshape.556 = f32[8,128,257]{2,1,0:T(8,128)} reshape(f32[8,32896]{1,0:T(8,128)S(1)} %concatenate.102) | data formatting | bytes 2105344 | tf_op jit(solution)/shard_map/reshape | solution.py:73
  129.7 1.1 slice_reduce_fusion.1
  130.7 1.1 slice_reduce_fusion
  131.8 0.6 maximum_multiply_fusion.1
  132.4 12.7 %all-to-all-done.2 = bf16[32,128,128]{2,1,0:T(8,128)(2,1)} async-done(((bf16[32,128,128]{2,1,0:T(8,128)(2,1)}), bf16[32,128,128]{2,1,0:T(8,128)(2,1)}, u32[]{:S(2)}, u32[]{:S(2)}) %all-to-all-start.2) | async-done | bytes 1048608 | tf_op jit(solution)/shard_map/all_to_all | solution.py:186
  145.1 1.6 %copy.43 = bf16[32,128,128]{1,2,0:T(8,128)(2,1)S(1)} copy(bf16[32,128,128]{2,1,0:T(8,128)(2,1)} %all-to-all-done.2) | data formatting | bytes 2097152 | tf_op jit(solution)/shard_map/all_to_all | solution.py:186
  146.7 1.3 copy.49
  (39 shorter events, 1.8 us)
Async XLA Ops:
  0.6 14.1 %copy-start = (bf16[1,2,8,128]{3,2,1,0:T(8,128)(2,1)S(1)}, bf16[1,2,8,128]{3,2,1,0:T(8,128)(2,1)}, u32[]{:S(2)}) copy-start(bf16[1,2,8,128]{3,2,1,0:T(8,128)(2,1)} %param.7) | copy-start | bytes 12292
  2.3 11.7 %copy-start.6 = (bf16[1,128,4096]{2,1,0:T(8,128)(2,1)S(1)}, bf16[1,128,4096]{2,1,0:T(8,128)(2,1)}, u32[]{:S(2)}) copy-start(bf16[1,128,4096]{2,1,0:T(8,128)(2,1)} %param.4) | copy-start | bytes 3145732
  3.6 39.2 %all-to-all-start = ((bf16[128,32,128]{2,0,1:T(8,128)(2,1)}), bf16[128,32,128]{2,0,1:T(8,128)(2,1)S(1)}, u32[]{:S(2)}, u32[]{:S(2)}) async-start(bf16[128,32,128]{2,0,1:T(8,128)(2,1)} %copy.35), calls=%async_computation | async-start | bytes 2097152 | tf_op jit(solution)/shard_map/all_to_all | solution.py:143
  14.6 1.4 copy-start.7
  44.6 34.7 %all-to-all-start.1 = ((bf16[128,32,128]{2,0,1:T(8,128)(2,1)}), bf16[128,32,128]{2,0,1:T(8,128)(2,1)S(1)}, u32[]{:S(2)}, u32[]{:S(2)}) async-start(bf16[128,32,128]{2,0,1:T(8,128)(2,1)} %copy.40), calls=%async_computation.1 | async-start | bytes 2097152 | tf_op jit(solution)/shard_map/all_to_all | solution.py:145
  49.8 1.0 copy-start.5
  49.9 1.3 copy-start.3
  56.9 41.0 %collective-permute-start = (bf16[64,4096]{1,0:T(8,128)(2,1)}, bf16[64,4096]{1,0:T(8,128)(2,1)}, u32[]{:S(2)}, u32[]{:S(2)}) collective-permute-start(bf16[64,4096]{1,0:T(8,128)(2,1)} %add_convert_fusion.3), channel_id=1, source_target_pairs={{32,0},{64,32},{96,64},{128,96},{160,128},{192,160},{224,192},{256... | collective-permute-start | bytes 1572872 | tf_op jit(solution)/shard_map/ppermute | solution.py:10
  75.4 22.6 %collective-permute-start.1 = (bf16[64,4096]{1,0:T(8,128)(2,1)}, bf16[64,4096]{1,0:T(8,128)(2,1)}, u32[]{:S(2)}, u32[]{:S(2)}) collective-permute-start(bf16[64,4096]{1,0:T(8,128)(2,1)} %add_convert_fusion.1), channel_id=1, source_target_pairs={{32,0},{64,32},{96,64},{128,96},{160,128},{192,160},{224,192},{256... | collective-permute-start | bytes 1572872 | tf_op jit(solution)/shard_map/ppermute | solution.py:10
  79.9 2.8 %copy-start.2 = (bf16[16,8,32,128]{3,2,1,0:T(8,128)(2,1)S(1)}, bf16[16,8,32,128]{3,2,1,0:T(8,128)(2,1)}, u32[]{:S(2)}) copy-start(bf16[16,8,32,128]{3,2,1,0:T(8,128)(2,1)} %copy.75) | copy-start | bytes 3145732
  94.1 1.5 %copy-start.4 = (bf16[2,8,128,128]{3,2,1,0:T(8,128)(2,1)S(1)}, bf16[2,8,128,128]{3,2,1,0:T(8,128)(2,1)}, u32[]{:S(2)}) copy-start(bf16[2,8,128,128]{3,2,1,0:T(8,128)(2,1)} %get-tuple-element.51) | copy-start | bytes 1572868
  106.3 38.8 %all-to-all-start.2 = ((bf16[32,128,128]{2,1,0:T(8,128)(2,1)}), bf16[32,128,128]{2,1,0:T(8,128)(2,1)}, u32[]{:S(2)}, u32[]{:S(2)}) async-start(bf16[32,128,128]{2,1,0:T(8,128)(2,1)} %bitcast.451), calls=%async_computation.2 | async-start | bytes 2097152 | tf_op jit(solution)/shard_map/all_to_all | solution.py:186
  120.1 4.8 %copy-start.1 = (bf16[16,8,32,128]{3,2,1,0:T(8,128)(2,1)S(1)}, bf16[16,8,32,128]{3,2,1,0:T(8,128)(2,1)}, u32[]{:S(2)}) copy-start(bf16[16,8,32,128]{3,2,1,0:T(8,128)(2,1)} %copy.77) | copy-start | bytes 3145732

commit v12 on v9

--- a/solution.py
+++ b/solution.py
@@ -179,7 +179,7 @@
     long_one = causal_long(mixed_one, circ_now[0], circ_past[0])
     middle = (source.astype(jnp.float32) + long_one).astype(jnp.bfloat16)
     mixed_two = short_mix(middle, short_all[1]).astype(jnp.bfloat16)
-    behinds = list(lax.optimization_barrier((*behinds, middle))[:-1])
+    behinds = list(lax.optimization_barrier((*behinds, mixed_one))[:-1])
     behind = jnp.concatenate(behinds)
     own_rows = lax.all_to_all(behind.T, "dp", split_axis=0, concat_axis=1, tiled=True)
     passed_grad = own_rows[None]

time: 143 us -> 145 us (1.014)
  waiting for transfers between devices: 37.8 us -> 39.6 us
    ppermute x2, waiting for transfers between devices: 2.92 us -> 12.5 us  [from_behind(): return lax.ppermute(shard, axis, pairs)]
    all_to_all x1, waiting for transfers between devices: 7.76 us -> 0.01 us  [body(): lax.all_to_all(behind.T, 'dp', split_axis=0, concat_axis=1, tiled=True)]
    unnamed x59 -> x57, local copies, waits for them, and re-layouts: 10.7 us -> 11.1 us
  transfers between devices with their start and end apart: 5 -> 5, of which waited for: 4 -> 4; matrix products, arithmetic and copies ran while one was open for 35% -> 34% of each run, Pallas kernels for 0% -> 0%
where the time goes in v12:
time: 145 us; the launch traced here: 144 us
  waiting for transfers between devices  39.6 us (27%)
  starting transfers between devices  38.6 us (27%)
  local copies, waits for them, and re-layouts  28.3 us (20%)
  other arithmetic  28.1 us (19%)
  matrix products  8.05 us (6%)
    all_to_all x1, waiting for transfers between devices, body(): lax.all_to_all(out_grad[0], 'dp', split_axis=1, concat_axis=0, tiled=True)  25.5 us
    ppermute x2, starting transfers between devices, from_behind(): return lax.ppermute(shard, axis, pairs)  13.8 us
    ppermute x2, waiting for transfers between devices, from_behind(): return lax.ppermute(shard, axis, pairs)  12.5 us
    unnamed x57, local copies, waits for them, and re-layouts  11.1 us
    all_to_all x1, starting transfers between devices, body(): lax.all_to_all(out_grad[0], 'dp', split_axis=1, concat_axis=0, tiled=True)  10.2 us
    all_to_all x1, starting transfers between devices, body(): lax.all_to_all(behind.T, 'dp', split_axis=0, concat_axis=1, tiled=True)  9.55 us
    reduce_sum x2, other arithmetic, short_corr_rows(): jnp.sum(grad_wide * padded[start:start + row_count].astype(jnp.float32),...  8.65 us
    reshape x2, local copies, waits for them, and re-layouts, lag_grad(): skewed = padded.reshape(group_count, taps, 2 * taps + 1)[:, :, :taps]  6.02 us
  transfers between devices with their start and end apart: 5, of which 4 were waited for; matrix products, arithmetic and copies ran while one was open for 34% of the time, Pallas kernels for 0%

profile of v12, /device:TPU:6, one launch (start us, length us, event | category | flops | bytes accessed | tf_op | source)
XLA Modules:
  0.0 144.0 jit_solution(15751399531483559688)
XLA Ops:
  0.6 1.6 %copy.34 = bf16[1,128,4096]{1,2,0:T(8,128)(2,1)S(1)} copy(bf16[1,128,4096]{2,1,0:T(8,128)(2,1)} %param.5) | data formatting | bytes 2097152 | tf_op args[1]
  2.3 1.3 copy.35
  3.6 10.2 %all-to-all-start = ((bf16[128,32,128]{2,0,1:T(8,128)(2,1)}), bf16[128,32,128]{2,0,1:T(8,128)(2,1)S(1)}, u32[]{:S(2)}, u32[]{:S(2)}) async-start(bf16[128,32,128]{2,0,1:T(8,128)(2,1)} %copy.35), calls=%async_computation | async-start | bytes 2097152 | tf_op jit(solution)/shard_map/all_to_all | solution.py:143
  14.0 0.7 copy.36
  14.7 1.4 fusion.27
  16.2 1.1 broadcast_select_fusion
  17.3 25.5 %all-to-all-done = bf16[128,32,128]{2,0,1:T(8,128)(2,1)S(1)} async-done(((bf16[128,32,128]{2,0,1:T(8,128)(2,1)}), bf16[128,32,128]{2,0,1:T(8,128)(2,1)S(1)}, u32[]{:S(2)}, u32[]{:S(2)}) %all-to-all-start) | async-done | bytes 1048608 | tf_op jit(solution)/shard_map/all_to_all | solution.py:143
  42.8 0.5 copy.37
  43.3 1.3 copy.40
  44.6 5.0 %all-to-all-start.1 = ((bf16[128,32,128]{2,0,1:T(8,128)(2,1)}), bf16[128,32,128]{2,0,1:T(8,128)(2,1)}, u32[]{:S(2)}, u32[]{:S(2)}) async-start(bf16[128,32,128]{2,0,1:T(8,128)(2,1)} %copy.40), calls=%async_computation.1 | async-start | bytes 2097152 | tf_op jit(solution)/shard_map/all_to_all | solution.py:145
  49.7 0.2 copy.78
  50.3 0.7 copy-done.16
  50.9 0.3 fusion.46
  51.3 0.3 fusion.23
  51.6 0.2 copy.91
  51.8 1.5 %add_convert_fusion.4 = bf16[64,4096]{1,0:T(8,128)(2,1)S(1)} fusion(bf16[64,4096]{1,0:T(8,128)(2,1)S(1)} %bitcast.474, f32[64]{0:T(128)S(1)} %get-tuple-element.85, f32[64]{0:T(128)S(1)} %get-tuple-element.86, f32[64]{0:T(128)S(1)} %get-tuple-element.87, f32[64]{0:T(128)S(1)} %get-tuple-element.88, f32[64]{0:T(128)S(1)} %get-tuple-element.89, ...), kind=kLoop, calls=%fused_computation.80 | loop fusion | flops 6029312 | bytes 1574656 | tf_op jit(solution)/shard_map/convert_element_type | solution.py:162
  53.6 0.3 fusion.45
  53.9 0.3 fusion.24
  54.2 0.2 copy.90
  54.4 2.3 %add_convert_fusion.3 = bf16[64,4096]{1,0:T(8,128)(2,1)} fusion(bf16[64,4096]{1,0:T(8,128)(2,1)S(1)} %bitcast.489, bf16[64,4096]{1,0:T(8,128)(2,1)S(1)} %add_convert_fusion.4, f32[64]{0:T(128)S(1)} %get-tuple-element.78, f32[64]{0:T(128)S(1)} %get-tuple-element.79, f32[64]{0:T(128)S(1)} %get-tuple-element.80, f32[64]{0:T(128)S(1)} %get-tuple-element.81, ...), kind=kLoop, calls=%fused_computation.79 | loop fusion | flops 6029312 | bytes 1574656 | tf_op jit(solution)/shard_map/convert_element_type | solution.py:168
  57.0 11.4 %collective-permute-start = (bf16[64,4096]{1,0:T(8,128)(2,1)}, bf16[64,4096]{1,0:T(8,128)(2,1)}, u32[]{:S(2)}, u32[]{:S(2)}) collective-permute-start(bf16[64,4096]{1,0:T(8,128)(2,1)} %add_convert_fusion.3), channel_id=1, source_target_pairs={{32,0},{64,32},{96,64},{128,96},{160,128},{192,160},{224,192},{256... | collective-permute-start | bytes 1572872 | tf_op jit(solution)/shard_map/ppermute | solution.py:10
  68.4 0.3 fusion.44
  68.7 0.3 fusion.25
  69.3 1.5 %add_convert_fusion.2 = bf16[64,4096]{1,0:T(8,128)(2,1)S(1)} fusion(bf16[64,4096]{1,0:T(8,128)(2,1)S(1)} %bitcast.477, bf16[64,4096]{1,0:T(8,128)(2,1)S(1)} %get-tuple-element.12, f32[64]{0:T(128)S(1)} %get-tuple-element.71, f32[64]{0:T(128)S(1)} %get-tuple-element.72, f32[64]{0:T(128)S(1)} %get-tuple-element.73, f32[64]{0:T(128)S(1)} %get-tuple-element.74, ...), kind=kLoop, calls=%fused_computation.78 | loop fusion | flops 6029312 | bytes 1574656 | tf_op jit(solution)/shard_map/convert_element_type | solution.py:162
  71.1 0.2 copy.75
  71.4 0.3 fusion.43
  71.7 0.3 fusion.26
  72.2 2.3 %add_convert_fusion.1 = bf16[64,4096]{1,0:T(8,128)(2,1)} fusion(bf16[64,4096]{1,0:T(8,128)(2,1)S(1)} %bitcast.491, bf16[64,4096]{1,0:T(8,128)(2,1)S(1)} %add_convert_fusion.2, f32[64]{0:T(128)S(1)} %get-tuple-element.65, f32[64]{0:T(128)S(1)} %get-tuple-element.66, f32[64]{0:T(128)S(1)} %get-tuple-element.67, f32[64]{0:T(128)S(1)} %get-tuple-element.68, ...), kind=kLoop, calls=%fused_computation.77 | loop fusion | flops 6029312 | bytes 1574656 | tf_op jit(solution)/shard_map/convert_element_type | solution.py:168
  74.6 2.4 %collective-permute-start.1 = (bf16[64,4096]{1,0:T(8,128)(2,1)}, bf16[64,4096]{1,0:T(8,128)(2,1)}, u32[]{:S(2)}, u32[]{:S(2)}) collective-permute-start(bf16[64,4096]{1,0:T(8,128)(2,1)} %add_convert_fusion.1), channel_id=1, source_target_pairs={{32,0},{64,32},{96,64},{128,96},{160,128},{192,160},{224,192},{256... | collective-permute-start | bytes 1572872 | tf_op jit(solution)/shard_map/ppermute | solution.py:10
  77.0 1.6 %all-to-all-done.1 = bf16[128,32,128]{2,0,1:T(8,128)(2,1)} async-done(((bf16[128,32,128]{2,0,1:T(8,128)(2,1)}), bf16[128,32,128]{2,0,1:T(8,128)(2,1)}, u32[]{:S(2)}, u32[]{:S(2)}) %all-to-all-start.1) | async-done | bytes 1048608 | tf_op jit(solution)/shard_map/all_to_all | solution.py:145
  78.6 1.5 %copy.41 = bf16[4096,128]{0,1:T(8,128)(2,1)S(1)} copy(bf16[4096,128]{1,0:T(8,128)(2,1)} %bitcast.66) | data formatting | bytes 2097152 | tf_op jit(solution)/shard_map/optimization_barrier | solution.py:176
  80.1 1.0 copy-done.2
  81.1 2.5 %fusion.92 = bf16[16,8,32,128]{3,1,2,0:T(8,128)(2,1)S(1)} fusion(f32[128]{0:T(128)S(1)} %get-tuple-element.55, f32[128]{0:T(128)S(1)} %get-tuple-element.56, f32[128]{0:T(128)S(1)} %get-tuple-element.57, f32[128]{0:T(128)S(1)} %get-tuple-element.58, f32[128]{0:T(128)S(1)} %get-tuple-element.59, bf16[128,4096]{1,0:T(8,128)(2,1)S(1)} %bitcast.470, ...), kind=kLoop, calls=%fused_computation.220 | loop fusion | flops 11010048 | bytes 2100736
  83.7 0.2 copy.73
  83.9 2.1 %collective-permute-done = bf16[64,4096]{1,0:T(8,128)(2,1)} collective-permute-done((bf16[64,4096]{1,0:T(8,128)(2,1)}, bf16[64,4096]{1,0:T(8,128)(2,1)}, u32[]{:S(2)}, u32[]{:S(2)}) %collective-permute-start) | collective-permute-done | bytes 524320 | tf_op jit(solution)/shard_map/ppermute | solution.py:10
  86.0 10.4 %collective-permute-done.1 = bf16[64,4096]{1,0:T(8,128)(2,1)} collective-permute-done((bf16[64,4096]{1,0:T(8,128)(2,1)}, bf16[64,4096]{1,0:T(8,128)(2,1)}, u32[]{:S(2)}, u32[]{:S(2)}) %collective-permute-start.1) | collective-permute-done | bytes 524320 | tf_op jit(solution)/shard_map/ppermute | solution.py:10
  96.5 2.3 %maximum_bitcast_fusion = bf16[4096,128]{0,1:T(8,128)(2,1)} fusion(bf16[64,4096]{1,0:T(8,128)(2,1)} %collective-permute-done.1, bf16[64,4096]{1,0:T(8,128)(2,1)} %collective-permute-done), kind=kLoop, calls=%fused_computation.62 | loop fusion | flops 2097152 | bytes 2097152 | tf_op jit(solution)/shard_map/transpose | solution.py:184
  98.7 2.3 %copy.42 = bf16[4096,128]{1,0:T(8,128)(2,1)} copy(bf16[4096,128]{0,1:T(8,128)(2,1)} %maximum_bitcast_fusion) | data formatting | bytes 2097152 | tf_op jit(solution)/shard_map/transpose | solution.py:184
  101.0 9.5 %all-to-all-start.2 = ((bf16[32,128,128]{2,1,0:T(8,128)(2,1)}), bf16[32,128,128]{2,1,0:T(8,128)(2,1)}, u32[]{:S(2)}, u32[]{:S(2)}) async-start(bf16[32,128,128]{2,1,0:T(8,128)(2,1)} %bitcast.495), calls=%async_computation.2 | async-start | bytes 2097152 | tf_op jit(solution)/shard_map/all_to_all | solution.py:184
  110.6 1.4 fusion.42
  112.0 0.7 convolution_bitcast_fusion.2
  112.7 0.4 copy-done.15
  113.1 0.5 convolution_add_fusion
  113.6 0.7 copy-done.3
  114.9 5.8 %fusion.22 = (f32[128]{0:T(128)S(1)}, f32[128]{0:T(128)S(1)}, f32[128]{0:T(128)S(1)}, f32[128]{0:T(128)S(1)}, f32[128]{0:T(128)S(1)}, /*index=5*/f32[128]{0:T(12...) fusion(bf16[4096,128]{0,1:T(8,128)(2,1)S(1)} %copy-done.3, bf16[64,4096]{1,0:T(8,128)(2,1)S(1)} %bitcast.492, ...), kind=kLoop, calls=%fused_computation.40 | loop fusion | flops 18349056 | bytes 6295552 | tf_op jit(solution)/shard_map/reduce_sum | solution.py:130
  120.7 0.5 fusion.28
  121.4 0.3 copy.47
  121.7 0.6 copy.76
  122.3 1.0 concatenate.98
  123.4 3.6 %reshape.552 = f32[8,128,257]{2,1,0:T(8,128)} reshape(f32[8,32896]{1,0:T(8,128)} %concatenate.98) | data formatting | bytes 2105344 | tf_op jit(solution)/shard_map/reshape | solution.py:73
  127.1 2.8 %fusion.15 = (f32[128]{0:T(128)S(1)}, f32[128]{0:T(128)S(1)}, f32[128]{0:T(128)S(1)}, f32[128]{0:T(128)S(1)}, f32[128]{0:T(128)S(1)}, /*index=5*/f32[128]{0:T(128)S(1)}) fusion(bf16[4096,128]{0,1:T(8,128)(2,1)S(1)} %bitcast.469, bf16[64,4096]{1,0:T(8,128)(2,1)S(1)} %bitcast.479, bf16[64,4096]{1,0:T(8,128)(2,1)S(1)} %bitcast.476), kind=kLoop, calls=%fused_computation.26 | loop fusion | flops 11533568 | bytes 2100224 | tf_op jit(solution)/shard_map/reduce_sum | solution.py:130
  129.9 0.6 copy.50
  130.5 2.8 %fusion.35 = bf16[16,8,32,128]{3,1,2,0:T(8,128)(2,1)S(1)} fusion(f32[128]{0:T(128)S(1)} %get-tuple-element.62, bf16[128,4096]{1,0:T(8,128)(2,1)S(1)} %copy-done.1, f32[128]{0:T(128)S(1)} %get-tuple-element.63, f32[128]{0:T(128)S(1)} %get-tuple-element.51, f32[128]{0:T(128)S(1)} %get-tuple-element.52, f32[128]{0:T(128)S(1)} %get-tuple-element.53, ...), kind=kLoop, calls=%fused_computation.81 | loop fusion | flops 11010048 | bytes 2100736
  133.3 0.2 copy.77
  133.6 0.6 convolution_bitcast_fusion
  134.2 0.5 fusion.29
  134.9 0.3 copy.48
  135.2 0.6 copy.79
  135.9 2.4 %reshape.556 = f32[8,128,257]{2,1,0:T(8,128)} reshape(f32[8,32896]{1,0:T(8,128)S(1)} %concatenate.102) | data formatting | bytes 2105344 | tf_op jit(solution)/shard_map/reshape | solution.py:73
  138.3 1.1 slice_reduce_fusion.1
  139.4 1.1 slice_reduce_fusion
  140.5 0.6 maximum_multiply_fusion.1
  141.1 1.6 %copy.43 = bf16[32,128,128]{1,2,0:T(8,128)(2,1)S(1)} copy(bf16[32,128,128]{2,1,0:T(8,128)(2,1)} %all-to-all-done.2) | data formatting | bytes 2097152 | tf_op jit(solution)/shard_map/all_to_all | solution.py:184
  142.7 1.3 copy.49
  (59 shorter events, 2.9 us)
Async XLA Ops:
  0.6 14.1 %copy-start = (bf16[1,2,8,128]{3,2,1,0:T(8,128)(2,1)S(1)}, bf16[1,2,8,128]{3,2,1,0:T(8,128)(2,1)}, u32[]{:S(2)}) copy-start(bf16[1,2,8,128]{3,2,1,0:T(8,128)(2,1)} %param.7) | copy-start | bytes 12292
  2.3 11.7 %copy-start.17 = (bf16[1,128,4096]{2,1,0:T(8,128)(2,1)S(1)}, bf16[1,128,4096]{2,1,0:T(8,128)(2,1)}, u32[]{:S(2)}) copy-start(bf16[1,128,4096]{2,1,0:T(8,128)(2,1)} %param.4) | copy-start | bytes 3145732
  3.6 39.2 %all-to-all-start = ((bf16[128,32,128]{2,0,1:T(8,128)(2,1)}), bf16[128,32,128]{2,0,1:T(8,128)(2,1)S(1)}, u32[]{:S(2)}, u32[]{:S(2)}) async-start(bf16[128,32,128]{2,0,1:T(8,128)(2,1)} %copy.35), calls=%async_computation | async-start | bytes 2097152 | tf_op jit(solution)/shard_map/all_to_all | solution.py:143
  14.6 1.4 copy-start.18
  44.6 34.0 %all-to-all-start.1 = ((bf16[128,32,128]{2,0,1:T(8,128)(2,1)}), bf16[128,32,128]{2,0,1:T(8,128)(2,1)}, u32[]{:S(2)}, u32[]{:S(2)}) async-start(bf16[128,32,128]{2,0,1:T(8,128)(2,1)} %copy.40), calls=%async_computation.1 | async-start | bytes 2097152 | tf_op jit(solution)/shard_map/all_to_all | solution.py:145
  49.9 1.0 copy-start.16
  50.0 1.3 copy-start.14
  51.8 2.1 %copy-start.4 = (bf16[8,8,32,128]{3,1,2,0:T(8,128)(2,1)}, bf16[8,8,32,128]{3,1,2,0:T(8,128)(2,1)S(1)}, u32[]{:S(2)}) copy-start(bf16[8,8,32,128]{3,1,2,0:T(8,128)(2,1)S(1)} %copy.91) | copy-start | bytes 1572868
  54.4 14.3 %copy-start.10 = (bf16[8,8,32,128]{3,1,2,0:T(8,128)(2,1)}, bf16[8,8,32,128]{3,1,2,0:T(8,128)(2,1)S(1)}, u32[]{:S(2)}) copy-start(bf16[8,8,32,128]{3,1,2,0:T(8,128)(2,1)S(1)} %copy.90) | copy-start | bytes 1572868
  57.0 29.0 %collective-permute-start = (bf16[64,4096]{1,0:T(8,128)(2,1)}, bf16[64,4096]{1,0:T(8,128)(2,1)}, u32[]{:S(2)}, u32[]{:S(2)}) collective-permute-start(bf16[64,4096]{1,0:T(8,128)(2,1)} %add_convert_fusion.3), channel_id=1, source_target_pairs={{32,0},{64,32},{96,64},{128,96},{160,128},{192,160},{224,192},{256... | collective-permute-start | bytes 1572872 | tf_op jit(solution)/shard_map/ppermute | solution.py:10
  69.3 1.9 %copy-start.7 = (bf16[8,8,32,128]{3,1,2,0:T(8,128)(2,1)}, bf16[8,8,32,128]{3,1,2,0:T(8,128)(2,1)S(1)}, u32[]{:S(2)}) copy-start(bf16[8,8,32,128]{3,1,2,0:T(8,128)(2,1)S(1)} %copy.89) | copy-start | bytes 1572868
  72.2 6.4 %copy-start.12 = (bf16[8,8,32,128]{3,1,2,0:T(8,128)(2,1)}, bf16[8,8,32,128]{3,1,2,0:T(8,128)(2,1)S(1)}, u32[]{:S(2)}) copy-start(bf16[8,8,32,128]{3,1,2,0:T(8,128)(2,1)S(1)} %copy.88) | copy-start | bytes 1572868
  74.6 21.9 %collective-permute-start.1 = (bf16[64,4096]{1,0:T(8,128)(2,1)}, bf16[64,4096]{1,0:T(8,128)(2,1)}, u32[]{:S(2)}, u32[]{:S(2)}) collective-permute-start(bf16[64,4096]{1,0:T(8,128)(2,1)} %add_convert_fusion.1), channel_id=1, source_target_pairs={{32,0},{64,32},{96,64},{128,96},{160,128},{192,160},{224,192},{256... | collective-permute-start | bytes 1572872 | tf_op jit(solution)/shard_map/ppermute | solution.py:10
  80.1 1.0 copy-start.2
  101.0 40.1 %all-to-all-start.2 = ((bf16[32,128,128]{2,1,0:T(8,128)(2,1)}), bf16[32,128,128]{2,1,0:T(8,128)(2,1)}, u32[]{:S(2)}, u32[]{:S(2)}) async-start(bf16[32,128,128]{2,1,0:T(8,128)(2,1)} %bitcast.495), calls=%async_computation.2 | async-start | bytes 2097152 | tf_op jit(solution)/shard_map/all_to_all | solution.py:184
  112.0 1.0 copy-start.15
  113.1 1.2 copy-start.3
  113.1 1.4 copy-start.5
  113.1 1.5 %copy-start.8 = (bf16[8,8,32,128]{3,1,2,0:T(8,128)(2,1)S(1)}, bf16[8,8,32,128]{3,1,2,0:T(8,128)(2,1)}, u32[]{:S(2)}) copy-start(bf16[8,8,32,128]{3,1,2,0:T(8,128)(2,1)} %copy-done.7) | copy-start | bytes 1572868
  113.1 1.7 %copy-start.11 = (bf16[8,8,32,128]{3,1,2,0:T(8,128)(2,1)S(1)}, bf16[8,8,32,128]{3,1,2,0:T(8,128)(2,1)}, u32[]{:S(2)}) copy-start(bf16[8,8,32,128]{3,1,2,0:T(8,128)(2,1)} %copy-done.10) | copy-start | bytes 1572868
  113.1 1.8 %copy-start.13 = (bf16[8,8,32,128]{3,1,2,0:T(8,128)(2,1)S(1)}, bf16[8,8,32,128]{3,1,2,0:T(8,128)(2,1)}, u32[]{:S(2)}) copy-start(bf16[8,8,32,128]{3,1,2,0:T(8,128)(2,1)} %copy-done.12) | copy-start | bytes 1572868
  122.3 4.7 %copy-start.1 = (bf16[128,4096]{1,0:T(8,128)(2,1)S(1)}, bf16[128,4096]{1,0:T(8,128)(2,1)}, u32[]{:S(2)}) copy-start(bf16[128,4096]{1,0:T(8,128)(2,1)} %get-tuple-element.45) | copy-start | bytes 3145732
  122.3 4.7 %copy-start.6 = (bf16[8,8,32,128]{3,1,2,0:T(8,128)(2,1)S(1)}, bf16[8,8,32,128]{3,1,2,0:T(8,128)(2,1)}, u32[]{:S(2)}) copy-start(bf16[8,8,32,128]{3,1,2,0:T(8,128)(2,1)} %copy-done.4) | copy-start | bytes 1572868
  122.3 4.7 %copy-start.9 = (bf16[8,8,32,128]{3,1,2,0:T(8,128)(2,1)S(1)}, bf16[8,8,32,128]{3,1,2,0:T(8,128)(2,1)}, u32[]{:S(2)}) copy-start(bf16[8,8,32,128]{3,1,2,0:T(8,128)(2,1)} %copy-done.7) | copy-start | bytes 1572868
